TPU v7x, 512 devices: a whole 4x4x16 slice. The times are simulated.
512 devices in a mesh: segment: 2 (over core), inline: 64 (over x, z), xline: 4 (over y).
Axes of the slice: x: 4, y: 4, z: 16, core: 2. Of those that a mesh axis runs over, the one named last changes fastest.
Arguments:
- survey: float32 [2, 256, 16, 1024], P(None, 'inline', 'xline'), may hold values from -6 to 6
- conduct: bfloat16 [3, 2, 256, 16, 1024], P(None, None, 'inline', 'xline'), may hold values from 0.099609375 to 1
- widths: int32 [2, 64], P(None, 'inline'), may hold values from 2 to 4, as said below
Outputs:
- coherence: float32 [2, 256, 16, 1024], P('segment', 'inline', 'xline')
- curvature: float32 [2, 256, 16, 1024], P('segment', 'inline', 'xline')
Inputs may be any that keep to these rules, and one draw needn't show every extreme that they name: `widths`: in every micro-batch some device holds exactly 4 live rows and another exactly 2.
All inputs are finite; a program needn't handle non-finite values.
Results may differ from a plain program's by a relative error of at most 0.0003.
Values sent between devices are 32-bit elements; how exact they have to be, the bound alone decides.
No kernel may reach another device: no remote copies, remote signals or barrier semaphores. Data moves between devices by JAX's collectives and lax.ppermute only.
A program may use at most 64 MiB of HBM per device.

v0:
```python
import jax
import jax.numpy as jnp
from jax import lax
from jax.sharding import PartitionSpec as P

STEPS = 2


step_size = 0.15
epsilon = 1e-06


def extended(value, sides, width):
    for axis, dim in sides:
        count, length = (lax.axis_size(axis), value.shape[dim])
        up = [(i, (i + 1) % count) for i in range(count - 1)]
        down = [(j, i) for i, j in up]
        last = lax.slice_in_dim(value, length - width, length, axis=dim)
        initial = lax.slice_in_dim(value, 0, width, axis=dim)
        before = lax.ppermute(last, axis, up)
        after = lax.ppermute(initial, axis, down)
        value = jnp.concatenate([before, value, after], axis=dim)
    return value


def shifted_2(value, axis, steps):
    count = lax.axis_size(axis)
    initial, last = (max(0, -steps), min(count, count - steps))
    return lax.ppermute(value, axis, [(source, source + steps) for source in range(initial, last)])


def shifted(source, which_axis, offset):
    length = source.shape[which_axis]
    margins = [(0, 0)] * source.ndim
    if offset > 0:
        margins[which_axis] = (0, offset)
        padded = jnp.pad(source, margins)
        return lax.slice_in_dim(padded, offset, offset + length, axis=which_axis)
    margins[which_axis] = (-offset, 0)
    padded = jnp.pad(source, margins)
    return lax.slice_in_dim(padded, 0, length, axis=which_axis)


def neighbor(source, which_axis, offset, opened):
    return jnp.where(opened, shifted(source, which_axis, offset), source)


def face_masks(depth, width, rows, cols, samples):
    inline_pos = lax.axis_index("inline")
    inline_count = lax.axis_size("inline")
    xline_pos = lax.axis_index("xline")
    xline_count = lax.axis_size("xline")
    own_row = jnp.arange(rows + 2 * depth, dtype=jnp.int32) - depth
    first_row = inline_pos == 0
    last_row = inline_pos == inline_count - 1
    row_up = jnp.logical_not(last_row & (own_row == width - 1) | first_row & (own_row == -1))
    row_down = jnp.logical_not(last_row & (own_row == width) | first_row & (own_row == 0))
    own_col = jnp.arange(cols + 2 * depth, dtype=jnp.int32) - depth
    first_col = xline_pos == 0
    last_col = xline_pos == xline_count - 1
    col_up = jnp.logical_not(last_col & (own_col == cols - 1) | first_col & (own_col == -1))
    col_down = jnp.logical_not(last_col & (own_col == cols) | first_col & (own_col == 0))
    sample = jnp.arange(samples, dtype=jnp.int32)
    return [
        (row_up[:, None, None], row_down[:, None, None]),
        (col_up[None, :, None], col_down[None, :, None]),
        ((sample < samples - 1)[None, None, :], (sample > 0)[None, None, :]),
    ]


def extend(field, depth, width):
    spread = extended(field, (("xline", 2),), depth)
    upper_rows = lax.dynamic_slice_in_dim(spread, width - depth, depth, 1)
    lower_rows = spread[:, :depth]
    from_lower = shifted_2(upper_rows, "inline", 1)
    from_upper = shifted_2(lower_rows, "inline", -1)
    padded = jnp.pad(spread, ((0, 0), (0, depth), (0, 0), (0, 0)))
    padded = lax.dynamic_update_slice_in_dim(padded, from_upper, width, 1)
    return jnp.concatenate([from_lower, padded], 1)


def relax_step(values, coeffs, masks):
    change = jnp.zeros_like(values)
    for which_axis in range(3):
        kk = coeffs[which_axis]
        up_open, down_open = masks[which_axis]
        for offset, opened in ((1, up_open), (-1, down_open)):
            change = change + 0.5 * (kk + neighbor(kk, which_axis, offset, opened)) * (
                neighbor(values, which_axis, offset, opened) - values
            )
    return values + step_size * change


def diffuse(field, conduct_batch, width):
    rows, cols, samples = field.shape
    rounds = [(1, 1)] * STEPS
    coeffs_own = conduct_batch.astype(jnp.float32)
    for depth, count in rounds:
        grown = extend(jnp.concatenate([field[None], coeffs_own], 0), depth, width)
        masks = face_masks(depth, width, rows, cols, samples)
        values = grown[0]
        coeffs = grown[1:]
        values = relax_step(values, coeffs, masks)
        field = values[depth : depth + rows, depth : depth + cols]
    return field


def attributes(smooth, width):
    rows, cols, samples = smooth.shape
    grown = extend(smooth[None], 2, width)[0]
    masks = face_masks(2, width, rows, cols, samples)
    grads = []
    for which_axis in range(3):
        up_open, down_open = masks[which_axis]
        grads.append(
            0.5
            * (neighbor(grown, which_axis, 1, up_open) - neighbor(grown, which_axis, -1, down_open))
        )
    seconds = []
    for which_axis in range(2):
        up_open, down_open = masks[which_axis]
        seconds.append(
            neighbor(grown, which_axis, 1, up_open)
            + neighbor(grown, which_axis, -1, down_open)
            - 2.0 * grown
        )
    combos = [(0, 0), (1, 1), (2, 2), (0, 1), (0, 2), (1, 2)]
    tensor = jnp.stack(
        [grads[first_index] * grads[second_index] for first_index, second_index in combos], 0
    )
    for which_axis in range(3):
        up_open, down_open = masks[which_axis]
        tensor = 0.25 * (
            neighbor(tensor, which_axis + 1, 1, up_open)
            + 2.0 * tensor
            + neighbor(tensor, which_axis + 1, -1, down_open)
        )
    trace = tensor[0] + tensor[1] + tensor[2]
    minors = (
        tensor[0] * tensor[1]
        - tensor[3] * tensor[3]
        + tensor[0] * tensor[2]
        - tensor[4] * tensor[4]
        + tensor[1] * tensor[2]
        - tensor[5] * tensor[5]
    )
    coherence = 1.0 - 3.0 * minors / (trace * trace + epsilon)
    curvature = (seconds[0] + seconds[1]) / (1.0 + grads[0] * grads[0] + grads[1] * grads[1]) ** 1.5
    outcome = jnp.stack([coherence, curvature], 0)[:, 2 : 2 + rows, 2 : 2 + cols]
    live_rows = (jnp.arange(rows, dtype=jnp.int32) < width)[None, :, None, None]
    return jnp.where(live_rows, outcome, 0.0)


def on_device(survey, conduct, widths):
    segment_pos = lax.axis_index("segment")
    batches = survey.shape[0]
    results = []
    for batch in range(batches):
        picked = (batch + segment_pos) % batches
        own_field = lax.dynamic_index_in_dim(survey, picked, 0, keepdims=False)
        own_coeffs = lax.dynamic_index_in_dim(conduct, picked, 1, keepdims=False)
        own_width = lax.dynamic_index_in_dim(widths[:, 0], picked, 0, keepdims=False)
        smooth = diffuse(own_field, own_coeffs, own_width)
        arrived = shifted_2(smooth, "segment", 1)
        results.append(attributes(arrived, widths[batch, 0]))
    returned = shifted_2(results[0], "segment", -1)
    chosen = jnp.where(segment_pos == 0, returned, results[1])
    return (chosen[0][None], chosen[1][None])


def solution(mesh):
    placed = (
        P(None, "inline", "xline", None),
        P(None, None, "inline", "xline", None),
        P(None, "inline"),
    )
    return jax.shard_map(
        on_device,
        mesh=mesh,
        in_specs=placed,
        out_specs=(P("segment", "inline", "xline", None), P("segment", "inline", "xline", None)),
        check_vma=False,
    )
```

profile of v0, /device:TPU:7, one launch (start us, length us, event | category | flops | bytes accessed | tf_op | source)
XLA Modules:
  0.0 152.7 jit_solution(5347754070597727528)
XLA Ops:
  2.7 3.2 %collective-permute-start.14 = (f32[4,4,1,1024]{3,2,1,0:T(1,128)S(1)}, f32[4,4,1,1024]{3,2,1,0:T(1,128)S(1)}, u32[]{:S(2)}, u32[]{:S(2)}) collective-permute-start(f32[4,4,1,1024]{3,2,1,0:T(1,128)S(1)} %get-tuple-element.40), channel_id=1, source_target_pairs={{0,1},{1,2},{2,3},{4,5},{5,6},{6,7},{8,9},{9,10},{10,11},{12,13},{... | collective-permute-start | bytes 196616 | tf_op jit(solution)/shard_map/ppermute | solution.py:20
  5.9 1.3 collective-permute-start.15
  7.3 4.0 %collective-permute-start = (f32[4,4,1,1024]{3,2,1,0:T(1,128)S(1)}, f32[4,4,1,1024]{3,2,1,0:T(1,128)S(1)}, u32[]{:S(2)}, u32[]{:S(2)}) collective-permute-start(f32[4,4,1,1024]{3,2,1,0:T(1,128)S(1)} %get-tuple-element.44), channel_id=1, source_target_pairs={{0,1},{1,2},{2,3},{4,5},{5,6},{6,7},{8,9},{9,10},{10,11},{12,13},{... | collective-permute-start | bytes 196616 | tf_op jit(solution)/shard_map/ppermute | solution.py:20
  11.3 1.3 collective-permute-start.1
  31.9 11.4 %collective-permute-start.17 = (f32[4,1,6,1024]{3,2,1,0:T(8,128)S(1)}, f32[4,1,6,1024]{3,2,1,0:T(8,128)S(1)}, u32[]{:S(2)}, u32[]{:S(2)}) collective-permute-start(f32[4,1,6,1024]{3,2,1,0:T(8,128)S(1)} %get-tuple-element.33), channel_id=1, source_target_pairs={{4,0},{8,4},{12,8},{16,12},{20,16},{24,20},{28,24},{32,28},{36,32}... | collective-permute-start | bytes 294920 | tf_op jit(solution)/shard_map/ppermute | solution.py:29
  43.7 1.9 %collective-permute-start.2 = (f32[4,1,6,1024]{3,2,1,0:T(8,128)S(1)}, f32[4,1,6,1024]{3,2,1,0:T(8,128)S(1)}, u32[]{:S(2)}, u32[]{:S(2)}) collective-permute-start(f32[4,1,6,1024]{3,2,1,0:T(8,128)S(1)} %get-tuple-element.36), channel_id=1, source_target_pairs={{0,4},{4,8},{8,12},{12,16},{16,20},{20,24},{24,28},{28,32},{32,36}... | collective-permute-start | bytes 294920 | tf_op jit(solution)/shard_map/ppermute | solution.py:29
  45.7 5.5 %collective-permute-start.3 = (f32[4,1,6,1024]{3,2,1,0:T(8,128)S(1)}, f32[4,1,6,1024]{3,2,1,0:T(8,128)S(1)}, u32[]{:S(2)}, u32[]{:S(2)}) collective-permute-start(f32[4,1,6,1024]{3,2,1,0:T(8,128)S(1)} %get-tuple-element.37), channel_id=1, source_target_pairs={{4,0},{8,4},{12,8},{16,12},{20,16},{24,20},{28,24},{32,28},{36,32}... | collective-permute-start | bytes 294920 | tf_op jit(solution)/shard_map/ppermute | solution.py:29
  51.1 1.9 %collective-permute-start.16 = (f32[4,1,6,1024]{3,2,1,0:T(8,128)S(1)}, f32[4,1,6,1024]{3,2,1,0:T(8,128)S(1)}, u32[]{:S(2)}, u32[]{:S(2)}) collective-permute-start(f32[4,1,6,1024]{3,2,1,0:T(8,128)S(1)} %get-tuple-element.32), channel_id=1, source_target_pairs={{0,4},{4,8},{8,12},{12,16},{16,20},{20,24},{24,28},{28,32},{32,36}... | collective-permute-start | bytes 294920 | tf_op jit(solution)/shard_map/ppermute | solution.py:29
  53.1 5.9 %collective-permute-done.16 = f32[4,1,6,1024]{3,2,1,0:T(8,128)S(1)} collective-permute-done((f32[4,1,6,1024]{3,2,1,0:T(8,128)S(1)}, f32[4,1,6,1024]{3,2,1,0:T(8,128)S(1)}, u32[]{:S(2)}, u32[]{:S(2)}) %collective-permute-start.16) | collective-permute-done | bytes 98336 | tf_op jit(solution)/shard_map/ppermute | solution.py:29
  59.8 4.0 %collective-permute-start.18 = (f32[4,4,1,1024]{3,2,1,0:T(1,128)S(1)}, f32[4,4,1,1024]{3,2,1,0:T(1,128)S(1)}, u32[]{:S(2)}, u32[]{:S(2)}) collective-permute-start(f32[4,4,1,1024]{3,2,1,0:T(1,128)S(1)} %get-tuple-element.38), channel_id=1, source_target_pairs={{0,1},{1,2},{2,3},{4,5},{5,6},{6,7},{8,9},{9,10},{10,11},{12,13},{... | collective-permute-start | bytes 196616 | tf_op jit(solution)/shard_map/ppermute | solution.py:20
  63.8 1.3 collective-permute-start.19
  65.3 3.5 %collective-permute-done.19 = f32[4,4,1,1024]{3,2,1,0:T(1,128)S(1)} collective-permute-done((f32[4,4,1,1024]{3,2,1,0:T(1,128)S(1)}, f32[4,4,1,1024]{3,2,1,0:T(1,128)S(1)}, u32[]{:S(2)}, u32[]{:S(2)}) %collective-permute-start.19) | collective-permute-done | bytes 65568 | tf_op jit(solution)/shard_map/ppermute | solution.py:21
  69.0 1.9 %collective-permute-start.21 = (f32[4,1,6,1024]{3,2,1,0:T(8,128)S(1)}, f32[4,1,6,1024]{3,2,1,0:T(8,128)S(1)}, u32[]{:S(2)}, u32[]{:S(2)}) collective-permute-start(f32[4,1,6,1024]{3,2,1,0:T(8,128)S(1)} %get-tuple-element.31), channel_id=1, source_target_pairs={{4,0},{8,4},{12,8},{16,12},{20,16},{24,20},{28,24},{32,28},{36,32}... | collective-permute-start | bytes 294920 | tf_op jit(solution)/shard_map/ppermute | solution.py:29
  71.3 3.4 %collective-permute-start.20 = (f32[4,1,6,1024]{3,2,1,0:T(8,128)S(1)}, f32[4,1,6,1024]{3,2,1,0:T(8,128)S(1)}, u32[]{:S(2)}, u32[]{:S(2)}) collective-permute-start(f32[4,1,6,1024]{3,2,1,0:T(8,128)S(1)} %get-tuple-element.30), channel_id=1, source_target_pairs={{0,4},{4,8},{8,12},{12,16},{16,20},{20,24},{24,28},{28,32},{32,36}... | collective-permute-start | bytes 294920 | tf_op jit(solution)/shard_map/ppermute | solution.py:29
  74.8 4.4 %collective-permute-done.20 = f32[4,1,6,1024]{3,2,1,0:T(8,128)S(1)} collective-permute-done((f32[4,1,6,1024]{3,2,1,0:T(8,128)S(1)}, f32[4,1,6,1024]{3,2,1,0:T(8,128)S(1)}, u32[]{:S(2)}, u32[]{:S(2)}) %collective-permute-start.20) | collective-permute-done | bytes 98336 | tf_op jit(solution)/shard_map/ppermute | solution.py:29
  80.0 1.3 collective-permute-start.22
  81.6 3.2 %collective-permute-start.4 = (f32[4,4,1,1024]{3,2,1,0:T(1,128)S(1)}, f32[4,4,1,1024]{3,2,1,0:T(1,128)S(1)}, u32[]{:S(2)}, u32[]{:S(2)}) collective-permute-start(f32[4,4,1,1024]{3,2,1,0:T(1,128)S(1)} %get-tuple-element.42), channel_id=1, source_target_pairs={{0,1},{1,2},{2,3},{4,5},{5,6},{6,7},{8,9},{9,10},{10,11},{12,13},{... | collective-permute-start | bytes 196616 | tf_op jit(solution)/shard_map/ppermute | solution.py:20
  86.1 2.3 %collective-permute-done.22 = f32[4,4,1024]{2,1,0:T(4,128)S(1)} collective-permute-done((f32[4,4,1024]{2,1,0:T(4,128)S(1)}, f32[4,4,1024]{2,1,0:T(4,128)S(1)}, u32[]{:S(2)}, u32[]{:S(2)}) %collective-permute-start.22) | collective-permute-done | bytes 65568 | tf_op jit(solution)/shard_map/ppermute | solution.py:29
  88.4 3.2 %collective-permute-start.23 = (f32[1,4,2,1024]{3,2,1,0:T(2,128)S(1)}, f32[1,4,2,1024]{3,2,1,0:T(2,128)S(1)}, u32[]{:S(2)}, u32[]{:S(2)}) collective-permute-start(f32[1,4,2,1024]{3,2,1,0:T(2,128)S(1)} %get-tuple-element.88), channel_id=1, source_target_pairs={{0,1},{1,2},{2,3},{4,5},{5,6},{6,7},{8,9},{9,10},{10,11},{12,13},{... | collective-permute-start | bytes 98312 | tf_op jit(solution)/shard_map/ppermute | solution.py:20
  93.2 1.9 %collective-permute-start.6 = (f32[4,1,6,1024]{3,2,1,0:T(8,128)S(1)}, f32[4,1,6,1024]{3,2,1,0:T(8,128)S(1)}, u32[]{:S(2)}, u32[]{:S(2)}) collective-permute-start(f32[4,1,6,1024]{3,2,1,0:T(8,128)S(1)} %get-tuple-element.34), channel_id=1, source_target_pairs={{0,4},{4,8},{8,12},{12,16},{16,20},{20,24},{24,28},{28,32},{32,36}... | collective-permute-start | bytes 294920 | tf_op jit(solution)/shard_map/ppermute | solution.py:29
  95.2 5.5 %collective-permute-start.7 = (f32[4,1,6,1024]{3,2,1,0:T(8,128)S(1)}, f32[4,1,6,1024]{3,2,1,0:T(8,128)S(1)}, u32[]{:S(2)}, u32[]{:S(2)}) collective-permute-start(f32[4,1,6,1024]{3,2,1,0:T(8,128)S(1)} %get-tuple-element.35), channel_id=1, source_target_pairs={{4,0},{8,4},{12,8},{16,12},{20,16},{24,20},{28,24},{32,28},{36,32}... | collective-permute-start | bytes 294920 | tf_op jit(solution)/shard_map/ppermute | solution.py:29
  100.8 1.9 %collective-permute-start.25 = (f32[1,2,8,1024]{3,2,1,0:T(8,128)S(1)}, f32[1,2,8,1024]{3,2,1,0:T(8,128)S(1)}, u32[]{:S(2)}, u32[]{:S(2)}) collective-permute-start(f32[1,2,8,1024]{3,2,1,0:T(8,128)S(1)} %get-tuple-element.82), channel_id=1, source_target_pairs={{0,4},{4,8},{8,12},{12,16},{16,20},{20,24},{24,28},{28,32},{32,36}... | collective-permute-start | bytes 196616 | tf_op jit(solution)/shard_map/ppermute | solution.py:29
  102.7 5.5 %collective-permute-start.26 = (f32[1,2,8,1024]{3,2,1,0:T(8,128)S(1)}, f32[1,2,8,1024]{3,2,1,0:T(8,128)S(1)}, u32[]{:S(2)}, u32[]{:S(2)}) collective-permute-start(f32[1,2,8,1024]{3,2,1,0:T(8,128)S(1)} %get-tuple-element.83), channel_id=1, source_target_pairs={{4,0},{8,4},{12,8},{16,12},{20,16},{24,20},{28,24},{32,28},{36,32}... | collective-permute-start | bytes 196616 | tf_op jit(solution)/shard_map/ppermute | solution.py:29
  110.3 7.5 %collective-permute-done.8 = f32[4,4,1024]{2,1,0:T(4,128)S(1)} collective-permute-done((f32[4,4,1024]{2,1,0:T(4,128)S(1)}, f32[4,4,1024]{2,1,0:T(4,128)S(1)}, u32[]{:S(2)}, u32[]{:S(2)}) %collective-permute-start.8) | collective-permute-done | bytes 65568 | tf_op jit(solution)/shard_map/ppermute | solution.py:29
  117.8 4.3 %collective-permute-start.9 = (f32[1,4,2,1024]{3,2,1,0:T(2,128)S(1)}, f32[1,4,2,1024]{3,2,1,0:T(2,128)S(1)}, u32[]{:S(2)}, u32[]{:S(2)}) collective-permute-start(f32[1,4,2,1024]{3,2,1,0:T(2,128)S(1)} %get-tuple-element.90), channel_id=1, source_target_pairs={{0,1},{1,2},{2,3},{4,5},{5,6},{6,7},{8,9},{9,10},{10,11},{12,13},{... | collective-permute-start | bytes 98312 | tf_op jit(solution)/shard_map/ppermute | solution.py:20
  123.5 3.3 %collective-permute-done.10 = f32[1,4,2,1024]{3,2,1,0:T(2,128)S(1)} collective-permute-done((f32[1,4,2,1024]{3,2,1,0:T(2,128)S(1)}, f32[1,4,2,1024]{3,2,1,0:T(2,128)S(1)}, u32[]{:S(2)}, u32[]{:S(2)}) %collective-permute-start.10) | collective-permute-done | bytes 32800 | tf_op jit(solution)/shard_map/ppermute | solution.py:21
  126.9 1.9 %collective-permute-start.12 = (f32[1,2,8,1024]{3,2,1,0:T(8,128)S(1)}, f32[1,2,8,1024]{3,2,1,0:T(8,128)S(1)}, u32[]{:S(2)}, u32[]{:S(2)}) collective-permute-start(f32[1,2,8,1024]{3,2,1,0:T(8,128)S(1)} %get-tuple-element.87), channel_id=1, source_target_pairs={{4,0},{8,4},{12,8},{16,12},{20,16},{24,20},{28,24},{32,28},{36,32}... | collective-permute-start | bytes 196616 | tf_op jit(solution)/shard_map/ppermute | solution.py:29
  128.9 3.5 %collective-permute-start.11 = (f32[1,2,8,1024]{3,2,1,0:T(8,128)S(1)}, f32[1,2,8,1024]{3,2,1,0:T(8,128)S(1)}, u32[]{:S(2)}, u32[]{:S(2)}) collective-permute-start(f32[1,2,8,1024]{3,2,1,0:T(8,128)S(1)} %get-tuple-element.86), channel_id=1, source_target_pairs={{0,4},{4,8},{8,12},{12,16},{16,20},{20,24},{24,28},{28,32},{32,36}... | collective-permute-start | bytes 196616 | tf_op jit(solution)/shard_map/ppermute | solution.py:29
  132.5 3.5 %collective-permute-done.11 = f32[1,2,8,1024]{3,2,1,0:T(8,128)S(1)} collective-permute-done((f32[1,2,8,1024]{3,2,1,0:T(8,128)S(1)}, f32[1,2,8,1024]{3,2,1,0:T(8,128)S(1)}, u32[]{:S(2)}, u32[]{:S(2)}) %collective-permute-start.11) | collective-permute-done | bytes 65568 | tf_op jit(solution)/shard_map/ppermute | solution.py:29
  139.4 1.6 %broadcast_multiply_fusion = (f32[6,8,8,1024]{3,2,1,0:T(8,128)S(1)}, f32[6,8,8,1024]{3,2,1,0:T(8,128)S(1)}, f32[6,8,8,1024]{3,2,1,0:T(8,128)S(1)}, f32[6,8,8,1024]{3,2,1,0:T(8,128)S(1)}) fusion(f32[6,8,8,1024]{3,2,1,0:T(8,128)S(1)} %get-tuple-element.4, pred[8]{0:T(512)(128)(4,1)S(1)} %get-tuple-element.111, f32[6,8,8,1024]{3,2,1,0:T(8,128)S(1)} %get-tuple-element.5, ...), kind=kLoop, calls=%fused_computation.62 | loop fusion | flops 4718592 | bytes 12582928 | tf_op jit(solution)/shard_map/mul | solution.py:133
  141.0 1.7 %fusion.16 = (f32[6,8,8,1024]{3,2,1,0:T(8,128)S(1)}, f32[6,8,8,1024]{3,2,1,0:T(8,128)S(1)}) fusion(f32[6,8,8,1024]{3,2,1,0:T(8,128)S(1)} %get-tuple-element.2, f32[6,8,8,1024]{3,2,1,0:T(8,128)S(1)} %get-tuple-element.3, pred[1024]{0:T(1024)(128)(4,1)S(1)} %get-tuple-element.118, pred[1024]{0:T(1024)(128)(4,1)S(1)} %get-tuple-element.119, ...), kind=kLoop, calls=%fused_computation.28 | loop fusion | flops 4718592 | bytes 9439232 | tf_op jit(solution)/shard_map/mul | solution.py:133
  143.0 8.0 %collective-permute-start.13 = (f32[2,4,4,1024]{3,2,1,0:T(4,128)S(1)}, f32[2,4,4,1024]{3,2,1,0:T(4,128)S(1)}, u32[]{:S(2)}, u32[]{:S(2)}) collective-permute-start(f32[2,4,4,1024]{3,2,1,0:T(4,128)S(1)} %fusion.136), channel_id=1, source_target_pairs={{256,0},{257,1},{258,2},{259,3},{260,4},{261,5},{262,6},{263,7},{2... | collective-permute-start | bytes 393224 | tf_op jit(solution)/shard_map/ppermute | solution.py:29
  (103 shorter events, 21.8 us)
Async XLA Ops:
  0.6 12.0 %copy-start = (s32[2,1]{0,1:T(1,128)S(1)}, s32[2,1]{0,1:T(1,128)}, u32[]{:S(2)}) copy-start(s32[2,1]{0,1:T(1,128)} %param.5) | copy-start | bytes 28
  2.7 29.0 %collective-permute-start.14 = (f32[4,4,1,1024]{3,2,1,0:T(1,128)S(1)}, f32[4,4,1,1024]{3,2,1,0:T(1,128)S(1)}, u32[]{:S(2)}, u32[]{:S(2)}) collective-permute-start(f32[4,4,1,1024]{3,2,1,0:T(1,128)S(1)} %get-tuple-element.40), channel_id=1, source_target_pairs={{0,1},{1,2},{2,3},{4,5},{5,6},{6,7},{8,9},{9,10},{10,11},{12,13},{... | collective-permute-start | bytes 196616 | tf_op jit(solution)/shard_map/ppermute | solution.py:20
  5.9 25.8 %collective-permute-start.15 = (f32[4,4,1,1024]{3,2,1,0:T(1,128)S(1)}, f32[4,4,1,1024]{3,2,1,0:T(1,128)S(1)}, u32[]{:S(2)}, u32[]{:S(2)}) collective-permute-start(f32[4,4,1,1024]{3,2,1,0:T(1,128)S(1)} %get-tuple-element.41), channel_id=1, source_target_pairs={{1,0},{2,1},{3,2},{5,4},{6,5},{7,6},{9,8},{10,9},{11,10},{13,12},{... | collective-permute-start | bytes 196616 | tf_op jit(solution)/shard_map/ppermute | solution.py:21
  7.3 36.0 %collective-permute-start = (f32[4,4,1,1024]{3,2,1,0:T(1,128)S(1)}, f32[4,4,1,1024]{3,2,1,0:T(1,128)S(1)}, u32[]{:S(2)}, u32[]{:S(2)}) collective-permute-start(f32[4,4,1,1024]{3,2,1,0:T(1,128)S(1)} %get-tuple-element.44), channel_id=1, source_target_pairs={{0,1},{1,2},{2,3},{4,5},{5,6},{6,7},{8,9},{9,10},{10,11},{12,13},{... | collective-permute-start | bytes 196616 | tf_op jit(solution)/shard_map/ppermute | solution.py:20
  11.3 32.1 %collective-permute-start.1 = (f32[4,4,1,1024]{3,2,1,0:T(1,128)S(1)}, f32[4,4,1,1024]{3,2,1,0:T(1,128)S(1)}, u32[]{:S(2)}, u32[]{:S(2)}) collective-permute-start(f32[4,4,1,1024]{3,2,1,0:T(1,128)S(1)} %get-tuple-element.45), channel_id=1, source_target_pairs={{1,0},{2,1},{3,2},{5,4},{6,5},{7,6},{9,8},{10,9},{11,10},{13,12},{... | collective-permute-start | bytes 196616 | tf_op jit(solution)/shard_map/ppermute | solution.py:21
  31.9 21.1 %collective-permute-start.17 = (f32[4,1,6,1024]{3,2,1,0:T(8,128)S(1)}, f32[4,1,6,1024]{3,2,1,0:T(8,128)S(1)}, u32[]{:S(2)}, u32[]{:S(2)}) collective-permute-start(f32[4,1,6,1024]{3,2,1,0:T(8,128)S(1)} %get-tuple-element.33), channel_id=1, source_target_pairs={{4,0},{8,4},{12,8},{16,12},{20,16},{24,20},{28,24},{32,28},{36,32}... | collective-permute-start | bytes 294920 | tf_op jit(solution)/shard_map/ppermute | solution.py:29
  43.7 21.4 %collective-permute-start.2 = (f32[4,1,6,1024]{3,2,1,0:T(8,128)S(1)}, f32[4,1,6,1024]{3,2,1,0:T(8,128)S(1)}, u32[]{:S(2)}, u32[]{:S(2)}) collective-permute-start(f32[4,1,6,1024]{3,2,1,0:T(8,128)S(1)} %get-tuple-element.36), channel_id=1, source_target_pairs={{0,4},{4,8},{8,12},{12,16},{16,20},{20,24},{24,28},{28,32},{32,36}... | collective-permute-start | bytes 294920 | tf_op jit(solution)/shard_map/ppermute | solution.py:29
  45.7 19.5 %collective-permute-start.3 = (f32[4,1,6,1024]{3,2,1,0:T(8,128)S(1)}, f32[4,1,6,1024]{3,2,1,0:T(8,128)S(1)}, u32[]{:S(2)}, u32[]{:S(2)}) collective-permute-start(f32[4,1,6,1024]{3,2,1,0:T(8,128)S(1)} %get-tuple-element.37), channel_id=1, source_target_pairs={{4,0},{8,4},{12,8},{16,12},{20,16},{24,20},{28,24},{32,28},{36,32}... | collective-permute-start | bytes 294920 | tf_op jit(solution)/shard_map/ppermute | solution.py:29
  51.1 7.8 %collective-permute-start.16 = (f32[4,1,6,1024]{3,2,1,0:T(8,128)S(1)}, f32[4,1,6,1024]{3,2,1,0:T(8,128)S(1)}, u32[]{:S(2)}, u32[]{:S(2)}) collective-permute-start(f32[4,1,6,1024]{3,2,1,0:T(8,128)S(1)} %get-tuple-element.32), channel_id=1, source_target_pairs={{0,4},{4,8},{8,12},{12,16},{16,20},{20,24},{24,28},{28,32},{32,36}... | collective-permute-start | bytes 294920 | tf_op jit(solution)/shard_map/ppermute | solution.py:29
  59.8 5.5 %collective-permute-start.18 = (f32[4,4,1,1024]{3,2,1,0:T(1,128)S(1)}, f32[4,4,1,1024]{3,2,1,0:T(1,128)S(1)}, u32[]{:S(2)}, u32[]{:S(2)}) collective-permute-start(f32[4,4,1,1024]{3,2,1,0:T(1,128)S(1)} %get-tuple-element.38), channel_id=1, source_target_pairs={{0,1},{1,2},{2,3},{4,5},{5,6},{6,7},{8,9},{9,10},{10,11},{12,13},{... | collective-permute-start | bytes 196616 | tf_op jit(solution)/shard_map/ppermute | solution.py:20
  63.8 5.0 %collective-permute-start.19 = (f32[4,4,1,1024]{3,2,1,0:T(1,128)S(1)}, f32[4,4,1,1024]{3,2,1,0:T(1,128)S(1)}, u32[]{:S(2)}, u32[]{:S(2)}) collective-permute-start(f32[4,4,1,1024]{3,2,1,0:T(1,128)S(1)} %get-tuple-element.39), channel_id=1, source_target_pairs={{1,0},{2,1},{3,2},{5,4},{6,5},{7,6},{9,8},{10,9},{11,10},{13,12},{... | collective-permute-start | bytes 196616 | tf_op jit(solution)/shard_map/ppermute | solution.py:21
  69.0 5.7 %collective-permute-start.21 = (f32[4,1,6,1024]{3,2,1,0:T(8,128)S(1)}, f32[4,1,6,1024]{3,2,1,0:T(8,128)S(1)}, u32[]{:S(2)}, u32[]{:S(2)}) collective-permute-start(f32[4,1,6,1024]{3,2,1,0:T(8,128)S(1)} %get-tuple-element.31), channel_id=1, source_target_pairs={{4,0},{8,4},{12,8},{16,12},{20,16},{24,20},{28,24},{32,28},{36,32}... | collective-permute-start | bytes 294920 | tf_op jit(solution)/shard_map/ppermute | solution.py:29
  71.3 7.8 %collective-permute-start.20 = (f32[4,1,6,1024]{3,2,1,0:T(8,128)S(1)}, f32[4,1,6,1024]{3,2,1,0:T(8,128)S(1)}, u32[]{:S(2)}, u32[]{:S(2)}) collective-permute-start(f32[4,1,6,1024]{3,2,1,0:T(8,128)S(1)} %get-tuple-element.30), channel_id=1, source_target_pairs={{0,4},{4,8},{8,12},{12,16},{16,20},{20,24},{24,28},{28,32},{32,36}... | collective-permute-start | bytes 294920 | tf_op jit(solution)/shard_map/ppermute | solution.py:29
  80.0 8.4 %collective-permute-start.22 = (f32[4,4,1024]{2,1,0:T(4,128)S(1)}, f32[4,4,1024]{2,1,0:T(4,128)S(1)}, u32[]{:S(2)}, u32[]{:S(2)}) collective-permute-start(f32[4,4,1024]{2,1,0:T(4,128)S(1)} %fusion.154), channel_id=1, source_target_pairs={{0,256},{1,257},{2,258},{3,259},{4,260},{5,261},{6,262},{7,263},{8... | collective-permute-start | bytes 196616 | tf_op jit(solution)/shard_map/ppermute | solution.py:29
  81.6 11.3 %collective-permute-start.4 = (f32[4,4,1,1024]{3,2,1,0:T(1,128)S(1)}, f32[4,4,1,1024]{3,2,1,0:T(1,128)S(1)}, u32[]{:S(2)}, u32[]{:S(2)}) collective-permute-start(f32[4,4,1,1024]{3,2,1,0:T(1,128)S(1)} %get-tuple-element.42), channel_id=1, source_target_pairs={{0,1},{1,2},{2,3},{4,5},{5,6},{6,7},{8,9},{9,10},{10,11},{12,13},{... | collective-permute-start | bytes 196616 | tf_op jit(solution)/shard_map/ppermute | solution.py:20
  84.8 8.1 %collective-permute-start.5 = (f32[4,4,1,1024]{3,2,1,0:T(1,128)S(1)}, f32[4,4,1,1024]{3,2,1,0:T(1,128)S(1)}, u32[]{:S(2)}, u32[]{:S(2)}) collective-permute-start(f32[4,4,1,1024]{3,2,1,0:T(1,128)S(1)} %get-tuple-element.43), channel_id=1, source_target_pairs={{1,0},{2,1},{3,2},{5,4},{6,5},{7,6},{9,8},{10,9},{11,10},{13,12},{... | collective-permute-start | bytes 196616 | tf_op jit(solution)/shard_map/ppermute | solution.py:21
  88.4 12.2 %collective-permute-start.23 = (f32[1,4,2,1024]{3,2,1,0:T(2,128)S(1)}, f32[1,4,2,1024]{3,2,1,0:T(2,128)S(1)}, u32[]{:S(2)}, u32[]{:S(2)}) collective-permute-start(f32[1,4,2,1024]{3,2,1,0:T(2,128)S(1)} %get-tuple-element.88), channel_id=1, source_target_pairs={{0,1},{1,2},{2,3},{4,5},{5,6},{6,7},{8,9},{9,10},{10,11},{12,13},{... | collective-permute-start | bytes 98312 | tf_op jit(solution)/shard_map/ppermute | solution.py:20
  91.6 9.0 %collective-permute-start.24 = (f32[1,4,2,1024]{3,2,1,0:T(2,128)S(1)}, f32[1,4,2,1024]{3,2,1,0:T(2,128)S(1)}, u32[]{:S(2)}, u32[]{:S(2)}) collective-permute-start(f32[1,4,2,1024]{3,2,1,0:T(2,128)S(1)} %get-tuple-element.89), channel_id=1, source_target_pairs={{1,0},{2,1},{3,2},{5,4},{6,5},{7,6},{9,8},{10,9},{11,10},{13,12},{... | collective-permute-start | bytes 98312 | tf_op jit(solution)/shard_map/ppermute | solution.py:21
  93.2 15.0 %collective-permute-start.6 = (f32[4,1,6,1024]{3,2,1,0:T(8,128)S(1)}, f32[4,1,6,1024]{3,2,1,0:T(8,128)S(1)}, u32[]{:S(2)}, u32[]{:S(2)}) collective-permute-start(f32[4,1,6,1024]{3,2,1,0:T(8,128)S(1)} %get-tuple-element.34), channel_id=1, source_target_pairs={{0,4},{4,8},{8,12},{12,16},{16,20},{20,24},{24,28},{28,32},{32,36}... | collective-permute-start | bytes 294920 | tf_op jit(solution)/shard_map/ppermute | solution.py:29
  95.2 13.0 %collective-permute-start.7 = (f32[4,1,6,1024]{3,2,1,0:T(8,128)S(1)}, f32[4,1,6,1024]{3,2,1,0:T(8,128)S(1)}, u32[]{:S(2)}, u32[]{:S(2)}) collective-permute-start(f32[4,1,6,1024]{3,2,1,0:T(8,128)S(1)} %get-tuple-element.35), channel_id=1, source_target_pairs={{4,0},{8,4},{12,8},{16,12},{20,16},{24,20},{28,24},{32,28},{36,32}... | collective-permute-start | bytes 294920 | tf_op jit(solution)/shard_map/ppermute | solution.py:29
  100.8 22.7 %collective-permute-start.25 = (f32[1,2,8,1024]{3,2,1,0:T(8,128)S(1)}, f32[1,2,8,1024]{3,2,1,0:T(8,128)S(1)}, u32[]{:S(2)}, u32[]{:S(2)}) collective-permute-start(f32[1,2,8,1024]{3,2,1,0:T(8,128)S(1)} %get-tuple-element.82), channel_id=1, source_target_pairs={{0,4},{4,8},{8,12},{12,16},{16,20},{20,24},{24,28},{28,32},{32,36}... | collective-permute-start | bytes 196616 | tf_op jit(solution)/shard_map/ppermute | solution.py:29
  102.7 7.6 %collective-permute-start.26 = (f32[1,2,8,1024]{3,2,1,0:T(8,128)S(1)}, f32[1,2,8,1024]{3,2,1,0:T(8,128)S(1)}, u32[]{:S(2)}, u32[]{:S(2)}) collective-permute-start(f32[1,2,8,1024]{3,2,1,0:T(8,128)S(1)} %get-tuple-element.83), channel_id=1, source_target_pairs={{4,0},{8,4},{12,8},{16,12},{20,16},{24,20},{28,24},{32,28},{36,32}... | collective-permute-start | bytes 196616 | tf_op jit(solution)/shard_map/ppermute | solution.py:29
  109.0 8.9 %collective-permute-start.8 = (f32[4,4,1024]{2,1,0:T(4,128)S(1)}, f32[4,4,1024]{2,1,0:T(4,128)S(1)}, u32[]{:S(2)}, u32[]{:S(2)}) collective-permute-start(f32[4,4,1024]{2,1,0:T(4,128)S(1)} %fusion.145), channel_id=1, source_target_pairs={{0,256},{1,257},{2,258},{3,259},{4,260},{5,261},{6,262},{7,263},{8... | collective-permute-start | bytes 196616 | tf_op jit(solution)/shard_map/ppermute | solution.py:29
  117.8 5.6 %collective-permute-start.9 = (f32[1,4,2,1024]{3,2,1,0:T(2,128)S(1)}, f32[1,4,2,1024]{3,2,1,0:T(2,128)S(1)}, u32[]{:S(2)}, u32[]{:S(2)}) collective-permute-start(f32[1,4,2,1024]{3,2,1,0:T(2,128)S(1)} %get-tuple-element.90), channel_id=1, source_target_pairs={{0,1},{1,2},{2,3},{4,5},{5,6},{6,7},{8,9},{9,10},{10,11},{12,13},{... | collective-permute-start | bytes 98312 | tf_op jit(solution)/shard_map/ppermute | solution.py:20
  122.1 4.7 %collective-permute-start.10 = (f32[1,4,2,1024]{3,2,1,0:T(2,128)S(1)}, f32[1,4,2,1024]{3,2,1,0:T(2,128)S(1)}, u32[]{:S(2)}, u32[]{:S(2)}) collective-permute-start(f32[1,4,2,1024]{3,2,1,0:T(2,128)S(1)} %get-tuple-element.91), channel_id=1, source_target_pairs={{1,0},{2,1},{3,2},{5,4},{6,5},{7,6},{9,8},{10,9},{11,10},{13,12},{... | collective-permute-start | bytes 98312 | tf_op jit(solution)/shard_map/ppermute | solution.py:21
  126.9 5.6 %collective-permute-start.12 = (f32[1,2,8,1024]{3,2,1,0:T(8,128)S(1)}, f32[1,2,8,1024]{3,2,1,0:T(8,128)S(1)}, u32[]{:S(2)}, u32[]{:S(2)}) collective-permute-start(f32[1,2,8,1024]{3,2,1,0:T(8,128)S(1)} %get-tuple-element.87), channel_id=1, source_target_pairs={{4,0},{8,4},{12,8},{16,12},{20,16},{24,20},{28,24},{32,28},{36,32}... | collective-permute-start | bytes 196616 | tf_op jit(solution)/shard_map/ppermute | solution.py:29
  128.9 7.1 %collective-permute-start.11 = (f32[1,2,8,1024]{3,2,1,0:T(8,128)S(1)}, f32[1,2,8,1024]{3,2,1,0:T(8,128)S(1)}, u32[]{:S(2)}, u32[]{:S(2)}) collective-permute-start(f32[1,2,8,1024]{3,2,1,0:T(8,128)S(1)} %get-tuple-element.86), channel_id=1, source_target_pairs={{0,4},{4,8},{8,12},{12,16},{16,20},{20,24},{24,28},{28,32},{32,36}... | collective-permute-start | bytes 196616 | tf_op jit(solution)/shard_map/ppermute | solution.py:29
  143.0 9.0 %collective-permute-start.13 = (f32[2,4,4,1024]{3,2,1,0:T(4,128)S(1)}, f32[2,4,4,1024]{3,2,1,0:T(4,128)S(1)}, u32[]{:S(2)}, u32[]{:S(2)}) collective-permute-start(f32[2,4,4,1024]{3,2,1,0:T(4,128)S(1)} %fusion.136), channel_id=1, source_target_pairs={{256,0},{257,1},{258,2},{259,3},{260,4},{261,5},{262,6},{263,7},{2... | collective-permute-start | bytes 393224 | tf_op jit(solution)/shard_map/ppermute | solution.py:29
where the time goes:
time: 154 us; the launch traced here: 153 us
  starting transfers between devices  86.5 us (56%)
  waiting for transfers between devices  31.3 us (20%)
  other arithmetic  16.3 us (11%)
  between operations  15.9 us (10%)
  local copies, waits for them, and re-layouts  2.77 us (2%)
    ppermute x15, starting transfers between devices, shifted_2(): lax.ppermute(value, axis, [(source, source + steps) for source in range(i...  56.9 us
    ppermute x15, waiting for transfers between devices, shifted_2(): lax.ppermute(value, axis, [(source, source + steps) for source in range(i...  24.4 us
    ppermute x6, starting transfers between devices, extended(): before = lax.ppermute(last, axis, up)  21.9 us
    ppermute x6, starting transfers between devices, extended(): after = lax.ppermute(initial, axis, down)  7.75 us
    ppermute x6, waiting for transfers between devices, extended(): after = lax.ppermute(initial, axis, down)  6.86 us
    mul x4, other arithmetic, attributes(): 0.25 * (neighbor(tensor, which_axis + 1, 1, up_open) + 2.0 * tensor + nei...  4.43 us
  transfers between devices with their start and end apart: 27, of which 8 were waited for; matrix products, arithmetic and copies ran while one was open for 6% of the time, Pallas kernels for 0%

commit v1 on v0

v1 whole, which is shorter than its diff:
```python
import jax
import jax.numpy as jnp
from jax import lax
from jax.sharding import PartitionSpec as P

STEPS = 2
HALO = 2


step_size = 0.15
epsilon = 1e-06


def shifted(source, which_axis, offset):
    length = source.shape[which_axis]
    margins = [(0, 0)] * source.ndim
    if offset > 0:
        margins[which_axis] = (0, offset)
        padded = jnp.pad(source, margins)
        return lax.slice_in_dim(padded, offset, offset + length, axis=which_axis)
    margins[which_axis] = (-offset, 0)
    padded = jnp.pad(source, margins)
    return lax.slice_in_dim(padded, 0, length, axis=which_axis)


def neighbor(source, which_axis, offset, opened):
    return jnp.where(opened, shifted(source, which_axis, offset), source)


def moved(value, d_inline, d_xline):
    n_i = lax.axis_size("inline")
    n_x = lax.axis_size("xline")
    if d_xline == 0:
        pairs = [(i, i + d_inline) for i in range(n_i) if 0 <= i + d_inline < n_i]
        return lax.ppermute(value, "inline", pairs)
    if d_inline == 0:
        pairs = [(x, x + d_xline) for x in range(n_x) if 0 <= x + d_xline < n_x]
        return lax.ppermute(value, "xline", pairs)
    pairs = []
    for i in range(n_i):
        for x in range(n_x):
            ti, tx = i + d_inline, x + d_xline
            if 0 <= ti < n_i and 0 <= tx < n_x:
                pairs.append((i * n_x + x, ti * n_x + tx))
    return lax.ppermute(value, ("inline", "xline"), pairs)


def gathered(block, width, corner):
    h = HALO
    rows, cols = block.shape[-3], block.shape[-2]
    ra, ca = block.ndim - 3, block.ndim - 2
    lead = block.shape[:-3]
    samples = block.shape[-1]
    last_rows = lax.dynamic_slice_in_dim(block, width - h, h, ra)
    first_rows = lax.slice_in_dim(block, 0, h, axis=ra)

    def cols_of(value, start, count):
        return lax.slice_in_dim(value, start, start + count, axis=ca)

    def corner_piece(rows_part, from_high_cols):
        start = cols - corner if from_high_cols else 0
        return cols_of(rows_part, start, corner)

    from_prev = moved(last_rows, 1, 0)
    from_next = moved(first_rows, -1, 0)
    from_left = moved(cols_of(block, cols - h, h), 0, 1)
    from_right = moved(cols_of(block, 0, h), 0, -1)
    c_prev_left = moved(corner_piece(lax.slice_in_dim(last_rows, h - corner, h, axis=ra), True), 1, 1)
    c_prev_right = moved(corner_piece(lax.slice_in_dim(last_rows, h - corner, h, axis=ra), False), 1, -1)
    c_next_left = moved(corner_piece(lax.slice_in_dim(first_rows, 0, corner, axis=ra), True), -1, 1)
    c_next_right = moved(corner_piece(lax.slice_in_dim(first_rows, 0, corner, axis=ra), False), -1, -1)

    def zeros(r, c):
        return jnp.zeros(lead + (r, c, samples), block.dtype)

    def band(top, middle, bottom):
        stacked = jnp.concatenate([top, middle, zeros(h, middle.shape[ca])], ra)
        return lax.dynamic_update_slice_in_dim(stacked, bottom, h + width, ra)

    def pad_corner(piece, at_high_cols, at_high_rows):
        row_pad = (0, h - corner) if at_high_rows else (h - corner, 0)
        col_pad = (0, h - corner) if at_high_cols else (h - corner, 0)
        margins = [(0, 0)] * len(lead) + [row_pad, col_pad, (0, 0)]
        return jnp.pad(piece, margins)

    center = band(from_prev, block, from_next)
    left = band(pad_corner(c_prev_left, False, False), from_left, pad_corner(c_next_left, False, True))
    right = band(pad_corner(c_prev_right, True, False), from_right, pad_corner(c_next_right, True, True))
    return jnp.concatenate([left, center, right], ca)


def face_masks(width, rows, cols, samples):
    h = HALO
    inline_pos = lax.axis_index("inline")
    inline_count = lax.axis_size("inline")
    xline_pos = lax.axis_index("xline")
    xline_count = lax.axis_size("xline")
    own_row = jnp.arange(rows + 2 * h, dtype=jnp.int32) - h
    row_up = jnp.logical_not((inline_pos == inline_count - 1) & (own_row == width - 1))
    row_down = jnp.logical_not((inline_pos == 0) & (own_row == 0))
    own_col = jnp.arange(cols + 2 * h, dtype=jnp.int32) - h
    col_up = jnp.logical_not((xline_pos == xline_count - 1) & (own_col == cols - 1))
    col_down = jnp.logical_not((xline_pos == 0) & (own_col == 0))
    sample = jnp.arange(samples, dtype=jnp.int32)
    return [
        (row_up[:, None, None], row_down[:, None, None]),
        (col_up[None, :, None], col_down[None, :, None]),
        ((sample < samples - 1)[None, None, :], (sample > 0)[None, None, :]),
    ]


def relax_step(values, coeffs, masks):
    change = jnp.zeros_like(values)
    for which_axis in range(3):
        kk = coeffs[which_axis]
        up_open, down_open = masks[which_axis]
        for offset, opened in ((1, up_open), (-1, down_open)):
            change = change + 0.5 * (kk + neighbor(kk, which_axis, offset, opened)) * (
                neighbor(values, which_axis, offset, opened) - values
            )
    return values + step_size * change


def attributes(grown, masks):
    grads = []
    for which_axis in range(3):
        up_open, down_open = masks[which_axis]
        grads.append(
            0.5
            * (neighbor(grown, which_axis, 1, up_open) - neighbor(grown, which_axis, -1, down_open))
        )
    seconds = []
    for which_axis in range(2):
        up_open, down_open = masks[which_axis]
        seconds.append(
            neighbor(grown, which_axis, 1, up_open)
            + neighbor(grown, which_axis, -1, down_open)
            - 2.0 * grown
        )
    combos = [(0, 0), (1, 1), (2, 2), (0, 1), (0, 2), (1, 2)]
    tensor = jnp.stack(
        [grads[first_index] * grads[second_index] for first_index, second_index in combos], 0
    )
    for which_axis in range(3):
        up_open, down_open = masks[which_axis]
        tensor = 0.25 * (
            neighbor(tensor, which_axis + 1, 1, up_open)
            + 2.0 * tensor
            + neighbor(tensor, which_axis + 1, -1, down_open)
        )
    trace = tensor[0] + tensor[1] + tensor[2]
    minors = (
        tensor[0] * tensor[1]
        - tensor[3] * tensor[3]
        + tensor[0] * tensor[2]
        - tensor[4] * tensor[4]
        + tensor[1] * tensor[2]
        - tensor[5] * tensor[5]
    )
    coherence = 1.0 - 3.0 * minors / (trace * trace + epsilon)
    curvature = (seconds[0] + seconds[1]) / (1.0 + grads[0] * grads[0] + grads[1] * grads[1]) ** 1.5
    return coherence, curvature


def on_device(survey, conduct, widths):
    h = HALO
    batch = lax.axis_index("segment")
    field = lax.dynamic_index_in_dim(survey, batch, 0, keepdims=False)
    coeffs = lax.dynamic_index_in_dim(conduct, batch, 1, keepdims=False).astype(jnp.float32)
    width = lax.dynamic_index_in_dim(widths[:, 0], batch, 0, keepdims=False)
    rows, cols, samples = field.shape
    live = (jnp.arange(rows, dtype=jnp.int32) < width)[:, None, None]
    masks = face_masks(width, rows, cols, samples)

    values = jnp.where(live, field, 0.0)
    grown = gathered(jnp.concatenate([values[None], coeffs], 0), width, 1)
    values, coeffs_grown = grown[0], grown[1:]
    for repeat in range(STEPS):
        values = relax_step(values, coeffs_grown, masks)
    smooth = values[h : h + rows, h : h + cols]

    grown = gathered(smooth, width, h)
    coherence, curvature = attributes(grown, masks)
    outcome = jnp.stack([coherence, curvature], 0)[:, h : h + rows, h : h + cols]
    outcome = jnp.where(live[None], outcome, 0.0)
    return (outcome[0][None], outcome[1][None])


def solution(mesh):
    placed = (
        P(None, "inline", "xline", None),
        P(None, None, "inline", "xline", None),
        P(None, "inline"),
    )
    return jax.shard_map(
        on_device,
        mesh=mesh,
        in_specs=placed,
        out_specs=(P("segment", "inline", "xline", None), P("segment", "inline", "xline", None)),
        check_vma=False,
    )
```

time: 154 us -> 83.6 us (0.54)
  the two profiles are of different devices: /device:TPU:7 before, /device:TPU:20 now
where the time goes in v1:
time: 83.6 us; the launch traced here: 83 us
  starting transfers between devices  64.1 us (77%)
  other arithmetic  8.58 us (10%)
  waiting for transfers between devices  4.25 us (5%)
  between operations  3.73 us (4%)
  local copies, waits for them, and re-layouts  2.3 us (3%)
    ppermute x8, starting transfers between devices, moved(): return lax.ppermute(value, ('inline', 'xline'), pairs)  40.6 us
    ppermute x4, starting transfers between devices, moved(): return lax.ppermute(value, 'inline', pairs)  12 us
    ppermute x4, starting transfers between devices, moved(): return lax.ppermute(value, 'xline', pairs)  11.5 us
    ppermute x4, waiting for transfers between devices, moved(): return lax.ppermute(value, 'inline', pairs)  4.21 us
    mul x3, other arithmetic, attributes(): 0.25 * (neighbor(tensor, which_axis + 1, 1, up_open) + 2.0 * tensor + nei...  2.21 us
  transfers between devices with their start and end apart: 16, of which 3 were waited for; matrix products, arithmetic and copies ran while one was open for 1% of the time, Pallas kernels for 0%

profile of v1, /device:TPU:20, one launch (start us, length us, event | category | flops | bytes accessed | tf_op | source)
XLA Modules:
  0.0 83.0 jit_solution(1749745420766025526)
XLA Ops:
  0.7 0.6 copy-done
  1.3 0.6 constant_dynamic-slice_fusion.3
  1.9 0.6 iota_compare_fusion.3
  2.5 0.9 %bitcast_convert_fusion = f32[3,4,4,1024]{3,2,1,0:T(4,128)S(1)} fusion(bf16[3,2,4,4,1024]{4,3,2,1,0:T(4,128)(2,1)} %param.4, s32[]{:T(128)S(6)} %select_n.135), kind=kLoop, calls=%fused_computation.152 | loop fusion | flops 49152 | bytes 294916 | tf_op jit(solution)/shard_map/convert_element_type | solution.py:169
  3.4 0.9 %dynamic-slice_select_fusion = f32[1,4,4,1024]{3,2,1,0:T(4,128)S(1)} fusion(f32[2,4,4,1024]{3,2,1,0:T(4,128)} %param.3, s32[]{:T(128)S(6)} %select_n.135, pred[4]{0:T(512)(128)(4,1)S(1)} %iota_compare_fusion.3), kind=kLoop, calls=%fused_computation.157 | loop fusion | flops 16384 | bytes 131080 | tf_op jit(solution)/shard_map/jit(_where)/select_n | solution.py:175
  4.4 12.1 %collective-permute-start.2 = (f32[4,1,1,1024]{3,2,1,0:T(1,128)S(1)}, f32[4,1,1,1024]{3,2,1,0:T(1,128)S(1)}, u32[]{:S(2)}, u32[]{:S(2)}) collective-permute-start(f32[4,1,1,1024]{3,2,1,0:T(1,128)S(1)} %get-tuple-element.16), channel_id=1, source_target_pairs={{4,1},{5,2},{6,3},{8,5},{9,6},{10,7},{12,9},{13,10},{14,11},{16,13... | collective-permute-start | bytes 49160 | tf_op jit(solution)/shard_map/ppermute | solution.py:45
  17.9 1.9 %collective-permute-start.3 = (f32[4,2,4,1024]{3,2,1,0:T(4,128)S(1)}, f32[4,2,4,1024]{3,2,1,0:T(4,128)S(1)}, u32[]{:S(2)}, u32[]{:S(2)}) collective-permute-start(f32[4,2,4,1024]{3,2,1,0:T(4,128)S(1)} %get-tuple-element.21), channel_id=1, source_target_pairs={{0,4},{4,8},{8,12},{12,16},{16,20},{20,24},{24,28},{28,32},{32,36}... | collective-permute-start | bytes 393224 | tf_op jit(solution)/shard_map/ppermute | solution.py:35
  19.9 1.9 %collective-permute-start = (f32[4,1,1,1024]{3,2,1,0:T(1,128)S(1)}, f32[4,1,1,1024]{3,2,1,0:T(1,128)S(1)}, u32[]{:S(2)}, u32[]{:S(2)}) collective-permute-start(f32[4,1,1,1024]{3,2,1,0:T(1,128)S(1)} %get-tuple-element.24), channel_id=1, source_target_pairs={{0,5},{1,6},{2,7},{4,9},{5,10},{6,11},{8,13},{9,14},{10,15},{12,17... | collective-permute-start | bytes 49160 | tf_op jit(solution)/shard_map/ppermute | solution.py:45
  21.8 1.9 %collective-permute-start.5 = (f32[4,1,1,1024]{3,2,1,0:T(1,128)S(1)}, f32[4,1,1,1024]{3,2,1,0:T(1,128)S(1)}, u32[]{:S(2)}, u32[]{:S(2)}) collective-permute-start(f32[4,1,1,1024]{3,2,1,0:T(1,128)S(1)} %get-tuple-element.25), channel_id=1, source_target_pairs={{1,4},{2,5},{3,6},{5,8},{6,9},{7,10},{9,12},{10,13},{11,14},{13,16... | collective-permute-start | bytes 49160 | tf_op jit(solution)/shard_map/ppermute | solution.py:45
  23.8 1.9 %collective-permute-start.1 = (f32[4,4,2,1024]{3,2,1,0:T(2,128)S(1)}, f32[4,4,2,1024]{3,2,1,0:T(2,128)S(1)}, u32[]{:S(2)}, u32[]{:S(2)}) collective-permute-start(f32[4,4,2,1024]{3,2,1,0:T(2,128)S(1)} %get-tuple-element.18), channel_id=1, source_target_pairs={{0,1},{1,2},{2,3},{4,5},{5,6},{6,7},{8,9},{9,10},{10,11},{12,13},{... | collective-permute-start | bytes 393224 | tf_op jit(solution)/shard_map/ppermute | solution.py:38
  27.2 3.9 %collective-permute-start.6 = (f32[4,4,2,1024]{3,2,1,0:T(2,128)S(1)}, f32[4,4,2,1024]{3,2,1,0:T(2,128)S(1)}, u32[]{:S(2)}, u32[]{:S(2)}) collective-permute-start(f32[4,4,2,1024]{3,2,1,0:T(2,128)S(1)} %get-tuple-element.19), channel_id=1, source_target_pairs={{1,0},{2,1},{3,2},{5,4},{6,5},{7,6},{9,8},{10,9},{11,10},{13,12},{... | collective-permute-start | bytes 393224 | tf_op jit(solution)/shard_map/ppermute | solution.py:38
  31.3 6.9 %collective-permute-start.7 = (f32[4,1,1,1024]{3,2,1,0:T(1,128)S(1)}, f32[4,1,1,1024]{3,2,1,0:T(1,128)S(1)}, u32[]{:S(2)}, u32[]{:S(2)}) collective-permute-start(f32[4,1,1,1024]{3,2,1,0:T(1,128)S(1)} %get-tuple-element.17), channel_id=1, source_target_pairs={{5,0},{6,1},{7,2},{9,4},{10,5},{11,6},{13,8},{14,9},{15,10},{17,12... | collective-permute-start | bytes 49160 | tf_op jit(solution)/shard_map/ppermute | solution.py:45
  38.3 4.1 %collective-permute-start.4 = (f32[4,2,4,1024]{3,2,1,0:T(4,128)S(1)}, f32[4,2,4,1024]{3,2,1,0:T(4,128)S(1)}, u32[]{:S(2)}, u32[]{:S(2)}) collective-permute-start(f32[4,2,4,1024]{3,2,1,0:T(4,128)S(1)} %get-tuple-element.20), channel_id=1, source_target_pairs={{4,0},{8,4},{12,8},{16,12},{20,16},{24,20},{28,24},{32,28},{36,32}... | collective-permute-start | bytes 393224 | tf_op jit(solution)/shard_map/ppermute | solution.py:35
  42.4 0.3 fusion.62
  42.6 2.5 %collective-permute-done.4 = f32[4,2,4,1024]{3,2,1,0:T(4,128)S(1)} collective-permute-done((f32[4,2,4,1024]{3,2,1,0:T(4,128)S(1)}, f32[4,2,4,1024]{3,2,1,0:T(4,128)S(1)}, u32[]{:S(2)}, u32[]{:S(2)}) %collective-permute-start.4) | collective-permute-done | bytes 131104 | tf_op jit(solution)/shard_map/ppermute | solution.py:35
  45.2 0.3 pad_maximum_fusion
  45.7 0.5 fusion.27
  46.2 0.5 fusion.45
  46.9 6.9 %collective-permute-start.10 = (f32[2,2,1024]{2,1,0:T(2,128)S(1)}, f32[2,2,1024]{2,1,0:T(2,128)S(1)}, u32[]{:S(2)}, u32[]{:S(2)}) collective-permute-start(f32[2,2,1024]{2,1,0:T(2,128)S(1)} %get-tuple-element.12), channel_id=1, source_target_pairs={{4,1},{5,2},{6,3},{8,5},{9,6},{10,7},{12,9},{13,10},{14,11},{16,13... | collective-permute-start | bytes 49160 | tf_op jit(solution)/shard_map/ppermute | solution.py:45
  53.8 1.9 %collective-permute-start.11 = (f32[2,4,1024]{2,1,0:T(4,128)S(1)}, f32[2,4,1024]{2,1,0:T(4,128)S(1)}, u32[]{:S(2)}, u32[]{:S(2)}) collective-permute-start(f32[2,4,1024]{2,1,0:T(4,128)S(1)} %constant_dynamic-slice_fusion.2), channel_id=1, source_target_pairs={{0,4},{4,8},{8,12},{12,16},{16,20},{20,24},{24,28},{28,32},{32,36}... | collective-permute-start | bytes 98312 | tf_op jit(solution)/shard_map/ppermute | solution.py:35
  55.8 1.9 %collective-permute-start.8 = (f32[2,2,1024]{2,1,0:T(2,128)S(1)}, f32[2,2,1024]{2,1,0:T(2,128)S(1)}, u32[]{:S(2)}, u32[]{:S(2)}) collective-permute-start(f32[2,2,1024]{2,1,0:T(2,128)S(1)} %get-tuple-element.26), channel_id=1, source_target_pairs={{0,5},{1,6},{2,7},{4,9},{5,10},{6,11},{8,13},{9,14},{10,15},{12,17... | collective-permute-start | bytes 49160 | tf_op jit(solution)/shard_map/ppermute | solution.py:45
  57.7 1.9 %collective-permute-start.13 = (f32[2,2,1024]{2,1,0:T(2,128)S(1)}, f32[2,2,1024]{2,1,0:T(2,128)S(1)}, u32[]{:S(2)}, u32[]{:S(2)}) collective-permute-start(f32[2,2,1024]{2,1,0:T(2,128)S(1)} %get-tuple-element.27), channel_id=1, source_target_pairs={{1,4},{2,5},{3,6},{5,8},{6,9},{7,10},{9,12},{10,13},{11,14},{13,16... | collective-permute-start | bytes 49160 | tf_op jit(solution)/shard_map/ppermute | solution.py:45
  59.6 1.9 %collective-permute-start.9 = (f32[4,2,1024]{2,1,0:T(2,128)S(1)}, f32[4,2,1024]{2,1,0:T(2,128)S(1)}, u32[]{:S(2)}, u32[]{:S(2)}) collective-permute-start(f32[4,2,1024]{2,1,0:T(2,128)S(1)} %get-tuple-element.14), channel_id=1, source_target_pairs={{0,1},{1,2},{2,3},{4,5},{5,6},{6,7},{8,9},{9,10},{10,11},{12,13},{... | collective-permute-start | bytes 98312 | tf_op jit(solution)/shard_map/ppermute | solution.py:38
  61.7 3.8 %collective-permute-start.14 = (f32[4,2,1024]{2,1,0:T(2,128)S(1)}, f32[4,2,1024]{2,1,0:T(2,128)S(1)}, u32[]{:S(2)}, u32[]{:S(2)}) collective-permute-start(f32[4,2,1024]{2,1,0:T(2,128)S(1)} %get-tuple-element.15), channel_id=1, source_target_pairs={{1,0},{2,1},{3,2},{5,4},{6,5},{7,6},{9,8},{10,9},{11,10},{13,12},{... | collective-permute-start | bytes 98312 | tf_op jit(solution)/shard_map/ppermute | solution.py:38
  65.6 6.9 %collective-permute-start.15 = (f32[2,2,1024]{2,1,0:T(2,128)S(1)}, f32[2,2,1024]{2,1,0:T(2,128)S(1)}, u32[]{:S(2)}, u32[]{:S(2)}) collective-permute-start(f32[2,2,1024]{2,1,0:T(2,128)S(1)} %get-tuple-element.13), channel_id=1, source_target_pairs={{5,0},{6,1},{7,2},{9,4},{10,5},{11,6},{13,8},{14,9},{15,10},{17,12... | collective-permute-start | bytes 49160 | tf_op jit(solution)/shard_map/ppermute | solution.py:45
  72.6 4.1 %collective-permute-start.12 = (f32[2,4,1024]{2,1,0:T(4,128)S(1)}, f32[2,4,1024]{2,1,0:T(4,128)S(1)}, u32[]{:S(2)}, u32[]{:S(2)}) collective-permute-start(f32[2,4,1024]{2,1,0:T(4,128)S(1)} %slice.289), channel_id=1, source_target_pairs={{4,0},{8,4},{12,8},{16,12},{20,16},{24,20},{28,24},{32,28},{36,32}... | collective-permute-start | bytes 98312 | tf_op jit(solution)/shard_map/ppermute | solution.py:35
  76.8 1.6 %collective-permute-done.12 = f32[2,4,1024]{2,1,0:T(4,128)S(1)} collective-permute-done((f32[2,4,1024]{2,1,0:T(4,128)S(1)}, f32[2,4,1024]{2,1,0:T(4,128)S(1)}, u32[]{:S(2)}, u32[]{:S(2)}) %collective-permute-start.12) | collective-permute-done | bytes 32800 | tf_op jit(solution)/shard_map/ppermute | solution.py:35
  78.5 0.4 multiply_bitcast_fusion
  79.8 0.5 broadcast_multiply_fusion.1
  80.3 0.8 broadcast_multiply_fusion
  81.1 0.9 %fusion.7 = f32[6,8,8,1024]{3,2,1,0:T(8,128)S(1)} fusion(f32[6,8,8,1024]{3,2,1,0:T(8,128)S(1)} %get-tuple-element.2, f32[6,8,8,1024]{3,2,1,0:T(8,128)S(1)} %get-tuple-element.3, pred[1024]{0:T(1024)(128)(4,1)S(1)} %get-tuple-element.34, pred[1024]{0:T(1024)(128)(4,1)S(1)} %get-tuple-element.35), kind=kLoop, calls=%fused_computation.13 | loop fusion | flops 2359296 | bytes 4720640 | tf_op jit(solution)/shard_map/mul | solution.py:146
  82.3 0.7 fusion.74
  (49 shorter events, 2.4 us)
Async XLA Ops:
  0.6 0.7 copy-start
  4.4 40.7 %collective-permute-start.2 = (f32[4,1,1,1024]{3,2,1,0:T(1,128)S(1)}, f32[4,1,1,1024]{3,2,1,0:T(1,128)S(1)}, u32[]{:S(2)}, u32[]{:S(2)}) collective-permute-start(f32[4,1,1,1024]{3,2,1,0:T(1,128)S(1)} %get-tuple-element.16), channel_id=1, source_target_pairs={{4,1},{5,2},{6,3},{8,5},{9,6},{10,7},{12,9},{13,10},{14,11},{16,13... | collective-permute-start | bytes 49160 | tf_op jit(solution)/shard_map/ppermute | solution.py:45
  17.9 9.3 %collective-permute-start.3 = (f32[4,2,4,1024]{3,2,1,0:T(4,128)S(1)}, f32[4,2,4,1024]{3,2,1,0:T(4,128)S(1)}, u32[]{:S(2)}, u32[]{:S(2)}) collective-permute-start(f32[4,2,4,1024]{3,2,1,0:T(4,128)S(1)} %get-tuple-element.21), channel_id=1, source_target_pairs={{0,4},{4,8},{8,12},{12,16},{16,20},{20,24},{24,28},{28,32},{32,36}... | collective-permute-start | bytes 393224 | tf_op jit(solution)/shard_map/ppermute | solution.py:35
  19.9 11.4 %collective-permute-start = (f32[4,1,1,1024]{3,2,1,0:T(1,128)S(1)}, f32[4,1,1,1024]{3,2,1,0:T(1,128)S(1)}, u32[]{:S(2)}, u32[]{:S(2)}) collective-permute-start(f32[4,1,1,1024]{3,2,1,0:T(1,128)S(1)} %get-tuple-element.24), channel_id=1, source_target_pairs={{0,5},{1,6},{2,7},{4,9},{5,10},{6,11},{8,13},{9,14},{10,15},{12,17... | collective-permute-start | bytes 49160 | tf_op jit(solution)/shard_map/ppermute | solution.py:45
  21.8 16.5 %collective-permute-start.5 = (f32[4,1,1,1024]{3,2,1,0:T(1,128)S(1)}, f32[4,1,1,1024]{3,2,1,0:T(1,128)S(1)}, u32[]{:S(2)}, u32[]{:S(2)}) collective-permute-start(f32[4,1,1,1024]{3,2,1,0:T(1,128)S(1)} %get-tuple-element.25), channel_id=1, source_target_pairs={{1,4},{2,5},{3,6},{5,8},{6,9},{7,10},{9,12},{10,13},{11,14},{13,16... | collective-permute-start | bytes 49160 | tf_op jit(solution)/shard_map/ppermute | solution.py:45
  23.8 18.5 %collective-permute-start.1 = (f32[4,4,2,1024]{3,2,1,0:T(2,128)S(1)}, f32[4,4,2,1024]{3,2,1,0:T(2,128)S(1)}, u32[]{:S(2)}, u32[]{:S(2)}) collective-permute-start(f32[4,4,2,1024]{3,2,1,0:T(2,128)S(1)} %get-tuple-element.18), channel_id=1, source_target_pairs={{0,1},{1,2},{2,3},{4,5},{5,6},{6,7},{8,9},{9,10},{10,11},{12,13},{... | collective-permute-start | bytes 393224 | tf_op jit(solution)/shard_map/ppermute | solution.py:38
  27.2 15.2 %collective-permute-start.6 = (f32[4,4,2,1024]{3,2,1,0:T(2,128)S(1)}, f32[4,4,2,1024]{3,2,1,0:T(2,128)S(1)}, u32[]{:S(2)}, u32[]{:S(2)}) collective-permute-start(f32[4,4,2,1024]{3,2,1,0:T(2,128)S(1)} %get-tuple-element.19), channel_id=1, source_target_pairs={{1,0},{2,1},{3,2},{5,4},{6,5},{7,6},{9,8},{10,9},{11,10},{13,12},{... | collective-permute-start | bytes 393224 | tf_op jit(solution)/shard_map/ppermute | solution.py:38
  31.3 13.9 %collective-permute-start.7 = (f32[4,1,1,1024]{3,2,1,0:T(1,128)S(1)}, f32[4,1,1,1024]{3,2,1,0:T(1,128)S(1)}, u32[]{:S(2)}, u32[]{:S(2)}) collective-permute-start(f32[4,1,1,1024]{3,2,1,0:T(1,128)S(1)} %get-tuple-element.17), channel_id=1, source_target_pairs={{5,0},{6,1},{7,2},{9,4},{10,5},{11,6},{13,8},{14,9},{15,10},{17,12... | collective-permute-start | bytes 49160 | tf_op jit(solution)/shard_map/ppermute | solution.py:45
  38.3 6.9 %collective-permute-start.4 = (f32[4,2,4,1024]{3,2,1,0:T(4,128)S(1)}, f32[4,2,4,1024]{3,2,1,0:T(4,128)S(1)}, u32[]{:S(2)}, u32[]{:S(2)}) collective-permute-start(f32[4,2,4,1024]{3,2,1,0:T(4,128)S(1)} %get-tuple-element.20), channel_id=1, source_target_pairs={{4,0},{8,4},{12,8},{16,12},{20,16},{24,20},{28,24},{32,28},{36,32}... | collective-permute-start | bytes 393224 | tf_op jit(solution)/shard_map/ppermute | solution.py:35
  46.9 31.5 %collective-permute-start.10 = (f32[2,2,1024]{2,1,0:T(2,128)S(1)}, f32[2,2,1024]{2,1,0:T(2,128)S(1)}, u32[]{:S(2)}, u32[]{:S(2)}) collective-permute-start(f32[2,2,1024]{2,1,0:T(2,128)S(1)} %get-tuple-element.12), channel_id=1, source_target_pairs={{4,1},{5,2},{6,3},{8,5},{9,6},{10,7},{12,9},{13,10},{14,11},{16,13... | collective-permute-start | bytes 49160 | tf_op jit(solution)/shard_map/ppermute | solution.py:45
  53.8 7.9 %collective-permute-start.11 = (f32[2,4,1024]{2,1,0:T(4,128)S(1)}, f32[2,4,1024]{2,1,0:T(4,128)S(1)}, u32[]{:S(2)}, u32[]{:S(2)}) collective-permute-start(f32[2,4,1024]{2,1,0:T(4,128)S(1)} %constant_dynamic-slice_fusion.2), channel_id=1, source_target_pairs={{0,4},{4,8},{8,12},{12,16},{16,20},{20,24},{24,28},{28,32},{32,36}... | collective-permute-start | bytes 98312 | tf_op jit(solution)/shard_map/ppermute | solution.py:35
  55.8 9.8 %collective-permute-start.8 = (f32[2,2,1024]{2,1,0:T(2,128)S(1)}, f32[2,2,1024]{2,1,0:T(2,128)S(1)}, u32[]{:S(2)}, u32[]{:S(2)}) collective-permute-start(f32[2,2,1024]{2,1,0:T(2,128)S(1)} %get-tuple-element.26), channel_id=1, source_target_pairs={{0,5},{1,6},{2,7},{4,9},{5,10},{6,11},{8,13},{9,14},{10,15},{12,17... | collective-permute-start | bytes 49160 | tf_op jit(solution)/shard_map/ppermute | solution.py:45
  57.7 14.8 %collective-permute-start.13 = (f32[2,2,1024]{2,1,0:T(2,128)S(1)}, f32[2,2,1024]{2,1,0:T(2,128)S(1)}, u32[]{:S(2)}, u32[]{:S(2)}) collective-permute-start(f32[2,2,1024]{2,1,0:T(2,128)S(1)} %get-tuple-element.27), channel_id=1, source_target_pairs={{1,4},{2,5},{3,6},{5,8},{6,9},{7,10},{9,12},{10,13},{11,14},{13,16... | collective-permute-start | bytes 49160 | tf_op jit(solution)/shard_map/ppermute | solution.py:45
  59.6 17.0 %collective-permute-start.9 = (f32[4,2,1024]{2,1,0:T(2,128)S(1)}, f32[4,2,1024]{2,1,0:T(2,128)S(1)}, u32[]{:S(2)}, u32[]{:S(2)}) collective-permute-start(f32[4,2,1024]{2,1,0:T(2,128)S(1)} %get-tuple-element.14), channel_id=1, source_target_pairs={{0,1},{1,2},{2,3},{4,5},{5,6},{6,7},{8,9},{9,10},{10,11},{12,13},{... | collective-permute-start | bytes 98312 | tf_op jit(solution)/shard_map/ppermute | solution.py:38
  61.7 14.9 %collective-permute-start.14 = (f32[4,2,1024]{2,1,0:T(2,128)S(1)}, f32[4,2,1024]{2,1,0:T(2,128)S(1)}, u32[]{:S(2)}, u32[]{:S(2)}) collective-permute-start(f32[4,2,1024]{2,1,0:T(2,128)S(1)} %get-tuple-element.15), channel_id=1, source_target_pairs={{1,0},{2,1},{3,2},{5,4},{6,5},{7,6},{9,8},{10,9},{11,10},{13,12},{... | collective-permute-start | bytes 98312 | tf_op jit(solution)/shard_map/ppermute | solution.py:38
  65.6 12.8 %collective-permute-start.15 = (f32[2,2,1024]{2,1,0:T(2,128)S(1)}, f32[2,2,1024]{2,1,0:T(2,128)S(1)}, u32[]{:S(2)}, u32[]{:S(2)}) collective-permute-start(f32[2,2,1024]{2,1,0:T(2,128)S(1)} %get-tuple-element.13), channel_id=1, source_target_pairs={{5,0},{6,1},{7,2},{9,4},{10,5},{11,6},{13,8},{14,9},{15,10},{17,12... | collective-permute-start | bytes 49160 | tf_op jit(solution)/shard_map/ppermute | solution.py:45
  72.6 5.8 %collective-permute-start.12 = (f32[2,4,1024]{2,1,0:T(4,128)S(1)}, f32[2,4,1024]{2,1,0:T(4,128)S(1)}, u32[]{:S(2)}, u32[]{:S(2)}) collective-permute-start(f32[2,4,1024]{2,1,0:T(4,128)S(1)} %slice.289), channel_id=1, source_target_pairs={{4,0},{8,4},{12,8},{16,12},{20,16},{24,20},{28,24},{32,28},{36,32}... | collective-permute-start | bytes 98312 | tf_op jit(solution)/shard_map/ppermute | solution.py:35

commit v2 on v1

--- a/solution.py
+++ b/solution.py
@@ -45,48 +45,18 @@
     return lax.ppermute(value, ("inline", "xline"), pairs)
 
 
-def gathered(block, width, corner):
+def gathered(block, width):
     h = HALO
     rows, cols = block.shape[-3], block.shape[-2]
     ra, ca = block.ndim - 3, block.ndim - 2
-    lead = block.shape[:-3]
-    samples = block.shape[-1]
-    last_rows = lax.dynamic_slice_in_dim(block, width - h, h, ra)
-    first_rows = lax.slice_in_dim(block, 0, h, axis=ra)
-
-    def cols_of(value, start, count):
-        return lax.slice_in_dim(value, start, start + count, axis=ca)
-
-    def corner_piece(rows_part, from_high_cols):
-        start = cols - corner if from_high_cols else 0
-        return cols_of(rows_part, start, corner)
-
-    from_prev = moved(last_rows, 1, 0)
-    from_next = moved(first_rows, -1, 0)
-    from_left = moved(cols_of(block, cols - h, h), 0, 1)
-    from_right = moved(cols_of(block, 0, h), 0, -1)
-    c_prev_left = moved(corner_piece(lax.slice_in_dim(last_rows, h - corner, h, axis=ra), True), 1, 1)
-    c_prev_right = moved(corner_piece(lax.slice_in_dim(last_rows, h - corner, h, axis=ra), False), 1, -1)
-    c_next_left = moved(corner_piece(lax.slice_in_dim(first_rows, 0, corner, axis=ra), True), -1, 1)
-    c_next_right = moved(corner_piece(lax.slice_in_dim(first_rows, 0, corner, axis=ra), False), -1, -1)
-
-    def zeros(r, c):
-        return jnp.zeros(lead + (r, c, samples), block.dtype)
-
-    def band(top, middle, bottom):
-        stacked = jnp.concatenate([top, middle, zeros(h, middle.shape[ca])], ra)
-        return lax.dynamic_update_slice_in_dim(stacked, bottom, h + width, ra)
-
-    def pad_corner(piece, at_high_cols, at_high_rows):
-        row_pad = (0, h - corner) if at_high_rows else (h - corner, 0)
-        col_pad = (0, h - corner) if at_high_cols else (h - corner, 0)
-        margins = [(0, 0)] * len(lead) + [row_pad, col_pad, (0, 0)]
-        return jnp.pad(piece, margins)
-
-    center = band(from_prev, block, from_next)
-    left = band(pad_corner(c_prev_left, False, False), from_left, pad_corner(c_next_left, False, True))
-    right = band(pad_corner(c_prev_right, True, False), from_right, pad_corner(c_next_right, True, True))
-    return jnp.concatenate([left, center, right], ca)
+    from_left = moved(lax.slice_in_dim(block, cols - h, cols, axis=ca), 0, 1)
+    from_right = moved(lax.slice_in_dim(block, 0, h, axis=ca), 0, -1)
+    wide = jnp.concatenate([from_left, block, from_right], ca)
+    from_prev = moved(lax.dynamic_slice_in_dim(wide, width - h, h, ra), 1, 0)
+    from_next = moved(lax.slice_in_dim(wide, 0, h, axis=ra), -1, 0)
+    tail = jnp.zeros_like(from_next)
+    stacked = jnp.concatenate([from_prev, wide, tail], ra)
+    return lax.dynamic_update_slice_in_dim(stacked, from_next, h + width, ra)
 
 
 def face_masks(width, rows, cols, samples):
@@ -173,13 +143,13 @@
     masks = face_masks(width, rows, cols, samples)
 
     values = jnp.where(live, field, 0.0)
-    grown = gathered(jnp.concatenate([values[None], coeffs], 0), width, 1)
+    grown = gathered(jnp.concatenate([values[None], coeffs], 0), width)
     values, coeffs_grown = grown[0], grown[1:]
     for repeat in range(STEPS):
         values = relax_step(values, coeffs_grown, masks)
     smooth = values[h : h + rows, h : h + cols]
 
-    grown = gathered(smooth, width, h)
+    grown = gathered(smooth, width)
     coherence, curvature = attributes(grown, masks)
     outcome = jnp.stack([coherence, curvature], 0)[:, h : h + rows, h : h + cols]
     outcome = jnp.where(live[None], outcome, 0.0)

time: 83.6 us -> 59.3 us (0.71)
  the two profiles are of different devices: /device:TPU:20 before, /device:TPU:6 now
where the time goes in v2:
time: 59.3 us; the launch traced here: 58.9 us
  starting transfers between devices  31.6 us (53%)
  waiting for transfers between devices  13.6 us (23%)
  other arithmetic  7.96 us (13%)
  between operations  3.52 us (6%)
  local copies, waits for them, and re-layouts  2.17 us (4%)
    ppermute x4, starting transfers between devices, moved(): return lax.ppermute(value, 'inline', pairs)  22 us
    ppermute x4, starting transfers between devices, moved(): return lax.ppermute(value, 'xline', pairs)  9.55 us
    ppermute x4, waiting for transfers between devices, moved(): return lax.ppermute(value, 'xline', pairs)  8.74 us
    ppermute x4, waiting for transfers between devices, moved(): return lax.ppermute(value, 'inline', pairs)  4.91 us
    mul x3, other arithmetic, attributes(): 0.25 * (neighbor(tensor, which_axis + 1, 1, up_open) + 2.0 * tensor + nei...  2.21 us
  transfers between devices with their start and end apart: 8, of which 8 were waited for; matrix products, arithmetic and copies ran while one was open for 1% of the time, Pallas kernels for 0%

profile of v2, /device:TPU:6, one launch (start us, length us, event | category | flops | bytes accessed | tf_op | source)
XLA Modules:
  0.0 58.9 jit_solution(647298092263101052)
XLA Ops:
  0.7 0.6 %copy-done = s32[2,1]{0,1:T(1,128)S(1)} copy-done((s32[2,1]{0,1:T(1,128)S(1)}, s32[2,1]{0,1:T(1,128)}, u32[]{:S(2)}) %copy-start) | copy-done | bytes 32
  1.3 0.6 constant_dynamic-slice_fusion.2
  1.9 0.6 %iota_compare_fusion.2 = pred[4]{0:T(512)(128)(4,1)S(1)} fusion(s32[]{:T(128)} %bitcast), kind=kLoop, calls=%fused_computation.151 | loop fusion | flops 4 | bytes 8 | tf_op jit(solution)/shard_map/lt | solution.py:142
  2.5 0.9 %bitcast_convert_fusion = f32[3,4,4,1024]{3,2,1,0:T(4,128)S(1)} fusion(bf16[3,2,4,4,1024]{4,3,2,1,0:T(4,128)(2,1)} %param.4, s32[]{:T(128)S(6)} %select_n.131), kind=kLoop, calls=%fused_computation.137 | loop fusion | flops 49152 | bytes 294916 | tf_op jit(solution)/shard_map/convert_element_type | solution.py:139
  3.4 0.9 %dynamic-slice_select_fusion = f32[1,4,4,1024]{3,2,1,0:T(4,128)S(1)} fusion(f32[2,4,4,1024]{3,2,1,0:T(4,128)} %param.3, s32[]{:T(128)S(6)} %select_n.131, pred[4]{0:T(512)(128)(4,1)S(1)} %iota_compare_fusion.2), kind=kLoop, calls=%fused_computation.138 | loop fusion | flops 16384 | bytes 131080 | tf_op jit(solution)/shard_map/jit(_where)/select_n | solution.py:145
  4.5 3.5 %collective-permute-start = (f32[4,4,2,1024]{3,2,1,0:T(2,128)S(1)}, f32[4,4,2,1024]{3,2,1,0:T(2,128)S(1)}, u32[]{:S(2)}, u32[]{:S(2)}) collective-permute-start(f32[4,4,2,1024]{3,2,1,0:T(2,128)S(1)} %get-tuple-element.16), channel_id=1, source_target_pairs={{0,1},{1,2},{2,3},{4,5},{5,6},{6,7},{8,9},{9,10},{10,11},{12,13},{... | collective-permute-start | bytes 393224 | tf_op jit(solution)/shard_map/ppermute | solution.py:38
  8.0 1.3 %collective-permute-start.1 = (f32[4,4,2,1024]{3,2,1,0:T(2,128)S(1)}, f32[4,4,2,1024]{3,2,1,0:T(2,128)S(1)}, u32[]{:S(2)}, u32[]{:S(2)}) collective-permute-start(f32[4,4,2,1024]{3,2,1,0:T(2,128)S(1)} %get-tuple-element.17), channel_id=1, source_target_pairs={{1,0},{2,1},{3,2},{5,4},{6,5},{7,6},{9,8},{10,9},{11,10},{13,12},{... | collective-permute-start | bytes 393224 | tf_op jit(solution)/shard_map/ppermute | solution.py:38
  10.7 4.1 %collective-permute-done.1 = f32[4,4,2,1024]{3,2,1,0:T(2,128)S(1)} collective-permute-done((f32[4,4,2,1024]{3,2,1,0:T(2,128)S(1)}, f32[4,4,2,1024]{3,2,1,0:T(2,128)S(1)}, u32[]{:S(2)}, u32[]{:S(2)}) %collective-permute-start.1) | collective-permute-done | bytes 131104 | tf_op jit(solution)/shard_map/ppermute | solution.py:38
  14.8 0.2 pad_maximum_fusion
  15.1 3.2 %collective-permute-start.2 = (f32[4,2,8,1024]{3,2,1,0:T(8,128)S(1)}, f32[4,2,8,1024]{3,2,1,0:T(8,128)S(1)}, u32[]{:S(2)}, u32[]{:S(2)}) collective-permute-start(f32[4,2,8,1024]{3,2,1,0:T(8,128)S(1)} %get-tuple-element.13), channel_id=1, source_target_pairs={{0,4},{4,8},{8,12},{12,16},{16,20},{20,24},{24,28},{28,32},{32,36}... | collective-permute-start | bytes 786440 | tf_op jit(solution)/shard_map/ppermute | solution.py:35
  19.0 10.4 %collective-permute-start.3 = (f32[4,2,8,1024]{3,2,1,0:T(8,128)S(1)}, f32[4,2,8,1024]{3,2,1,0:T(8,128)S(1)}, u32[]{:S(2)}, u32[]{:S(2)}) collective-permute-start(f32[4,2,8,1024]{3,2,1,0:T(8,128)S(1)} %get-tuple-element.12), channel_id=1, source_target_pairs={{4,0},{8,4},{12,8},{16,12},{20,16},{24,20},{28,24},{32,28},{36,32}... | collective-permute-start | bytes 786440 | tf_op jit(solution)/shard_map/ppermute | solution.py:35
  30.1 1.5 %collective-permute-done.2 = f32[4,2,8,1024]{3,2,1,0:T(8,128)S(1)} collective-permute-done((f32[4,2,8,1024]{3,2,1,0:T(8,128)S(1)}, f32[4,2,8,1024]{3,2,1,0:T(8,128)S(1)}, u32[]{:S(2)}, u32[]{:S(2)}) %collective-permute-start.2) | collective-permute-done | bytes 262176 | tf_op jit(solution)/shard_map/ppermute | solution.py:35
  31.6 0.2 maximum_maximum_fusion
  31.8 1.6 %collective-permute-done.3 = f32[4,2,8,1024]{3,2,1,0:T(8,128)S(1)} collective-permute-done((f32[4,2,8,1024]{3,2,1,0:T(8,128)S(1)}, f32[4,2,8,1024]{3,2,1,0:T(8,128)S(1)}, u32[]{:S(2)}, u32[]{:S(2)}) %collective-permute-start.3) | collective-permute-done | bytes 262176 | tf_op jit(solution)/shard_map/ppermute | solution.py:35
  33.6 0.5 fusion.27
  34.1 0.5 fusion.45
  34.7 3.5 %collective-permute-start.4 = (f32[4,2,1024]{2,1,0:T(2,128)S(1)}, f32[4,2,1024]{2,1,0:T(2,128)S(1)}, u32[]{:S(2)}, u32[]{:S(2)}) collective-permute-start(f32[4,2,1024]{2,1,0:T(2,128)S(1)} %get-tuple-element.14), channel_id=1, source_target_pairs={{0,1},{1,2},{2,3},{4,5},{5,6},{6,7},{8,9},{9,10},{10,11},{12,13},{... | collective-permute-start | bytes 98312 | tf_op jit(solution)/shard_map/ppermute | solution.py:38
  38.2 1.3 %collective-permute-start.5 = (f32[4,2,1024]{2,1,0:T(2,128)S(1)}, f32[4,2,1024]{2,1,0:T(2,128)S(1)}, u32[]{:S(2)}, u32[]{:S(2)}) collective-permute-start(f32[4,2,1024]{2,1,0:T(2,128)S(1)} %get-tuple-element.15), channel_id=1, source_target_pairs={{1,0},{2,1},{3,2},{5,4},{6,5},{7,6},{9,8},{10,9},{11,10},{13,12},{... | collective-permute-start | bytes 98312 | tf_op jit(solution)/shard_map/ppermute | solution.py:38
  39.5 0.3 collective-permute-done.4
  39.8 4.2 %collective-permute-done.5 = f32[4,2,1024]{2,1,0:T(2,128)S(1)} collective-permute-done((f32[4,2,1024]{2,1,0:T(2,128)S(1)}, f32[4,2,1024]{2,1,0:T(2,128)S(1)}, u32[]{:S(2)}, u32[]{:S(2)}) %collective-permute-start.5) | collective-permute-done | bytes 32800 | tf_op jit(solution)/shard_map/ppermute | solution.py:38
  44.1 1.9 %collective-permute-start.6 = (f32[2,8,1024]{2,1,0:T(8,128)S(1)}, f32[2,8,1024]{2,1,0:T(8,128)S(1)}, u32[]{:S(2)}, u32[]{:S(2)}) collective-permute-start(f32[2,8,1024]{2,1,0:T(8,128)S(1)} %get-tuple-element.21), channel_id=1, source_target_pairs={{0,4},{4,8},{8,12},{12,16},{16,20},{20,24},{24,28},{28,32},{32,36}... | collective-permute-start | bytes 196616 | tf_op jit(solution)/shard_map/ppermute | solution.py:35
  46.0 6.5 %collective-permute-start.7 = (f32[2,8,1024]{2,1,0:T(8,128)S(1)}, f32[2,8,1024]{2,1,0:T(8,128)S(1)}, u32[]{:S(2)}, u32[]{:S(2)}) collective-permute-start(f32[2,8,1024]{2,1,0:T(8,128)S(1)} %get-tuple-element.20), channel_id=1, source_target_pairs={{4,0},{8,4},{12,8},{16,12},{20,16},{24,20},{28,24},{32,28},{36,32}... | collective-permute-start | bytes 196616 | tf_op jit(solution)/shard_map/ppermute | solution.py:35
  52.5 0.3 collective-permute-done.6
  52.9 1.5 %collective-permute-done.7 = f32[2,8,1024]{2,1,0:T(8,128)S(1)} collective-permute-done((f32[2,8,1024]{2,1,0:T(8,128)S(1)}, f32[2,8,1024]{2,1,0:T(8,128)S(1)}, u32[]{:S(2)}, u32[]{:S(2)}) %collective-permute-start.7) | collective-permute-done | bytes 65568 | tf_op jit(solution)/shard_map/ppermute | solution.py:35
  54.4 0.4 multiply_bitcast_fusion
  55.0 0.2 bitcast_dynamic-update-slice_fusion.3
  55.3 0.2 bitcast_dynamic-update-slice_fusion.2
  55.7 0.5 broadcast_multiply_fusion.1
  56.2 0.8 %broadcast_multiply_fusion = (f32[6,8,8,1024]{3,2,1,0:T(8,128)S(1)}, f32[6,8,8,1024]{3,2,1,0:T(8,128)S(1)}) fusion(f32[6,8,8,1024]{3,2,1,0:T(8,128)S(1)} %get-tuple-element.4, pred[8]{0:T(512)(128)(4,1)S(1)} %get-tuple-element.22, f32[6,8,8,1024]{3,2,1,0:T(8,128)S(1)} %get-tuple-element.5, pred[8]{0:T(512)(128)(4,1)S(1)} %get-tuple-element.27), kind=kLoop, calls=%fused_computation.20 | loop fusion | flops 2359296 | bytes 6291472 | tf_op jit(solution)/shard_map/mul | solution.py:116
  57.0 0.9 %fusion.7 = f32[6,8,8,1024]{3,2,1,0:T(8,128)S(1)} fusion(f32[6,8,8,1024]{3,2,1,0:T(8,128)S(1)} %get-tuple-element.2, f32[6,8,8,1024]{3,2,1,0:T(8,128)S(1)} %get-tuple-element.3, pred[1024]{0:T(1024)(128)(4,1)S(1)} %get-tuple-element.24, pred[1024]{0:T(1024)(128)(4,1)S(1)} %get-tuple-element.25), kind=kLoop, calls=%fused_computation.13 | loop fusion | flops 2359296 | bytes 4720640 | tf_op jit(solution)/shard_map/mul | solution.py:116
  57.9 0.2 fusion.56
  58.2 0.7 %fusion.68 = (f32[1,4,4,1024]{3,2,1,0:T(4,128)}, f32[1,4,4,1024]{3,2,1,0:T(4,128)}) fusion(f32[2,4,4,1024]{3,2,1,0:T(4,128)S(1)} %fusion.62), kind=kLoop, calls=%fused_computation.154 | loop fusion | bytes 262144 | tf_op jit(solution)/shard_map/slice | solution.py:156
  (22 shorter events, 1.3 us)
Async XLA Ops:
  0.6 0.7 %copy-start = (s32[2,1]{0,1:T(1,128)S(1)}, s32[2,1]{0,1:T(1,128)}, u32[]{:S(2)}) copy-start(s32[2,1]{0,1:T(1,128)} %param.5) | copy-start | bytes 28
  4.5 6.2 %collective-permute-start = (f32[4,4,2,1024]{3,2,1,0:T(2,128)S(1)}, f32[4,4,2,1024]{3,2,1,0:T(2,128)S(1)}, u32[]{:S(2)}, u32[]{:S(2)}) collective-permute-start(f32[4,4,2,1024]{3,2,1,0:T(2,128)S(1)} %get-tuple-element.16), channel_id=1, source_target_pairs={{0,1},{1,2},{2,3},{4,5},{5,6},{6,7},{8,9},{9,10},{10,11},{12,13},{... | collective-permute-start | bytes 393224 | tf_op jit(solution)/shard_map/ppermute | solution.py:38
  8.0 6.9 %collective-permute-start.1 = (f32[4,4,2,1024]{3,2,1,0:T(2,128)S(1)}, f32[4,4,2,1024]{3,2,1,0:T(2,128)S(1)}, u32[]{:S(2)}, u32[]{:S(2)}) collective-permute-start(f32[4,4,2,1024]{3,2,1,0:T(2,128)S(1)} %get-tuple-element.17), channel_id=1, source_target_pairs={{1,0},{2,1},{3,2},{5,4},{6,5},{7,6},{9,8},{10,9},{11,10},{13,12},{... | collective-permute-start | bytes 393224 | tf_op jit(solution)/shard_map/ppermute | solution.py:38
  15.1 16.5 %collective-permute-start.2 = (f32[4,2,8,1024]{3,2,1,0:T(8,128)S(1)}, f32[4,2,8,1024]{3,2,1,0:T(8,128)S(1)}, u32[]{:S(2)}, u32[]{:S(2)}) collective-permute-start(f32[4,2,8,1024]{3,2,1,0:T(8,128)S(1)} %get-tuple-element.13), channel_id=1, source_target_pairs={{0,4},{4,8},{8,12},{12,16},{16,20},{20,24},{24,28},{28,32},{32,36}... | collective-permute-start | bytes 786440 | tf_op jit(solution)/shard_map/ppermute | solution.py:35
  19.0 14.5 %collective-permute-start.3 = (f32[4,2,8,1024]{3,2,1,0:T(8,128)S(1)}, f32[4,2,8,1024]{3,2,1,0:T(8,128)S(1)}, u32[]{:S(2)}, u32[]{:S(2)}) collective-permute-start(f32[4,2,8,1024]{3,2,1,0:T(8,128)S(1)} %get-tuple-element.12), channel_id=1, source_target_pairs={{4,0},{8,4},{12,8},{16,12},{20,16},{24,20},{28,24},{32,28},{36,32}... | collective-permute-start | bytes 786440 | tf_op jit(solution)/shard_map/ppermute | solution.py:35
  34.7 5.1 %collective-permute-start.4 = (f32[4,2,1024]{2,1,0:T(2,128)S(1)}, f32[4,2,1024]{2,1,0:T(2,128)S(1)}, u32[]{:S(2)}, u32[]{:S(2)}) collective-permute-start(f32[4,2,1024]{2,1,0:T(2,128)S(1)} %get-tuple-element.14), channel_id=1, source_target_pairs={{0,1},{1,2},{2,3},{4,5},{5,6},{6,7},{8,9},{9,10},{10,11},{12,13},{... | collective-permute-start | bytes 98312 | tf_op jit(solution)/shard_map/ppermute | solution.py:38
  38.2 5.8 %collective-permute-start.5 = (f32[4,2,1024]{2,1,0:T(2,128)S(1)}, f32[4,2,1024]{2,1,0:T(2,128)S(1)}, u32[]{:S(2)}, u32[]{:S(2)}) collective-permute-start(f32[4,2,1024]{2,1,0:T(2,128)S(1)} %get-tuple-element.15), channel_id=1, source_target_pairs={{1,0},{2,1},{3,2},{5,4},{6,5},{7,6},{9,8},{10,9},{11,10},{13,12},{... | collective-permute-start | bytes 98312 | tf_op jit(solution)/shard_map/ppermute | solution.py:38
  44.1 8.7 %collective-permute-start.6 = (f32[2,8,1024]{2,1,0:T(8,128)S(1)}, f32[2,8,1024]{2,1,0:T(8,128)S(1)}, u32[]{:S(2)}, u32[]{:S(2)}) collective-permute-start(f32[2,8,1024]{2,1,0:T(8,128)S(1)} %get-tuple-element.21), channel_id=1, source_target_pairs={{0,4},{4,8},{8,12},{12,16},{16,20},{20,24},{24,28},{28,32},{32,36}... | collective-permute-start | bytes 196616 | tf_op jit(solution)/shard_map/ppermute | solution.py:35
  46.0 8.4 %collective-permute-start.7 = (f32[2,8,1024]{2,1,0:T(8,128)S(1)}, f32[2,8,1024]{2,1,0:T(8,128)S(1)}, u32[]{:S(2)}, u32[]{:S(2)}) collective-permute-start(f32[2,8,1024]{2,1,0:T(8,128)S(1)} %get-tuple-element.20), channel_id=1, source_target_pairs={{4,0},{8,4},{12,8},{16,12},{20,16},{24,20},{28,24},{32,28},{36,32}... | collective-permute-start | bytes 196616 | tf_op jit(solution)/shard_map/ppermute | solution.py:35

commit v3 on v2

--- a/solution.py
+++ b/solution.py
@@ -45,30 +45,31 @@
     return lax.ppermute(value, ("inline", "xline"), pairs)
 
 
-def gathered(block, width):
-    h = HALO
-    rows, cols = block.shape[-3], block.shape[-2]
-    ra, ca = block.ndim - 3, block.ndim - 2
-    from_left = moved(lax.slice_in_dim(block, cols - h, cols, axis=ca), 0, 1)
-    from_right = moved(lax.slice_in_dim(block, 0, h, axis=ca), 0, -1)
-    wide = jnp.concatenate([from_left, block, from_right], ca)
-    from_prev = moved(lax.dynamic_slice_in_dim(wide, width - h, h, ra), 1, 0)
-    from_next = moved(lax.slice_in_dim(wide, 0, h, axis=ra), -1, 0)
-    tail = jnp.zeros_like(from_next)
-    stacked = jnp.concatenate([from_prev, wide, tail], ra)
-    return lax.dynamic_update_slice_in_dim(stacked, from_next, h + width, ra)
+def with_columns(block, depth):
+    ca = block.ndim - 2
+    cols = block.shape[ca]
+    from_left = moved(lax.slice_in_dim(block, cols - depth, cols, axis=ca), 0, 1)
+    from_right = moved(lax.slice_in_dim(block, 0, depth, axis=ca), 0, -1)
+    return jnp.concatenate([from_left, block, from_right], ca)
 
 
-def face_masks(width, rows, cols, samples):
-    h = HALO
+def with_rows(block, width, depth):
+    ra = block.ndim - 3
+    from_prev = moved(lax.dynamic_slice_in_dim(block, width - depth, depth, ra), 1, 0)
+    from_next = moved(lax.slice_in_dim(block, 0, depth, axis=ra), -1, 0)
+    stacked = jnp.concatenate([from_prev, block, jnp.zeros_like(from_next)], ra)
+    return lax.dynamic_update_slice_in_dim(stacked, from_next, depth + width, ra)
+
+
+def face_masks(width, rows, cols, samples, row_halo, col_halo):
     inline_pos = lax.axis_index("inline")
     inline_count = lax.axis_size("inline")
     xline_pos = lax.axis_index("xline")
     xline_count = lax.axis_size("xline")
-    own_row = jnp.arange(rows + 2 * h, dtype=jnp.int32) - h
+    own_row = jnp.arange(rows + 2 * row_halo, dtype=jnp.int32) - row_halo
     row_up = jnp.logical_not((inline_pos == inline_count - 1) & (own_row == width - 1))
     row_down = jnp.logical_not((inline_pos == 0) & (own_row == 0))
-    own_col = jnp.arange(cols + 2 * h, dtype=jnp.int32) - h
+    own_col = jnp.arange(cols + 2 * col_halo, dtype=jnp.int32) - col_halo
     col_up = jnp.logical_not((xline_pos == xline_count - 1) & (own_col == cols - 1))
     col_down = jnp.logical_not((xline_pos == 0) & (own_col == 0))
     sample = jnp.arange(samples, dtype=jnp.int32)
@@ -140,16 +141,18 @@
     width = lax.dynamic_index_in_dim(widths[:, 0], batch, 0, keepdims=False)
     rows, cols, samples = field.shape
     live = (jnp.arange(rows, dtype=jnp.int32) < width)[:, None, None]
-    masks = face_masks(width, rows, cols, samples)
 
     values = jnp.where(live, field, 0.0)
-    grown = gathered(jnp.concatenate([values[None], coeffs], 0), width)
+    wide = with_columns(jnp.concatenate([values[None], coeffs], 0), cols)
+    grown = with_rows(wide, width, h)
+    masks = face_masks(width, rows, cols, samples, h, cols)
     values, coeffs_grown = grown[0], grown[1:]
     for repeat in range(STEPS):
         values = relax_step(values, coeffs_grown, masks)
-    smooth = values[h : h + rows, h : h + cols]
+    smooth = values[h : h + rows, cols - h : 2 * cols + h]
 
-    grown = gathered(smooth, width)
+    grown = with_rows(smooth, width, h)
+    masks = face_masks(width, rows, cols, samples, h, h)
     coherence, curvature = attributes(grown, masks)
     outcome = jnp.stack([coherence, curvature], 0)[:, h : h + rows, h : h + cols]
     outcome = jnp.where(live[None], outcome, 0.0)

time: 59.3 us -> 58.5 us (0.987)
  the two profiles are of different devices: /device:TPU:6 before, /device:TPU:30 now
where the time goes in v3:
time: 58.5 us; the launch traced here: 58.1 us
  starting transfers between devices  26 us (44%)
  waiting for transfers between devices  17 us (29%)
  other arithmetic  9.3 us (16%)
  between operations  3.5 us (6%)
  local copies, waits for them, and re-layouts  2.27 us (4%)
    ppermute x4, starting transfers between devices, moved(): return lax.ppermute(value, 'inline', pairs)  22 us
    ppermute x4, waiting for transfers between devices, moved(): return lax.ppermute(value, 'inline', pairs)  10.6 us
    ppermute x2, waiting for transfers between devices, moved(): return lax.ppermute(value, 'xline', pairs)  6.4 us
    ppermute x2, starting transfers between devices, moved(): return lax.ppermute(value, 'xline', pairs)  3.96 us
    add x2, other arithmetic, relax_step(): return values + step_size * change  2.37 us
    mul x3, other arithmetic, attributes(): 0.25 * (neighbor(tensor, which_axis + 1, 1, up_open) + 2.0 * tensor + nei...  2.21 us
  transfers between devices with their start and end apart: 6, of which 6 were waited for; matrix products, arithmetic and copies ran while one was open for 1% of the time, Pallas kernels for 0%

profile of v3, /device:TPU:30, one launch (start us, length us, event | category | flops | bytes accessed | tf_op | source)
XLA Modules:
  0.0 58.1 jit_solution(8985208464076152118)
XLA Ops:
  0.7 0.6 %copy-done = s32[2,1]{0,1:T(1,128)S(1)} copy-done((s32[2,1]{0,1:T(1,128)S(1)}, s32[2,1]{0,1:T(1,128)}, u32[]{:S(2)}) %copy-start) | copy-done | bytes 32
  1.3 0.6 constant_dynamic-slice_fusion.2
  1.9 0.6 %iota_compare_fusion.2 = pred[4]{0:T(512)(128)(4,1)S(1)} fusion(s32[]{:T(128)} %bitcast), kind=kLoop, calls=%fused_computation.144 | loop fusion | flops 4 | bytes 8 | tf_op jit(solution)/shard_map/lt | solution.py:143
  2.5 0.9 %bitcast_convert_fusion = f32[3,4,4,1024]{3,2,1,0:T(4,128)S(1)} fusion(bf16[3,2,4,4,1024]{4,3,2,1,0:T(4,128)(2,1)} %param.4, s32[]{:T(128)S(6)} %select_n.134), kind=kLoop, calls=%fused_computation.127 | loop fusion | flops 49152 | bytes 294916 | tf_op jit(solution)/shard_map/convert_element_type | solution.py:140
  3.4 0.9 %dynamic-slice_select_fusion = f32[1,4,4,1024]{3,2,1,0:T(4,128)S(1)} fusion(f32[2,4,4,1024]{3,2,1,0:T(4,128)} %param.3, s32[]{:T(128)S(6)} %select_n.134, pred[4]{0:T(512)(128)(4,1)S(1)} %iota_compare_fusion.2), kind=kLoop, calls=%fused_computation.128 | loop fusion | flops 16384 | bytes 131080 | tf_op jit(solution)/shard_map/jit(_where)/select_n | solution.py:145
  4.5 2.7 %collective-permute-start.1 = (f32[4,4,4,1024]{3,2,1,0:T(4,128)S(1)}, f32[4,4,4,1024]{3,2,1,0:T(4,128)S(1)}, u32[]{:S(2)}, u32[]{:S(2)}) collective-permute-start(f32[4,4,4,1024]{3,2,1,0:T(4,128)S(1)} %pad_maximum_fusion.1), channel_id=1, source_target_pairs={{1,0},{2,1},{3,2},{5,4},{6,5},{7,6},{9,8},{10,9},{11,10},{13,12},{... | collective-permute-start | bytes 786440 | tf_op jit(solution)/shard_map/ppermute | solution.py:38
  7.1 1.3 %collective-permute-start = (f32[4,4,4,1024]{3,2,1,0:T(4,128)S(1)}, f32[4,4,4,1024]{3,2,1,0:T(4,128)S(1)}, u32[]{:S(2)}, u32[]{:S(2)}) collective-permute-start(f32[4,4,4,1024]{3,2,1,0:T(4,128)S(1)} %pad_maximum_fusion.1), channel_id=1, source_target_pairs={{0,1},{1,2},{2,3},{4,5},{5,6},{6,7},{8,9},{9,10},{10,11},{12,13},{... | collective-permute-start | bytes 786440 | tf_op jit(solution)/shard_map/ppermute | solution.py:38
  10.4 2.3 %collective-permute-done.1 = f32[4,4,4,1024]{3,2,1,0:T(4,128)S(1)} collective-permute-done((f32[4,4,4,1024]{3,2,1,0:T(4,128)S(1)}, f32[4,4,4,1024]{3,2,1,0:T(4,128)S(1)}, u32[]{:S(2)}, u32[]{:S(2)}) %collective-permute-start.1) | collective-permute-done | bytes 262176 | tf_op jit(solution)/shard_map/ppermute | solution.py:38
  12.7 4.1 %collective-permute-done = f32[4,4,4,1024]{3,2,1,0:T(4,128)S(1)} collective-permute-done((f32[4,4,4,1024]{3,2,1,0:T(4,128)S(1)}, f32[4,4,4,1024]{3,2,1,0:T(4,128)S(1)}, u32[]{:S(2)}, u32[]{:S(2)}) %collective-permute-start) | collective-permute-done | bytes 262176 | tf_op jit(solution)/shard_map/ppermute | solution.py:38
  16.8 0.2 pad_maximum_fusion
  17.1 3.8 %collective-permute-start.2 = (f32[4,2,12,1024]{3,2,1,0:T(8,128)S(1)}, f32[4,2,12,1024]{3,2,1,0:T(8,128)S(1)}, u32[]{:S(2)}, u32[]{:S(2)}) collective-permute-start(f32[4,2,12,1024]{3,2,1,0:T(8,128)S(1)} %get-tuple-element.13), channel_id=1, source_target_pairs={{0,4},{4,8},{8,12},{12,16},{16,20},{20,24},{24,28},{28,32},{32,36}... | collective-permute-start | bytes 1179656 | tf_op jit(solution)/shard_map/ppermute | solution.py:35
  20.9 9.8 %collective-permute-start.3 = (f32[4,2,12,1024]{3,2,1,0:T(8,128)S(1)}, f32[4,2,12,1024]{3,2,1,0:T(8,128)S(1)}, u32[]{:S(2)}, u32[]{:S(2)}) collective-permute-start(f32[4,2,12,1024]{3,2,1,0:T(8,128)S(1)} %get-tuple-element.12), channel_id=1, source_target_pairs={{4,0},{8,4},{12,8},{16,12},{20,16},{24,20},{28,24},{32,28},{36,32}... | collective-permute-start | bytes 1179656 | tf_op jit(solution)/shard_map/ppermute | solution.py:35
  31.5 8.0 %collective-permute-done.2 = f32[4,2,12,1024]{3,2,1,0:T(8,128)S(1)} collective-permute-done((f32[4,2,12,1024]{3,2,1,0:T(8,128)S(1)}, f32[4,2,12,1024]{3,2,1,0:T(8,128)S(1)}, u32[]{:S(2)}, u32[]{:S(2)}) %collective-permute-start.2) | collective-permute-done | bytes 393248 | tf_op jit(solution)/shard_map/ppermute | solution.py:35
  39.5 0.3 maximum_maximum_fusion
  39.8 0.9 %collective-permute-done.3 = f32[4,2,12,1024]{3,2,1,0:T(8,128)S(1)} collective-permute-done((f32[4,2,12,1024]{3,2,1,0:T(8,128)S(1)}, f32[4,2,12,1024]{3,2,1,0:T(8,128)S(1)}, u32[]{:S(2)}, u32[]{:S(2)}) %collective-permute-start.3) | collective-permute-done | bytes 393248 | tf_op jit(solution)/shard_map/ppermute | solution.py:35
  40.7 0.1 slice_bitcast_fusion.2
  40.9 1.2 %fusion.21 = f32[8,12,1024]{2,1,0:T(8,128)S(1)} fusion(f32[8,12,1024]{2,1,0:T(8,128)S(1)} %get-tuple-element.11, pred[12]{0:T(512)(128)(4,1)S(1)} %get-tuple-element.18, pred[12]{0:T(512)(128)(4,1)S(1)} %get-tuple-element.19, pred[8]{0:T(512)(128)(4,1)S(1)} %and_not_fusion.3, pred[8]{0:T(512)(128)(4,1)S(1)} %and_not_fusion.4, ...), kind=kLoop, calls=%fused_computation.61 | loop fusion | flops 4227072 | bytes 1968168 | tf_op jit(solution)/shard_map/add | solution.py:92
  42.1 1.2 %fusion.39 = f32[8,12,1024]{2,1,0:T(8,128)S(1)} fusion(f32[8,12,1024]{2,1,0:T(8,128)S(1)} %fusion.21, pred[12]{0:T(512)(128)(4,1)S(1)} %get-tuple-element.18, pred[12]{0:T(512)(128)(4,1)S(1)} %get-tuple-element.19, pred[8]{0:T(512)(128)(4,1)S(1)} %and_not_fusion.3, pred[8]{0:T(512)(128)(4,1)S(1)} %and_not_fusion.4, ...), kind=kLoop, calls=%fused_computation.79 | loop fusion | flops 4227072 | bytes 1968168 | tf_op jit(solution)/shard_map/add | solution.py:92
  43.3 1.9 %collective-permute-start.4 = (f32[2,8,1024]{2,1,0:T(8,128)S(1)}, f32[2,8,1024]{2,1,0:T(8,128)S(1)}, u32[]{:S(2)}, u32[]{:S(2)}) collective-permute-start(f32[2,8,1024]{2,1,0:T(8,128)S(1)} %constant_dynamic-slice_fusion), channel_id=1, source_target_pairs={{0,4},{4,8},{8,12},{12,16},{16,20},{20,24},{24,28},{28,32},{32,36}... | collective-permute-start | bytes 196616 | tf_op jit(solution)/shard_map/ppermute | solution.py:35
  45.2 6.5 %collective-permute-start.5 = (f32[2,8,1024]{2,1,0:T(8,128)S(1)}, f32[2,8,1024]{2,1,0:T(8,128)S(1)}, u32[]{:S(2)}, u32[]{:S(2)}) collective-permute-start(f32[2,8,1024]{2,1,0:T(8,128)S(1)} %slice.217), channel_id=1, source_target_pairs={{4,0},{8,4},{12,8},{16,12},{20,16},{24,20},{28,24},{32,28},{36,32}... | collective-permute-start | bytes 196616 | tf_op jit(solution)/shard_map/ppermute | solution.py:35
  51.8 0.3 collective-permute-done.4
  52.1 1.5 %collective-permute-done.5 = f32[2,8,1024]{2,1,0:T(8,128)S(1)} collective-permute-done((f32[2,8,1024]{2,1,0:T(8,128)S(1)}, f32[2,8,1024]{2,1,0:T(8,128)S(1)}, u32[]{:S(2)}, u32[]{:S(2)}) %collective-permute-start.5) | collective-permute-done | bytes 65568 | tf_op jit(solution)/shard_map/ppermute | solution.py:35
  53.8 0.4 multiply_bitcast_fusion
  54.1 0.1 bitcast_dynamic-update-slice_fusion.4
  54.3 0.2 bitcast_dynamic-update-slice_fusion.3
  54.5 0.2 bitcast_dynamic-update-slice_fusion.2
  54.8 0.1 bitcast_dynamic-update-slice_fusion
  54.9 0.5 broadcast_multiply_fusion.1
  55.5 0.8 %broadcast_multiply_fusion = (f32[6,8,8,1024]{3,2,1,0:T(8,128)S(1)}, f32[6,8,8,1024]{3,2,1,0:T(8,128)S(1)}) fusion(f32[6,8,8,1024]{3,2,1,0:T(8,128)S(1)} %get-tuple-element.4, pred[8]{0:T(512)(128)(4,1)S(1)} %get-tuple-element.20, f32[6,8,8,1024]{3,2,1,0:T(8,128)S(1)} %get-tuple-element.5, pred[8]{0:T(512)(128)(4,1)S(1)} %get-tuple-element.21), kind=kLoop, calls=%fused_computation.21 | loop fusion | flops 2359296 | bytes 6291472 | tf_op jit(solution)/shard_map/mul | solution.py:117
  56.3 0.9 %fusion.7 = f32[6,8,8,1024]{3,2,1,0:T(8,128)S(1)} fusion(f32[6,8,8,1024]{3,2,1,0:T(8,128)S(1)} %get-tuple-element.2, f32[6,8,8,1024]{3,2,1,0:T(8,128)S(1)} %get-tuple-element.3, pred[1024]{0:T(1024)(128)(4,1)S(1)} %get-tuple-element.16, pred[1024]{0:T(1024)(128)(4,1)S(1)} %get-tuple-element.17), kind=kLoop, calls=%fused_computation.14 | loop fusion | flops 2359296 | bytes 4720640 | tf_op jit(solution)/shard_map/mul | solution.py:117
  57.2 0.2 fusion.56
  57.4 0.7 %fusion.66 = (f32[1,4,4,1024]{3,2,1,0:T(4,128)}, f32[1,4,4,1024]{3,2,1,0:T(4,128)}) fusion(f32[2,4,4,1024]{3,2,1,0:T(4,128)S(1)} %fusion.61), kind=kLoop, calls=%fused_computation.146 | loop fusion | bytes 262144 | tf_op jit(solution)/shard_map/slice | solution.py:159
  (19 shorter events, 0.8 us)
Async XLA Ops:
  0.6 0.7 %copy-start = (s32[2,1]{0,1:T(1,128)S(1)}, s32[2,1]{0,1:T(1,128)}, u32[]{:S(2)}) copy-start(s32[2,1]{0,1:T(1,128)} %param.5) | copy-start | bytes 28
  4.5 8.2 %collective-permute-start.1 = (f32[4,4,4,1024]{3,2,1,0:T(4,128)S(1)}, f32[4,4,4,1024]{3,2,1,0:T(4,128)S(1)}, u32[]{:S(2)}, u32[]{:S(2)}) collective-permute-start(f32[4,4,4,1024]{3,2,1,0:T(4,128)S(1)} %pad_maximum_fusion.1), channel_id=1, source_target_pairs={{1,0},{2,1},{3,2},{5,4},{6,5},{7,6},{9,8},{10,9},{11,10},{13,12},{... | collective-permute-start | bytes 786440 | tf_op jit(solution)/shard_map/ppermute | solution.py:38
  7.1 9.7 %collective-permute-start = (f32[4,4,4,1024]{3,2,1,0:T(4,128)S(1)}, f32[4,4,4,1024]{3,2,1,0:T(4,128)S(1)}, u32[]{:S(2)}, u32[]{:S(2)}) collective-permute-start(f32[4,4,4,1024]{3,2,1,0:T(4,128)S(1)} %pad_maximum_fusion.1), channel_id=1, source_target_pairs={{0,1},{1,2},{2,3},{4,5},{5,6},{6,7},{8,9},{9,10},{10,11},{12,13},{... | collective-permute-start | bytes 786440 | tf_op jit(solution)/shard_map/ppermute | solution.py:38
  17.1 22.4 %collective-permute-start.2 = (f32[4,2,12,1024]{3,2,1,0:T(8,128)S(1)}, f32[4,2,12,1024]{3,2,1,0:T(8,128)S(1)}, u32[]{:S(2)}, u32[]{:S(2)}) collective-permute-start(f32[4,2,12,1024]{3,2,1,0:T(8,128)S(1)} %get-tuple-element.13), channel_id=1, source_target_pairs={{0,4},{4,8},{8,12},{12,16},{16,20},{20,24},{24,28},{28,32},{32,36}... | collective-permute-start | bytes 1179656 | tf_op jit(solution)/shard_map/ppermute | solution.py:35
  20.9 19.7 %collective-permute-start.3 = (f32[4,2,12,1024]{3,2,1,0:T(8,128)S(1)}, f32[4,2,12,1024]{3,2,1,0:T(8,128)S(1)}, u32[]{:S(2)}, u32[]{:S(2)}) collective-permute-start(f32[4,2,12,1024]{3,2,1,0:T(8,128)S(1)} %get-tuple-element.12), channel_id=1, source_target_pairs={{4,0},{8,4},{12,8},{16,12},{20,16},{24,20},{28,24},{32,28},{36,32}... | collective-permute-start | bytes 1179656 | tf_op jit(solution)/shard_map/ppermute | solution.py:35
  43.3 8.7 %collective-permute-start.4 = (f32[2,8,1024]{2,1,0:T(8,128)S(1)}, f32[2,8,1024]{2,1,0:T(8,128)S(1)}, u32[]{:S(2)}, u32[]{:S(2)}) collective-permute-start(f32[2,8,1024]{2,1,0:T(8,128)S(1)} %constant_dynamic-slice_fusion), channel_id=1, source_target_pairs={{0,4},{4,8},{8,12},{12,16},{16,20},{20,24},{24,28},{28,32},{32,36}... | collective-permute-start | bytes 196616 | tf_op jit(solution)/shard_map/ppermute | solution.py:35
  45.2 8.4 %collective-permute-start.5 = (f32[2,8,1024]{2,1,0:T(8,128)S(1)}, f32[2,8,1024]{2,1,0:T(8,128)S(1)}, u32[]{:S(2)}, u32[]{:S(2)}) collective-permute-start(f32[2,8,1024]{2,1,0:T(8,128)S(1)} %slice.217), channel_id=1, source_target_pairs={{4,0},{8,4},{12,8},{16,12},{20,16},{24,20},{28,24},{32,28},{36,32}... | collective-permute-start | bytes 196616 | tf_op jit(solution)/shard_map/ppermute | solution.py:35

commit v4 on v3

--- a/solution.py
+++ b/solution.py
@@ -57,8 +57,77 @@
     ra = block.ndim - 3
     from_prev = moved(lax.dynamic_slice_in_dim(block, width - depth, depth, ra), 1, 0)
     from_next = moved(lax.slice_in_dim(block, 0, depth, axis=ra), -1, 0)
+    return placed_rows(block, from_prev, from_next, width, depth)
+
+
+def placed_rows(block, from_prev, from_next, width, depth):
+    ra = block.ndim - 3
     stacked = jnp.concatenate([from_prev, block, jnp.zeros_like(from_next)], ra)
     return lax.dynamic_update_slice_in_dim(stacked, from_next, depth + width, ra)
+
+
+def packed(pieces):
+    samples = pieces[0].shape[-1]
+    return jnp.concatenate([piece.reshape(-1, samples) for piece in pieces], 0)
+
+
+def unpacked(flat, shapes):
+    out, at = [], 0
+    for shape in shapes:
+        count = 1
+        for size in shape[:-1]:
+            count *= size
+        out.append(flat[at : at + count].reshape(shape))
+        at += count
+    return out
+
+
+def diffusion_columns(fields):
+    n_f, rows, cols, samples = fields.shape
+    far = jnp.stack([fields[0], fields[2]], 0)
+    to_right = packed([fields[:, :, 1:], far[:, :, 0]])
+    to_left = packed([fields[:, :, : cols - 1], far[:, :, cols - 1]])
+    from_left = unpacked(moved(to_right, 0, 1), [(n_f, rows, cols - 1, samples), (2, rows, samples)])
+    from_right = unpacked(moved(to_left, 0, -1), [(n_f, rows, cols - 1, samples), (2, rows, samples)])
+
+    def edge(near, outer, outer_first):
+        zero = jnp.zeros_like(outer[0])
+        column = jnp.stack([outer[0], zero, outer[1], zero], 0)[:, :, None]
+        parts = [column, near] if outer_first else [near, column]
+        return jnp.concatenate(parts, 2)
+
+    left = edge(from_left[0], from_left[1], True)
+    right = edge(from_right[0], from_right[1], False)
+    return jnp.concatenate([left, fields, right], 2)
+
+
+def diffusion_rows(wide, width, cols):
+    n_f, rows, n_c, samples = wide.shape
+    h = HALO
+    near = slice(cols - 3, 2 * cols + 3)
+    mid = slice(cols - 2, 2 * cols + 2)
+
+    def pieces(row_near, row_far):
+        return packed([row_near[0:3, near], row_near[3, mid], row_far[0:2, mid]])
+
+    last = lax.dynamic_slice_in_dim(wide, width - h, h, 1)
+    to_next = pieces(last[:, 1], last[:, 0])
+    to_prev = pieces(wide[:, 0], wide[:, 1])
+    shapes = [(3, cols + 6, samples), (cols + 4, samples), (2, cols + 4, samples)]
+
+    def rebuilt(flat):
+        p_near, p_time, p_far = unpacked(flat, shapes)
+        pad_near = [(0, 0), (cols - 3, cols - 3), (0, 0)]
+        pad_mid = [(0, 0), (cols - 2, cols - 2), (0, 0)]
+        row_near = jnp.concatenate([jnp.pad(p_near, pad_near), jnp.pad(p_time[None], pad_mid)], 0)
+        row_far = jnp.pad(jnp.pad(p_far, pad_mid), [(0, 2), (0, 0), (0, 0)])
+        return row_near, row_far
+
+    prev_near, prev_far = rebuilt(moved(to_next, 1, 0))
+    next_near, next_far = rebuilt(moved(to_prev, -1, 0))
+    from_prev = jnp.stack([prev_far, prev_near], 1)
+    from_next = jnp.stack([next_near, next_far], 1)
+    return placed_rows(wide, from_prev, from_next, width, h)
 
 
 def face_masks(width, rows, cols, samples, row_halo, col_halo):
@@ -143,8 +212,8 @@
     live = (jnp.arange(rows, dtype=jnp.int32) < width)[:, None, None]
 
     values = jnp.where(live, field, 0.0)
-    wide = with_columns(jnp.concatenate([values[None], coeffs], 0), cols)
-    grown = with_rows(wide, width, h)
+    wide = diffusion_columns(jnp.concatenate([values[None], coeffs], 0))
+    grown = diffusion_rows(wide, width, cols)
     masks = face_masks(width, rows, cols, samples, h, cols)
     values, coeffs_grown = grown[0], grown[1:]
     for repeat in range(STEPS):

time: 58.5 us -> 53.8 us (0.920)
  waiting for transfers between devices: 17 us -> 10.1 us
  local copies, waits for them, and re-layouts: 2.27 us -> 3.93 us
    ppermute x4, waiting for transfers between devices: 10.6 us -> 5.37 us  [moved(): return lax.ppermute(value, 'inline', pairs)]
    ppermute x2, waiting for transfers between devices: 6.4 us -> 4.7 us  [moved(): return lax.ppermute(value, 'xline', pairs)]
    select_n x1 -> x2, other arithmetic: 0.92 us -> 1.85 us  [on_device(): values = jnp.where(live, field, 0.0)]
    convert_element_type x1, other arithmetic: 0.92 us -> 0.04 us  [on_device(): lax.dynamic_index_in_dim(conduct, batch, 1, keepdims=False)]
    dynamic_slice x1, local copies, waits for them, and re-layouts: 0.58 us -> 1.28 us  [on_device(): width = lax.dynamic_index_in_dim(widths[:, 0], batch, 0, keepdims=False)]
    concatenate x1 -> x2, local copies, waits for them, and re-layouts: 0.07 us -> 0.73 us  [the longest x1 0.66 us: diffusion_columns(): return jnp.concatenate([left, fields, right], 2)]
    unnamed x2, local copies, waits for them, and re-layouts: 0.65 us -> 0.01 us
where the time goes in v4:
time: 53.8 us; the launch traced here: 53.4 us
  starting transfers between devices  26 us (48%)
  waiting for transfers between devices  10.1 us (19%)
  other arithmetic  9.64 us (18%)
  local copies, waits for them, and re-layouts  3.93 us (7%)
  between operations  3.82 us (7%)
    ppermute x4, starting transfers between devices, moved(): return lax.ppermute(value, 'inline', pairs)  22 us
    ppermute x4, waiting for transfers between devices, moved(): return lax.ppermute(value, 'inline', pairs)  5.37 us
    ppermute x2, waiting for transfers between devices, moved(): return lax.ppermute(value, 'xline', pairs)  4.7 us
    ppermute x2, starting transfers between devices, moved(): return lax.ppermute(value, 'xline', pairs)  3.95 us
    add x2, other arithmetic, relax_step(): return values + step_size * change  2.37 us
    mul x3, other arithmetic, attributes(): 0.25 * (neighbor(tensor, which_axis + 1, 1, up_open) + 2.0 * tensor + nei...  2.21 us
    select_n x2, other arithmetic, on_device(): values = jnp.where(live, field, 0.0)  1.85 us
    dynamic_slice x1, local copies, waits for them, and re-layouts, on_device(): width = lax.dynamic_index_in_dim(widths[:, 0], batch, 0, keepdims=False)  1.28 us
  transfers between devices with their start and end apart: 6, of which 6 were waited for; matrix products, arithmetic and copies ran while one was open for 1% of the time, Pallas kernels for 0%

profile of v4, /device:TPU:30, one launch (start us, length us, event | category | flops | bytes accessed | tf_op | source)
XLA Modules:
  0.0 53.4 jit_solution(7897769526122167089)
XLA Ops:
  0.7 1.3 %constant_dynamic-slice_fusion.2 = s32[1,1]{0,1:T(1,128)} fusion(s32[2,1]{0,1:T(1,128)} %param.5, s32[]{:T(128)S(6)} %select_n.134), kind=kLoop, calls=%fused_computation.181 | loop fusion | bytes 12 | tf_op jit(solution)/shard_map/jit(dynamic_index_in_dim)/dynamic_slice | solution.py:210
  1.9 0.6 %iota_compare_fusion.4 = pred[4]{0:T(512)(128)(4,1)S(1)} fusion(s32[]{:T(128)} %bitcast), kind=kLoop, calls=%fused_computation.190 | loop fusion | flops 4 | bytes 8 | tf_op jit(solution)/shard_map/lt | solution.py:212
  2.6 0.9 %fusion.76 = f32[1,4,4,1024]{3,2,0,1:T(4,128)S(1)} fusion(f32[2,4,4,1024]{3,2,1,0:T(4,128)} %param.3, s32[]{:T(128)S(6)} %select_n.134, pred[4]{0:T(512)(128)(4,1)S(1)} %iota_compare_fusion.4), kind=kLoop, calls=%fused_computation.192 | loop fusion | flops 16384 | bytes 131080 | tf_op jit(solution)/shard_map/jit(_where)/select_n | solution.py:214
  3.5 0.9 %dynamic-slice_select_fusion = f32[1,4,4,1024]{3,2,1,0:T(4,128)S(1)} fusion(f32[2,4,4,1024]{3,2,1,0:T(4,128)} %param.3, s32[]{:T(128)S(6)} %select_n.134, pred[4]{0:T(512)(128)(4,1)S(1)} %iota_compare_fusion.4), kind=kLoop, calls=%fused_computation.163 | loop fusion | flops 16384 | bytes 131080 | tf_op jit(solution)/shard_map/jit(_where)/select_n | solution.py:214
  4.5 0.2 fusion.70
  5.0 2.7 %collective-permute-start.1 = (f32[56,1024]{1,0:T(8,128)S(1)}, f32[56,1024]{1,0:T(8,128)S(1)}, u32[]{:S(2)}, u32[]{:S(2)}) collective-permute-start(f32[56,1024]{1,0:T(8,128)S(1)} %pad_maximum_fusion.2), channel_id=1, source_target_pairs={{1,0},{2,1},{3,2},{5,4},{6,5},{7,6},{9,8},{10,9},{11,10},{13,12},{... | collective-permute-start | bytes 688136 | tf_op jit(solution)/shard_map/ppermute | solution.py:38
  7.9 1.3 %collective-permute-start = (f32[56,1024]{1,0:T(8,128)S(1)}, f32[56,1024]{1,0:T(8,128)S(1)}, u32[]{:S(2)}, u32[]{:S(2)}) collective-permute-start(f32[56,1024]{1,0:T(8,128)S(1)} %pad_maximum_fusion.1), channel_id=1, source_target_pairs={{0,1},{1,2},{2,3},{4,5},{5,6},{6,7},{8,9},{9,10},{10,11},{12,13},{... | collective-permute-start | bytes 688136 | tf_op jit(solution)/shard_map/ppermute | solution.py:38
  12.0 0.5 %collective-permute-done.1 = f32[56,1024]{1,0:T(8,128)S(1)} collective-permute-done((f32[56,1024]{1,0:T(8,128)S(1)}, f32[56,1024]{1,0:T(8,128)S(1)}, u32[]{:S(2)}, u32[]{:S(2)}) %collective-permute-start.1) | collective-permute-done | bytes 229408 | tf_op jit(solution)/shard_map/ppermute | solution.py:38
  12.7 4.2 %collective-permute-done = f32[56,1024]{1,0:T(8,128)S(1)} collective-permute-done((f32[56,1024]{1,0:T(8,128)S(1)}, f32[56,1024]{1,0:T(8,128)S(1)}, u32[]{:S(2)}, u32[]{:S(2)}) %collective-permute-start) | collective-permute-done | bytes 229408 | tf_op jit(solution)/shard_map/ppermute | solution.py:38
  17.2 0.7 %concatenate.33 = f32[4,4,12,1024]{3,2,0,1:T(8,128)S(1)} concatenate(f32[4,4,1,1024]{3,2,0,1:T(1,128)S(1)} %copy.19, f32[4,4,3,1024]{3,2,0,1:T(4,128)S(1)} %copy.20, f32[4,4,4,1024]{3,2,0,1:T(4,128)S(1)} %pad_maximum_fusion, f32[4,4,3,1024]{3,2,0,1:T(4,128)S(1)} %copy.21, f32[4,4,1,1024]{3,2,0,1:T(1,128)S(1)} %copy.22), dimensions={2} | concatenate | bytes 1572864 | tf_op jit(solution)/shard_map/concatenate | solution.py:101
  18.2 3.8 %collective-permute-start.2 = (f32[54,1024]{1,0:T(8,128)S(1)}, f32[54,1024]{1,0:T(8,128)S(1)}, u32[]{:S(2)}, u32[]{:S(2)}) collective-permute-start(f32[54,1024]{1,0:T(8,128)S(1)} %pad_maximum_fusion.3), channel_id=1, source_target_pairs={{0,4},{4,8},{8,12},{12,16},{16,20},{20,24},{24,28},{28,32},{32,36}... | collective-permute-start | bytes 663560 | tf_op jit(solution)/shard_map/ppermute | solution.py:35
  22.1 9.8 %collective-permute-start.3 = (f32[54,1024]{1,0:T(8,128)S(1)}, f32[54,1024]{1,0:T(8,128)S(1)}, u32[]{:S(2)}, u32[]{:S(2)}) collective-permute-start(f32[54,1024]{1,0:T(8,128)S(1)} %pad_maximum_fusion.4), channel_id=1, source_target_pairs={{4,0},{8,4},{12,8},{16,12},{20,16},{24,20},{28,24},{32,28},{36,32}... | collective-permute-start | bytes 663560 | tf_op jit(solution)/shard_map/ppermute | solution.py:35
  31.9 2.4 %collective-permute-done.2 = f32[54,1024]{1,0:T(8,128)S(1)} collective-permute-done((f32[54,1024]{1,0:T(8,128)S(1)}, f32[54,1024]{1,0:T(8,128)S(1)}, u32[]{:S(2)}, u32[]{:S(2)}) %collective-permute-start.2) | collective-permute-done | bytes 221216 | tf_op jit(solution)/shard_map/ppermute | solution.py:35
  34.3 1.2 %collective-permute-done.3 = f32[54,1024]{1,0:T(8,128)S(1)} collective-permute-done((f32[54,1024]{1,0:T(8,128)S(1)}, f32[54,1024]{1,0:T(8,128)S(1)}, u32[]{:S(2)}, u32[]{:S(2)}) %collective-permute-start.3) | collective-permute-done | bytes 221216 | tf_op jit(solution)/shard_map/ppermute | solution.py:35
  35.7 0.3 maximum_maximum_fusion
  36.1 0.1 slice_bitcast_fusion.2
  36.2 1.2 %fusion.21 = f32[8,12,1024]{2,1,0:T(8,128)S(1)} fusion(f32[8,12,1024]{2,1,0:T(8,128)S(1)} %get-tuple-element.11, pred[12]{0:T(512)(128)(4,1)S(1)} %get-tuple-element.36, pred[12]{0:T(512)(128)(4,1)S(1)} %get-tuple-element.37, pred[8]{0:T(512)(128)(4,1)S(1)} %get-tuple-element.38, pred[8]{0:T(512)(128)(4,1)S(1)} %get-tuple-element.39, ...), kind=kLoop, calls=%fused_computation.60 | loop fusion | flops 4227072 | bytes 1968168 | tf_op jit(solution)/shard_map/add | solution.py:161
  37.4 1.2 %fusion.39 = f32[8,12,1024]{2,1,0:T(8,128)S(1)} fusion(f32[8,12,1024]{2,1,0:T(8,128)S(1)} %fusion.21, pred[12]{0:T(512)(128)(4,1)S(1)} %get-tuple-element.36, pred[12]{0:T(512)(128)(4,1)S(1)} %get-tuple-element.37, pred[8]{0:T(512)(128)(4,1)S(1)} %get-tuple-element.38, pred[8]{0:T(512)(128)(4,1)S(1)} %get-tuple-element.39, ...), kind=kLoop, calls=%fused_computation.78 | loop fusion | flops 4227072 | bytes 1968168 | tf_op jit(solution)/shard_map/add | solution.py:161
  38.6 1.9 %collective-permute-start.4 = (f32[2,8,1024]{2,1,0:T(8,128)S(1)}, f32[2,8,1024]{2,1,0:T(8,128)S(1)}, u32[]{:S(2)}, u32[]{:S(2)}) collective-permute-start(f32[2,8,1024]{2,1,0:T(8,128)S(1)} %constant_dynamic-slice_fusion), channel_id=1, source_target_pairs={{0,4},{4,8},{8,12},{12,16},{16,20},{20,24},{24,28},{28,32},{32,36}... | collective-permute-start | bytes 196616 | tf_op jit(solution)/shard_map/ppermute | solution.py:35
  40.6 6.5 %collective-permute-start.5 = (f32[2,8,1024]{2,1,0:T(8,128)S(1)}, f32[2,8,1024]{2,1,0:T(8,128)S(1)}, u32[]{:S(2)}, u32[]{:S(2)}) collective-permute-start(f32[2,8,1024]{2,1,0:T(8,128)S(1)} %slice.371), channel_id=1, source_target_pairs={{4,0},{8,4},{12,8},{16,12},{20,16},{24,20},{28,24},{32,28},{36,32}... | collective-permute-start | bytes 196616 | tf_op jit(solution)/shard_map/ppermute | solution.py:35
  47.1 0.3 collective-permute-done.4
  47.5 1.5 %collective-permute-done.5 = f32[2,8,1024]{2,1,0:T(8,128)S(1)} collective-permute-done((f32[2,8,1024]{2,1,0:T(8,128)S(1)}, f32[2,8,1024]{2,1,0:T(8,128)S(1)}, u32[]{:S(2)}, u32[]{:S(2)}) %collective-permute-start.5) | collective-permute-done | bytes 65568 | tf_op jit(solution)/shard_map/ppermute | solution.py:35
  49.1 0.4 multiply_bitcast_fusion
  49.5 0.1 bitcast_dynamic-update-slice_fusion.4
  49.6 0.2 bitcast_dynamic-update-slice_fusion.3
  49.8 0.2 bitcast_dynamic-update-slice_fusion.2
  50.1 0.1 bitcast_dynamic-update-slice_fusion
  50.3 0.5 broadcast_multiply_fusion.1
  50.8 0.8 %broadcast_multiply_fusion = (f32[6,8,8,1024]{3,2,1,0:T(8,128)S(1)}, f32[6,8,8,1024]{3,2,1,0:T(8,128)S(1)}) fusion(f32[6,8,8,1024]{3,2,1,0:T(8,128)S(1)} %get-tuple-element.6, pred[8]{0:T(512)(128)(4,1)S(1)} %get-tuple-element.40, f32[6,8,8,1024]{3,2,1,0:T(8,128)S(1)} %get-tuple-element.7, pred[8]{0:T(512)(128)(4,1)S(1)} %get-tuple-element.41), kind=kLoop, calls=%fused_computation.20 | loop fusion | flops 2359296 | bytes 6291472 | tf_op jit(solution)/shard_map/mul | solution.py:186
  51.6 0.9 %fusion.7 = f32[6,8,8,1024]{3,2,1,0:T(8,128)S(1)} fusion(f32[6,8,8,1024]{3,2,1,0:T(8,128)S(1)} %get-tuple-element.4, f32[6,8,8,1024]{3,2,1,0:T(8,128)S(1)} %get-tuple-element.5, pred[1024]{0:T(1024)(128)(4,1)S(1)} %get-tuple-element.34, pred[1024]{0:T(1024)(128)(4,1)S(1)} %get-tuple-element.35), kind=kLoop, calls=%fused_computation.14 | loop fusion | flops 2359296 | bytes 4720640 | tf_op jit(solution)/shard_map/mul | solution.py:186
  52.5 0.2 fusion.58
  52.8 0.7 %fusion.75 = (f32[1,4,4,1024]{3,2,1,0:T(4,128)}, f32[1,4,4,1024]{3,2,1,0:T(4,128)}) fusion(f32[2,4,4,1024]{3,2,1,0:T(4,128)S(1)} %fusion.65), kind=kLoop, calls=%fused_computation.191 | loop fusion | bytes 262144 | tf_op jit(solution)/shard_map/slice | solution.py:228
  (62 shorter events, 2.1 us)
Async XLA Ops:
  0.6 3.8 %copy-start = (bf16[3,2,4,4,1024]{4,3,2,1,0:T(4,128)(2,1)S(1)}, bf16[3,2,4,4,1024]{4,3,2,1,0:T(4,128)(2,1)}, u32[]{:S(2)}) copy-start(bf16[3,2,4,4,1024]{4,3,2,1,0:T(4,128)(2,1)} %param.4) | copy-start | bytes 589828
  5.0 7.5 %collective-permute-start.1 = (f32[56,1024]{1,0:T(8,128)S(1)}, f32[56,1024]{1,0:T(8,128)S(1)}, u32[]{:S(2)}, u32[]{:S(2)}) collective-permute-start(f32[56,1024]{1,0:T(8,128)S(1)} %pad_maximum_fusion.2), channel_id=1, source_target_pairs={{1,0},{2,1},{3,2},{5,4},{6,5},{7,6},{9,8},{10,9},{11,10},{13,12},{... | collective-permute-start | bytes 688136 | tf_op jit(solution)/shard_map/ppermute | solution.py:38
  7.9 9.0 %collective-permute-start = (f32[56,1024]{1,0:T(8,128)S(1)}, f32[56,1024]{1,0:T(8,128)S(1)}, u32[]{:S(2)}, u32[]{:S(2)}) collective-permute-start(f32[56,1024]{1,0:T(8,128)S(1)} %pad_maximum_fusion.1), channel_id=1, source_target_pairs={{0,1},{1,2},{2,3},{4,5},{5,6},{6,7},{8,9},{9,10},{10,11},{12,13},{... | collective-permute-start | bytes 688136 | tf_op jit(solution)/shard_map/ppermute | solution.py:38
  18.2 16.1 %collective-permute-start.2 = (f32[54,1024]{1,0:T(8,128)S(1)}, f32[54,1024]{1,0:T(8,128)S(1)}, u32[]{:S(2)}, u32[]{:S(2)}) collective-permute-start(f32[54,1024]{1,0:T(8,128)S(1)} %pad_maximum_fusion.3), channel_id=1, source_target_pairs={{0,4},{4,8},{8,12},{12,16},{16,20},{20,24},{24,28},{28,32},{32,36}... | collective-permute-start | bytes 663560 | tf_op jit(solution)/shard_map/ppermute | solution.py:35
  22.1 13.4 %collective-permute-start.3 = (f32[54,1024]{1,0:T(8,128)S(1)}, f32[54,1024]{1,0:T(8,128)S(1)}, u32[]{:S(2)}, u32[]{:S(2)}) collective-permute-start(f32[54,1024]{1,0:T(8,128)S(1)} %pad_maximum_fusion.4), channel_id=1, source_target_pairs={{4,0},{8,4},{12,8},{16,12},{20,16},{24,20},{28,24},{32,28},{36,32}... | collective-permute-start | bytes 663560 | tf_op jit(solution)/shard_map/ppermute | solution.py:35
  38.6 8.7 %collective-permute-start.4 = (f32[2,8,1024]{2,1,0:T(8,128)S(1)}, f32[2,8,1024]{2,1,0:T(8,128)S(1)}, u32[]{:S(2)}, u32[]{:S(2)}) collective-permute-start(f32[2,8,1024]{2,1,0:T(8,128)S(1)} %constant_dynamic-slice_fusion), channel_id=1, source_target_pairs={{0,4},{4,8},{8,12},{12,16},{16,20},{20,24},{24,28},{28,32},{32,36}... | collective-permute-start | bytes 196616 | tf_op jit(solution)/shard_map/ppermute | solution.py:35
  40.6 8.4 %collective-permute-start.5 = (f32[2,8,1024]{2,1,0:T(8,128)S(1)}, f32[2,8,1024]{2,1,0:T(8,128)S(1)}, u32[]{:S(2)}, u32[]{:S(2)}) collective-permute-start(f32[2,8,1024]{2,1,0:T(8,128)S(1)} %slice.371), channel_id=1, source_target_pairs={{4,0},{8,4},{12,8},{16,12},{20,16},{24,20},{28,24},{32,28},{36,32}... | collective-permute-start | bytes 196616 | tf_op jit(solution)/shard_map/ppermute | solution.py:35

commit v5 on v4

--- a/solution.py
+++ b/solution.py
@@ -87,8 +87,21 @@
     far = jnp.stack([fields[0], fields[2]], 0)
     to_right = packed([fields[:, :, 1:], far[:, :, 0]])
     to_left = packed([fields[:, :, : cols - 1], far[:, :, cols - 1]])
-    from_left = unpacked(moved(to_right, 0, 1), [(n_f, rows, cols - 1, samples), (2, rows, samples)])
-    from_right = unpacked(moved(to_left, 0, -1), [(n_f, rows, cols - 1, samples), (2, rows, samples)])
+    position = lax.axis_index("xline")
+    count = lax.axis_size("xline")
+    chunks = jnp.stack(
+        [
+            jnp.where(j == position + 1, to_right, jnp.where(j == position - 1, to_left, 0.0))
+            for j in range(count)
+        ],
+        0,
+    )
+    arrived = lax.all_to_all(chunks, "xline", 0, 0)
+    shapes = [(n_f, rows, cols - 1, samples), (2, rows, samples)]
+    from_left = unpacked(lax.dynamic_index_in_dim(arrived, jnp.maximum(position - 1, 0), 0, False), shapes)
+    from_right = unpacked(
+        lax.dynamic_index_in_dim(arrived, jnp.minimum(position + 1, count - 1), 0, False), shapes
+    )
 
     def edge(near, outer, outer_first):
         zero = jnp.zeros_like(outer[0])

time: 53.8 us -> 61.7 us (1.15)
  the two profiles are of different devices: /device:TPU:30 before, /device:TPU:6 now
where the time goes in v5:
time: 61.7 us; the launch traced here: 61.3 us
  starting transfers between devices  26.5 us (43%)
  waiting for transfers between devices  16.3 us (26%)
  other arithmetic  10.7 us (17%)
  local copies, waits for them, and re-layouts  4.04 us (7%)
  between operations  3.84 us (6%)
    ppermute x4, starting transfers between devices, moved(): return lax.ppermute(value, 'inline', pairs)  22 us
    all_to_all x1, waiting for transfers between devices, diffusion_columns(): arrived = lax.all_to_all(chunks, 'xline', 0, 0)  10.9 us
    ppermute x4, waiting for transfers between devices, moved(): return lax.ppermute(value, 'inline', pairs)  5.36 us
    all_to_all x1, starting transfers between devices, diffusion_columns(): arrived = lax.all_to_all(chunks, 'xline', 0, 0)  4.46 us
    add x2, other arithmetic, relax_step(): return values + step_size * change  2.37 us
    mul x3, other arithmetic, attributes(): 0.25 * (neighbor(tensor, which_axis + 1, 1, up_open) + 2.0 * tensor + nei...  2.21 us
    select_n x2, other arithmetic, on_device(): values = jnp.where(live, field, 0.0)  1.85 us
    dynamic_slice x1, local copies, waits for them, and re-layouts, on_device(): width = lax.dynamic_index_in_dim(widths[:, 0], batch, 0, keepdims=False)  1.29 us
  transfers between devices with their start and end apart: 5, of which 5 were waited for; matrix products, arithmetic and copies ran while one was open for 1% of the time, Pallas kernels for 0%

profile of v5, /device:TPU:6, one launch (start us, length us, event | category | flops | bytes accessed | tf_op | source)
XLA Modules:
  0.0 61.3 jit_solution(1022841675676857472)
XLA Ops:
  0.7 1.3 %constant_dynamic-slice_fusion.8 = s32[1,1]{0,1:T(1,128)} fusion(s32[2,1]{0,1:T(1,128)} %param.5, s32[]{:T(128)S(6)} %select_n.247), kind=kLoop, calls=%fused_computation.190 | loop fusion | bytes 12 | tf_op jit(solution)/shard_map/jit(dynamic_index_in_dim)/dynamic_slice | solution.py:223
  2.0 0.6 %iota_compare_fusion.4 = pred[4]{0:T(512)(128)(4,1)S(1)} fusion(s32[]{:T(128)} %bitcast), kind=kLoop, calls=%fused_computation.199 | loop fusion | flops 4 | bytes 8 | tf_op jit(solution)/shard_map/lt | solution.py:225
  2.6 0.9 %fusion.76 = f32[1,4,4,1024]{3,2,0,1:T(4,128)S(1)} fusion(f32[2,4,4,1024]{3,2,1,0:T(4,128)} %param.3, s32[]{:T(128)S(6)} %select_n.247, pred[4]{0:T(512)(128)(4,1)S(1)} %iota_compare_fusion.4), kind=kLoop, calls=%fused_computation.201 | loop fusion | flops 16384 | bytes 131080 | tf_op jit(solution)/shard_map/jit(_where)/select_n | solution.py:227
  3.5 0.9 %dynamic-slice_select_fusion = f32[1,4,4,1024]{3,2,1,0:T(4,128)S(1)} fusion(f32[2,4,4,1024]{3,2,1,0:T(4,128)} %param.3, s32[]{:T(128)S(6)} %select_n.247, pred[4]{0:T(512)(128)(4,1)S(1)} %iota_compare_fusion.4), kind=kLoop, calls=%fused_computation.166 | loop fusion | flops 16384 | bytes 131080 | tf_op jit(solution)/shard_map/jit(_where)/select_n | solution.py:227
  4.5 0.2 fusion.70
  4.8 0.1 fusion.46
  5.4 1.0 %pad_maximum_fusion = f32[4,56,1024]{2,1,0:T(8,128)} fusion(f32[1,56,1024]{2,1,0:T(8,128)S(1)} %get-tuple-element.25, f32[1,56,1024]{2,1,0:T(8,128)S(1)} %get-tuple-element.26, f32[1,56,1024]{2,1,0:T(8,128)S(1)} %get-tuple-element.27, f32[1,56,1024]{2,1,0:T(8,128)S(1)} %get-tuple-element.24), kind=kLoop, calls=%fused_computation.20 | loop fusion | flops 688128 | bytes 1835008 | tf_op jit(solution)/shard_map/stack | solution.py:92
  6.4 4.5 %all-to-all-start = ((f32[4,56,1024]{2,1,0:T(8,128)}), f32[4,56,1024]{2,1,0:T(8,128)S(1)}, u32[]{:S(2)}, u32[]{:S(2)}) async-start(f32[4,56,1024]{2,1,0:T(8,128)} %pad_maximum_fusion), calls=%async_computation | async-start | bytes 1835008 | tf_op jit(solution)/shard_map/all_to_all | solution.py:99
  13.7 10.9 %all-to-all-done = f32[4,56,1024]{2,1,0:T(8,128)S(1)} async-done(((f32[4,56,1024]{2,1,0:T(8,128)}), f32[4,56,1024]{2,1,0:T(8,128)S(1)}, u32[]{:S(2)}, u32[]{:S(2)}) %all-to-all-start) | async-done | bytes 917536 | tf_op jit(solution)/shard_map/all_to_all | solution.py:99
  25.1 0.7 %concatenate.101 = f32[4,4,12,1024]{3,2,0,1:T(8,128)S(1)} concatenate(f32[4,4,1,1024]{3,2,0,1:T(1,128)S(1)} %copy.17, f32[4,4,3,1024]{3,2,0,1:T(4,128)S(1)} %copy.18, f32[4,4,4,1024]{3,2,0,1:T(4,128)S(1)} %pad_maximum_fusion.1, f32[4,4,3,1024]{3,2,0,1:T(4,128)S(1)} %copy.19, f32[4,4,1,1024]{3,2,0,1:T(1,128)S(1)} %copy.20), dimensions={2} | concatenate | bytes 1572864 | tf_op jit(solution)/shard_map/concatenate | solution.py:114
  26.0 3.8 %collective-permute-start = (f32[54,1024]{1,0:T(8,128)S(1)}, f32[54,1024]{1,0:T(8,128)S(1)}, u32[]{:S(2)}, u32[]{:S(2)}) collective-permute-start(f32[54,1024]{1,0:T(8,128)S(1)} %pad_maximum_fusion.2), channel_id=1, source_target_pairs={{0,4},{4,8},{8,12},{12,16},{16,20},{20,24},{24,28},{28,32},{32,36}... | collective-permute-start | bytes 663560 | tf_op jit(solution)/shard_map/ppermute | solution.py:35
  30.0 9.8 %collective-permute-start.1 = (f32[54,1024]{1,0:T(8,128)S(1)}, f32[54,1024]{1,0:T(8,128)S(1)}, u32[]{:S(2)}, u32[]{:S(2)}) collective-permute-start(f32[54,1024]{1,0:T(8,128)S(1)} %pad_maximum_fusion.3), channel_id=1, source_target_pairs={{4,0},{8,4},{12,8},{16,12},{20,16},{24,20},{28,24},{32,28},{36,32}... | collective-permute-start | bytes 663560 | tf_op jit(solution)/shard_map/ppermute | solution.py:35
  39.7 2.4 %collective-permute-done = f32[54,1024]{1,0:T(8,128)S(1)} collective-permute-done((f32[54,1024]{1,0:T(8,128)S(1)}, f32[54,1024]{1,0:T(8,128)S(1)}, u32[]{:S(2)}, u32[]{:S(2)}) %collective-permute-start) | collective-permute-done | bytes 221216 | tf_op jit(solution)/shard_map/ppermute | solution.py:35
  42.2 1.2 %collective-permute-done.1 = f32[54,1024]{1,0:T(8,128)S(1)} collective-permute-done((f32[54,1024]{1,0:T(8,128)S(1)}, f32[54,1024]{1,0:T(8,128)S(1)}, u32[]{:S(2)}, u32[]{:S(2)}) %collective-permute-start.1) | collective-permute-done | bytes 221216 | tf_op jit(solution)/shard_map/ppermute | solution.py:35
  43.6 0.3 maximum_maximum_fusion
  43.9 0.1 slice_bitcast_fusion.2
  44.1 1.2 %fusion.21 = f32[8,12,1024]{2,1,0:T(8,128)S(1)} fusion(f32[8,12,1024]{2,1,0:T(8,128)S(1)} %get-tuple-element.11, pred[12]{0:T(512)(128)(4,1)S(1)} %get-tuple-element.40, pred[12]{0:T(512)(128)(4,1)S(1)} %get-tuple-element.41, pred[8]{0:T(512)(128)(4,1)S(1)} %get-tuple-element.42, pred[8]{0:T(512)(128)(4,1)S(1)} %get-tuple-element.43, ...), kind=kLoop, calls=%fused_computation.61 | loop fusion | flops 4227072 | bytes 1968168 | tf_op jit(solution)/shard_map/add | solution.py:174
  45.3 1.2 %fusion.39 = f32[8,12,1024]{2,1,0:T(8,128)S(1)} fusion(f32[8,12,1024]{2,1,0:T(8,128)S(1)} %fusion.21, pred[12]{0:T(512)(128)(4,1)S(1)} %get-tuple-element.40, pred[12]{0:T(512)(128)(4,1)S(1)} %get-tuple-element.41, pred[8]{0:T(512)(128)(4,1)S(1)} %get-tuple-element.42, pred[8]{0:T(512)(128)(4,1)S(1)} %get-tuple-element.43, ...), kind=kLoop, calls=%fused_computation.79 | loop fusion | flops 4227072 | bytes 1968168 | tf_op jit(solution)/shard_map/add | solution.py:174
  46.5 1.9 %collective-permute-start.2 = (f32[2,8,1024]{2,1,0:T(8,128)S(1)}, f32[2,8,1024]{2,1,0:T(8,128)S(1)}, u32[]{:S(2)}, u32[]{:S(2)}) collective-permute-start(f32[2,8,1024]{2,1,0:T(8,128)S(1)} %constant_dynamic-slice_fusion.4), channel_id=1, source_target_pairs={{0,4},{4,8},{8,12},{12,16},{16,20},{20,24},{24,28},{28,32},{32,36}... | collective-permute-start | bytes 196616 | tf_op jit(solution)/shard_map/ppermute | solution.py:35
  48.5 6.5 %collective-permute-start.3 = (f32[2,8,1024]{2,1,0:T(8,128)S(1)}, f32[2,8,1024]{2,1,0:T(8,128)S(1)}, u32[]{:S(2)}, u32[]{:S(2)}) collective-permute-start(f32[2,8,1024]{2,1,0:T(8,128)S(1)} %slice.357), channel_id=1, source_target_pairs={{4,0},{8,4},{12,8},{16,12},{20,16},{24,20},{28,24},{32,28},{36,32}... | collective-permute-start | bytes 196616 | tf_op jit(solution)/shard_map/ppermute | solution.py:35
  55.0 0.3 collective-permute-done.2
  55.3 1.5 %collective-permute-done.3 = f32[2,8,1024]{2,1,0:T(8,128)S(1)} collective-permute-done((f32[2,8,1024]{2,1,0:T(8,128)S(1)}, f32[2,8,1024]{2,1,0:T(8,128)S(1)}, u32[]{:S(2)}, u32[]{:S(2)}) %collective-permute-start.3) | collective-permute-done | bytes 65568 | tf_op jit(solution)/shard_map/ppermute | solution.py:35
  57.0 0.4 multiply_bitcast_fusion
  57.4 0.1 bitcast_dynamic-update-slice_fusion.4
  57.5 0.2 bitcast_dynamic-update-slice_fusion.3
  57.7 0.2 bitcast_dynamic-update-slice_fusion.2
  58.0 0.1 bitcast_dynamic-update-slice_fusion
  58.1 0.5 broadcast_multiply_fusion.1
  58.7 0.8 %broadcast_multiply_fusion = (f32[6,8,8,1024]{3,2,1,0:T(8,128)S(1)}, f32[6,8,8,1024]{3,2,1,0:T(8,128)S(1)}) fusion(f32[6,8,8,1024]{3,2,1,0:T(8,128)S(1)} %get-tuple-element.6, pred[8]{0:T(512)(128)(4,1)S(1)} %get-tuple-element.44, f32[6,8,8,1024]{3,2,1,0:T(8,128)S(1)} %get-tuple-element.7, pred[8]{0:T(512)(128)(4,1)S(1)} %get-tuple-element.45), kind=kLoop, calls=%fused_computation.21 | loop fusion | flops 2359296 | bytes 6291472 | tf_op jit(solution)/shard_map/mul | solution.py:199
  59.5 0.9 %fusion.7 = f32[6,8,8,1024]{3,2,1,0:T(8,128)S(1)} fusion(f32[6,8,8,1024]{3,2,1,0:T(8,128)S(1)} %get-tuple-element.4, f32[6,8,8,1024]{3,2,1,0:T(8,128)S(1)} %get-tuple-element.5, pred[1024]{0:T(1024)(128)(4,1)S(1)} %get-tuple-element.38, pred[1024]{0:T(1024)(128)(4,1)S(1)} %get-tuple-element.39), kind=kLoop, calls=%fused_computation.14 | loop fusion | flops 2359296 | bytes 4720640 | tf_op jit(solution)/shard_map/mul | solution.py:199
  60.4 0.2 fusion.58
  60.6 0.7 %fusion.75 = (f32[1,4,4,1024]{3,2,1,0:T(4,128)}, f32[1,4,4,1024]{3,2,1,0:T(4,128)}) fusion(f32[2,4,4,1024]{3,2,1,0:T(4,128)S(1)} %fusion.65), kind=kLoop, calls=%fused_computation.200 | loop fusion | bytes 262144 | tf_op jit(solution)/shard_map/slice | solution.py:241
  (63 shorter events, 2.1 us)
Async XLA Ops:
  0.6 3.8 %copy-start = (bf16[3,2,4,4,1024]{4,3,2,1,0:T(4,128)(2,1)S(1)}, bf16[3,2,4,4,1024]{4,3,2,1,0:T(4,128)(2,1)}, u32[]{:S(2)}) copy-start(bf16[3,2,4,4,1024]{4,3,2,1,0:T(4,128)(2,1)} %param.4) | copy-start | bytes 589828
  6.4 18.2 %all-to-all-start = ((f32[4,56,1024]{2,1,0:T(8,128)}), f32[4,56,1024]{2,1,0:T(8,128)S(1)}, u32[]{:S(2)}, u32[]{:S(2)}) async-start(f32[4,56,1024]{2,1,0:T(8,128)} %pad_maximum_fusion), calls=%async_computation | async-start | bytes 1835008 | tf_op jit(solution)/shard_map/all_to_all | solution.py:99
  26.0 16.1 %collective-permute-start = (f32[54,1024]{1,0:T(8,128)S(1)}, f32[54,1024]{1,0:T(8,128)S(1)}, u32[]{:S(2)}, u32[]{:S(2)}) collective-permute-start(f32[54,1024]{1,0:T(8,128)S(1)} %pad_maximum_fusion.2), channel_id=1, source_target_pairs={{0,4},{4,8},{8,12},{12,16},{16,20},{20,24},{24,28},{28,32},{32,36}... | collective-permute-start | bytes 663560 | tf_op jit(solution)/shard_map/ppermute | solution.py:35
  30.0 13.4 %collective-permute-start.1 = (f32[54,1024]{1,0:T(8,128)S(1)}, f32[54,1024]{1,0:T(8,128)S(1)}, u32[]{:S(2)}, u32[]{:S(2)}) collective-permute-start(f32[54,1024]{1,0:T(8,128)S(1)} %pad_maximum_fusion.3), channel_id=1, source_target_pairs={{4,0},{8,4},{12,8},{16,12},{20,16},{24,20},{28,24},{32,28},{36,32}... | collective-permute-start | bytes 663560 | tf_op jit(solution)/shard_map/ppermute | solution.py:35
  46.5 8.7 %collective-permute-start.2 = (f32[2,8,1024]{2,1,0:T(8,128)S(1)}, f32[2,8,1024]{2,1,0:T(8,128)S(1)}, u32[]{:S(2)}, u32[]{:S(2)}) collective-permute-start(f32[2,8,1024]{2,1,0:T(8,128)S(1)} %constant_dynamic-slice_fusion.4), channel_id=1, source_target_pairs={{0,4},{4,8},{8,12},{12,16},{16,20},{20,24},{24,28},{28,32},{32,36}... | collective-permute-start | bytes 196616 | tf_op jit(solution)/shard_map/ppermute | solution.py:35
  48.5 8.4 %collective-permute-start.3 = (f32[2,8,1024]{2,1,0:T(8,128)S(1)}, f32[2,8,1024]{2,1,0:T(8,128)S(1)}, u32[]{:S(2)}, u32[]{:S(2)}) collective-permute-start(f32[2,8,1024]{2,1,0:T(8,128)S(1)} %slice.357), channel_id=1, source_target_pairs={{4,0},{8,4},{12,8},{16,12},{20,16},{24,20},{28,24},{32,28},{36,32}... | collective-permute-start | bytes 196616 | tf_op jit(solution)/shard_map/ppermute | solution.py:35

commit v6 on v4

--- a/solution.py
+++ b/solution.py
@@ -178,16 +178,17 @@
             - 2.0 * grown
         )
     combos = [(0, 0), (1, 1), (2, 2), (0, 1), (0, 2), (1, 2)]
-    tensor = jnp.stack(
-        [grads[first_index] * grads[second_index] for first_index, second_index in combos], 0
-    )
-    for which_axis in range(3):
-        up_open, down_open = masks[which_axis]
-        tensor = 0.25 * (
-            neighbor(tensor, which_axis + 1, 1, up_open)
-            + 2.0 * tensor
-            + neighbor(tensor, which_axis + 1, -1, down_open)
-        )
+    tensor = []
+    for first_index, second_index in combos:
+        member = grads[first_index] * grads[second_index]
+        for which_axis in range(3):
+            up_open, down_open = masks[which_axis]
+            member = 0.25 * (
+                neighbor(member, which_axis, 1, up_open)
+                + 2.0 * member
+                + neighbor(member, which_axis, -1, down_open)
+            )
+        tensor.append(member)
     trace = tensor[0] + tensor[1] + tensor[2]
     minors = (
         tensor[0] * tensor[1]
@@ -211,8 +212,7 @@
     rows, cols, samples = field.shape
     live = (jnp.arange(rows, dtype=jnp.int32) < width)[:, None, None]
 
-    values = jnp.where(live, field, 0.0)
-    wide = diffusion_columns(jnp.concatenate([values[None], coeffs], 0))
+    wide = diffusion_columns(jnp.concatenate([field[None], coeffs], 0))
     grown = diffusion_rows(wide, width, cols)
     masks = face_masks(width, rows, cols, samples, h, cols)
     values, coeffs_grown = grown[0], grown[1:]
@@ -222,10 +222,8 @@
 
     grown = with_rows(smooth, width, h)
     masks = face_masks(width, rows, cols, samples, h, h)
-    coherence, curvature = attributes(grown, masks)
-    outcome = jnp.stack([coherence, curvature], 0)[:, h : h + rows, h : h + cols]
-    outcome = jnp.where(live[None], outcome, 0.0)
-    return (outcome[0][None], outcome[1][None])
+    results = attributes(grown, masks)
+    return tuple(jnp.where(live, value[h : h + rows, h : h + cols], 0.0)[None] for value in results)
 
 
 def solution(mesh):

time: 53.8 us -> 51.9 us (0.965)
  other arithmetic: 9.64 us -> 7.84 us
    select_n x3 -> x0, other arithmetic: 1.94 us -> none  [the longest x2 1.85 us: on_device(): values = jnp.where(live, field, 0.0)]
    dynamic_slice x0 -> x2, local copies, waits for them, and re-layouts: none -> 1.73 us  [on_device(): field = lax.dynamic_index_in_dim(survey, batch, 0, keepdims=False)]
    broadcast_in_dim x0 -> x1, other arithmetic: none -> 0.92 us  [on_device(): jnp.where(live, value[h:h + rows, h:h + cols], 0.0)[None]]
    unnamed x5 -> x0, other arithmetic: 0.73 us -> none
    dynamic_slice x1, local copies, waits for them, and re-layouts: 1.28 us -> 0.59 us  [on_device(): width = lax.dynamic_index_in_dim(widths[:, 0], batch, 0, keepdims=False)]
    slice x1 -> x0, local copies, waits for them, and re-layouts: 0.66 us -> none  [on_device(): return (outcome[0][None], outcome[1][None])]
    add x0 -> x1, other arithmetic: none -> 0.66 us  [attributes(): tensor[0] * tensor[1] - tensor[3] * tensor[3] + tensor[0] * tensor[2]]
    mul x3 -> x8, other arithmetic: 2.21 us -> 2.18 us  [the longest x4 1.37 us: attributes(): 0.25 * (neighbor(member, which_axis, 1, up_open) + 2.0 * member + neighbo...]
  transfers between devices with their start and end apart: 6 -> 6, of which waited for: 6 -> 4; matrix products, arithmetic and copies ran while one was open for 1% -> 3% of each run, Pallas kernels for 0% -> 0%
where the time goes in v6:
time: 51.9 us; the launch traced here: 51.6 us
  starting transfers between devices  26 us (50%)
  waiting for transfers between devices  9.61 us (19%)
  other arithmetic  7.84 us (15%)
  local copies, waits for them, and re-layouts  4.33 us (8%)
  between operations  3.82 us (7%)
    ppermute x4, starting transfers between devices, moved(): return lax.ppermute(value, 'inline', pairs)  22 us
    ppermute x4, waiting for transfers between devices, moved(): return lax.ppermute(value, 'inline', pairs)  5.36 us
    ppermute x2, waiting for transfers between devices, moved(): return lax.ppermute(value, 'xline', pairs)  4.25 us
    ppermute x2, starting transfers between devices, moved(): return lax.ppermute(value, 'xline', pairs)  3.95 us
    add x2, other arithmetic, relax_step(): return values + step_size * change  2.36 us
    dynamic_slice x2, local copies, waits for them, and re-layouts, on_device(): field = lax.dynamic_index_in_dim(survey, batch, 0, keepdims=False)  1.73 us
    mul x4, other arithmetic, attributes(): 0.25 * (neighbor(member, which_axis, 1, up_open) + 2.0 * member + neighbo...  1.37 us
  transfers between devices with their start and end apart: 6, of which 4 were waited for; matrix products, arithmetic and copies ran while one was open for 3% of the time, Pallas kernels for 0%

profile of v6, /device:TPU:30, one launch (start us, length us, event | category | flops | bytes accessed | tf_op | source)
XLA Modules:
  0.0 51.6 jit_solution(11682934853033000508)
XLA Ops:
  0.7 0.9 %constant_dynamic-slice_fusion.2 = f32[1,4,4,1024]{3,2,1,0:T(4,128)S(1)} fusion(f32[2,4,4,1024]{3,2,1,0:T(4,128)} %param.3, s32[]{:T(128)S(6)} %select_n.219), kind=kLoop, calls=%fused_computation.292 | loop fusion | bytes 131076 | tf_op jit(solution)/shard_map/jit(dynamic_index_in_dim)/dynamic_slice | solution.py:209
  1.5 0.8 %fusion.171 = f32[1,4,4,1024]{3,2,0,1:T(4,128)S(1)} fusion(f32[2,4,4,1024]{3,2,1,0:T(4,128)} %param.3, s32[]{:T(128)S(6)} %select_n.219), kind=kLoop, calls=%fused_computation.308 | loop fusion | bytes 131076 | tf_op jit(solution)/shard_map/jit(dynamic_index_in_dim)/dynamic_slice | solution.py:209
  2.4 0.2 fusion.144
  2.7 0.1 fusion.33
  2.8 0.1 reshape.100
  3.0 2.7 %collective-permute-start.1 = (f32[56,1024]{1,0:T(8,128)S(1)}, f32[56,1024]{1,0:T(8,128)S(1)}, u32[]{:S(2)}, u32[]{:S(2)}) collective-permute-start(f32[56,1024]{1,0:T(8,128)S(1)} %pad_maximum_fusion.2), channel_id=1, source_target_pairs={{1,0},{2,1},{3,2},{5,4},{6,5},{7,6},{9,8},{10,9},{11,10},{13,12},{... | collective-permute-start | bytes 688136 | tf_op jit(solution)/shard_map/ppermute | solution.py:38
  5.7 0.1 reshape.98
  5.8 1.3 %collective-permute-start = (f32[56,1024]{1,0:T(8,128)S(1)}, f32[56,1024]{1,0:T(8,128)S(1)}, u32[]{:S(2)}, u32[]{:S(2)}) collective-permute-start(f32[56,1024]{1,0:T(8,128)S(1)} %pad_maximum_fusion.1), channel_id=1, source_target_pairs={{0,1},{1,2},{2,3},{4,5},{5,6},{6,7},{8,9},{9,10},{10,11},{12,13},{... | collective-permute-start | bytes 688136 | tf_op jit(solution)/shard_map/ppermute | solution.py:38
  7.3 0.6 %constant_dynamic-slice_fusion.3 = s32[1,1]{0,1:T(1,128)} fusion(s32[2,1]{0,1:T(1,128)S(1)} %copy-done.1, s32[]{:T(128)S(6)} %select_n.219), kind=kLoop, calls=%fused_computation.293 | loop fusion | bytes 12 | tf_op jit(solution)/shard_map/jit(dynamic_index_in_dim)/dynamic_slice | solution.py:211
  10.6 4.2 %collective-permute-done = f32[56,1024]{1,0:T(8,128)S(1)} collective-permute-done((f32[56,1024]{1,0:T(8,128)S(1)}, f32[56,1024]{1,0:T(8,128)S(1)}, u32[]{:S(2)}, u32[]{:S(2)}) %collective-permute-start) | collective-permute-done | bytes 229408 | tf_op jit(solution)/shard_map/ppermute | solution.py:38
  15.3 0.7 %concatenate.33 = f32[4,4,12,1024]{3,2,0,1:T(8,128)S(1)} concatenate(f32[4,4,1,1024]{3,2,0,1:T(1,128)S(1)} %copy.19, f32[4,4,3,1024]{3,2,0,1:T(4,128)S(1)} %copy.20, f32[4,4,4,1024]{3,2,0,1:T(4,128)S(1)} %pad_maximum_fusion, f32[4,4,3,1024]{3,2,0,1:T(4,128)S(1)} %copy.21, f32[4,4,1,1024]{3,2,0,1:T(1,128)S(1)} %copy.22), dimensions={2} | concatenate | bytes 1572864 | tf_op jit(solution)/shard_map/concatenate | solution.py:101
  16.3 3.8 %collective-permute-start.2 = (f32[54,1024]{1,0:T(8,128)S(1)}, f32[54,1024]{1,0:T(8,128)S(1)}, u32[]{:S(2)}, u32[]{:S(2)}) collective-permute-start(f32[54,1024]{1,0:T(8,128)S(1)} %pad_maximum_fusion.3), channel_id=1, source_target_pairs={{0,4},{4,8},{8,12},{12,16},{16,20},{20,24},{24,28},{28,32},{32,36}... | collective-permute-start | bytes 663560 | tf_op jit(solution)/shard_map/ppermute | solution.py:35
  20.2 9.8 %collective-permute-start.3 = (f32[54,1024]{1,0:T(8,128)S(1)}, f32[54,1024]{1,0:T(8,128)S(1)}, u32[]{:S(2)}, u32[]{:S(2)}) collective-permute-start(f32[54,1024]{1,0:T(8,128)S(1)} %pad_maximum_fusion.4), channel_id=1, source_target_pairs={{4,0},{8,4},{12,8},{16,12},{20,16},{24,20},{28,24},{32,28},{36,32}... | collective-permute-start | bytes 663560 | tf_op jit(solution)/shard_map/ppermute | solution.py:35
  30.0 2.4 %collective-permute-done.2 = f32[54,1024]{1,0:T(8,128)S(1)} collective-permute-done((f32[54,1024]{1,0:T(8,128)S(1)}, f32[54,1024]{1,0:T(8,128)S(1)}, u32[]{:S(2)}, u32[]{:S(2)}) %collective-permute-start.2) | collective-permute-done | bytes 221216 | tf_op jit(solution)/shard_map/ppermute | solution.py:35
  32.4 1.2 %collective-permute-done.3 = f32[54,1024]{1,0:T(8,128)S(1)} collective-permute-done((f32[54,1024]{1,0:T(8,128)S(1)}, f32[54,1024]{1,0:T(8,128)S(1)}, u32[]{:S(2)}, u32[]{:S(2)}) %collective-permute-start.3) | collective-permute-done | bytes 221216 | tf_op jit(solution)/shard_map/ppermute | solution.py:35
  33.7 0.3 maximum_maximum_fusion
  34.2 0.1 slice_bitcast_fusion.2
  34.3 1.2 %fusion.8 = f32[8,12,1024]{2,1,0:T(8,128)S(1)} fusion(f32[8,12,1024]{2,1,0:T(8,128)S(1)} %get-tuple-element.40, pred[12]{0:T(512)(128)(4,1)S(1)} %get-tuple-element.87, pred[12]{0:T(512)(128)(4,1)S(1)} %get-tuple-element.88, pred[8]{0:T(512)(128)(4,1)S(1)} %get-tuple-element.89, pred[8]{0:T(512)(128)(4,1)S(1)} %get-tuple-element.90, ...), kind=kLoop, calls=%fused_computation.39 | loop fusion | flops 4227072 | bytes 1968168 | tf_op jit(solution)/shard_map/add | solution.py:161
  35.5 1.2 %fusion.26 = f32[8,12,1024]{2,1,0:T(8,128)S(1)} fusion(f32[8,12,1024]{2,1,0:T(8,128)S(1)} %fusion.8, pred[12]{0:T(512)(128)(4,1)S(1)} %get-tuple-element.87, pred[12]{0:T(512)(128)(4,1)S(1)} %get-tuple-element.88, pred[8]{0:T(512)(128)(4,1)S(1)} %get-tuple-element.89, pred[8]{0:T(512)(128)(4,1)S(1)} %get-tuple-element.90, ...), kind=kLoop, calls=%fused_computation.57 | loop fusion | flops 4227072 | bytes 1968168 | tf_op jit(solution)/shard_map/add | solution.py:161
  36.7 1.9 %collective-permute-start.4 = (f32[2,8,1024]{2,1,0:T(8,128)S(1)}, f32[2,8,1024]{2,1,0:T(8,128)S(1)}, u32[]{:S(2)}, u32[]{:S(2)}) collective-permute-start(f32[2,8,1024]{2,1,0:T(8,128)S(1)} %constant_dynamic-slice_fusion), channel_id=1, source_target_pairs={{0,4},{4,8},{8,12},{12,16},{16,20},{20,24},{24,28},{28,32},{32,36}... | collective-permute-start | bytes 196616 | tf_op jit(solution)/shard_map/ppermute | solution.py:35
  38.7 0.7 %iota_compare_fusion.4 = pred[4]{0:T(512)(128)(4,1)S(1)} fusion(s32[]{:T(128)} %bitcast), kind=kLoop, calls=%fused_computation.302 | loop fusion | flops 4 | bytes 8 | tf_op jit(solution)/shard_map/lt | solution.py:213
  39.3 6.5 %collective-permute-start.5 = (f32[2,8,1024]{2,1,0:T(8,128)S(1)}, f32[2,8,1024]{2,1,0:T(8,128)S(1)}, u32[]{:S(2)}, u32[]{:S(2)}) collective-permute-start(f32[2,8,1024]{2,1,0:T(8,128)S(1)} %slice.454), channel_id=1, source_target_pairs={{4,0},{8,4},{12,8},{16,12},{20,16},{24,20},{28,24},{32,28},{36,32}... | collective-permute-start | bytes 196616 | tf_op jit(solution)/shard_map/ppermute | solution.py:35
  46.0 1.8 %collective-permute-done.5 = f32[2,8,1024]{2,1,0:T(8,128)S(1)} collective-permute-done((f32[2,8,1024]{2,1,0:T(8,128)S(1)}, f32[2,8,1024]{2,1,0:T(8,128)S(1)}, u32[]{:S(2)}, u32[]{:S(2)}) %collective-permute-start.5) | collective-permute-done | bytes 65568 | tf_op jit(solution)/shard_map/ppermute | solution.py:35
  47.7 0.2 fusion.147
  47.9 0.2 fusion.146
  48.1 0.2 broadcast_multiply_fusion.11
  48.4 0.5 broadcast_multiply_fusion.3
  48.9 0.3 broadcast_multiply_fusion
  49.2 0.4 broadcast_multiply_fusion.2
  49.6 0.3 fusion.87
  50.0 0.7 %fusion.64 = (f32[8,8,1024]{2,1,0:T(8,128)S(1)}, f32[8,8,1024]{2,1,0:T(8,128)S(1)}, f32[8,8,1024]{2,1,0:T(8,128)S(1)}, f32[8,8,1024]{2,1,0:T(8,128)S(1)}) fusion(f32[8,8,1024]{2,1,0:T(8,128)S(1)} %get-tuple-element.65, f32[8,8,1024]{2,1,0:T(8,128)S(1)} %get-tuple-element.66, pred[1024]{0:T(1024)(128)(4,1)S(1)} %get-tuple-element.85, ...), kind=kLoop, calls=%fused_computation.147 | loop fusion | flops 1900544 | bytes 3147776 | tf_op jit(solution)/shard_map/add | solution.py:194
  50.6 0.9 %fusion.132 = (f32[1,4,4,1024]{3,2,1,0:T(4,128)}, f32[1,4,4,1024]{3,2,1,0:T(4,128)}) fusion(f32[8,8,1024]{2,1,0:T(8,128)S(1)} %get-tuple-element.48, f32[8,8,1024]{2,1,0:T(8,128)S(1)} %get-tuple-element.50, f32[8,8,1024]{2,1,0:T(8,128)S(1)} %get-tuple-element.13, f32[8,8,1024]{2,1,0:T(8,128)S(1)} %get-tuple-element.14, ...), kind=kLoop, calls=%fused_computation.250 | loop fusion | flops 393216 | bytes 983044 | tf_op jit(solution)/shard_map/broadcast_in_dim | solution.py:226
  (61 shorter events, 1.6 us)
Async XLA Ops:
  0.6 1.8 %copy-start = (bf16[3,2,4,4,1024]{4,3,2,1,0:T(4,128)(2,1)S(1)}, bf16[3,2,4,4,1024]{4,3,2,1,0:T(4,128)(2,1)}, u32[]{:S(2)}) copy-start(bf16[3,2,4,4,1024]{4,3,2,1,0:T(4,128)(2,1)} %param.4) | copy-start | bytes 589828
  2.6 4.6 %copy-start.1 = (s32[2,1]{0,1:T(1,128)S(1)}, s32[2,1]{0,1:T(1,128)}, u32[]{:S(2)}) copy-start(s32[2,1]{0,1:T(1,128)} %param.5) | copy-start | bytes 28
  3.0 7.6 %collective-permute-start.1 = (f32[56,1024]{1,0:T(8,128)S(1)}, f32[56,1024]{1,0:T(8,128)S(1)}, u32[]{:S(2)}, u32[]{:S(2)}) collective-permute-start(f32[56,1024]{1,0:T(8,128)S(1)} %pad_maximum_fusion.2), channel_id=1, source_target_pairs={{1,0},{2,1},{3,2},{5,4},{6,5},{7,6},{9,8},{10,9},{11,10},{13,12},{... | collective-permute-start | bytes 688136 | tf_op jit(solution)/shard_map/ppermute | solution.py:38
  5.8 9.0 %collective-permute-start = (f32[56,1024]{1,0:T(8,128)S(1)}, f32[56,1024]{1,0:T(8,128)S(1)}, u32[]{:S(2)}, u32[]{:S(2)}) collective-permute-start(f32[56,1024]{1,0:T(8,128)S(1)} %pad_maximum_fusion.1), channel_id=1, source_target_pairs={{0,1},{1,2},{2,3},{4,5},{5,6},{6,7},{8,9},{9,10},{10,11},{12,13},{... | collective-permute-start | bytes 688136 | tf_op jit(solution)/shard_map/ppermute | solution.py:38
  16.3 16.1 %collective-permute-start.2 = (f32[54,1024]{1,0:T(8,128)S(1)}, f32[54,1024]{1,0:T(8,128)S(1)}, u32[]{:S(2)}, u32[]{:S(2)}) collective-permute-start(f32[54,1024]{1,0:T(8,128)S(1)} %pad_maximum_fusion.3), channel_id=1, source_target_pairs={{0,4},{4,8},{8,12},{12,16},{16,20},{20,24},{24,28},{28,32},{32,36}... | collective-permute-start | bytes 663560 | tf_op jit(solution)/shard_map/ppermute | solution.py:35
  20.2 13.4 %collective-permute-start.3 = (f32[54,1024]{1,0:T(8,128)S(1)}, f32[54,1024]{1,0:T(8,128)S(1)}, u32[]{:S(2)}, u32[]{:S(2)}) collective-permute-start(f32[54,1024]{1,0:T(8,128)S(1)} %pad_maximum_fusion.4), channel_id=1, source_target_pairs={{4,0},{8,4},{12,8},{16,12},{20,16},{24,20},{28,24},{32,28},{36,32}... | collective-permute-start | bytes 663560 | tf_op jit(solution)/shard_map/ppermute | solution.py:35
  36.7 9.1 %collective-permute-start.4 = (f32[2,8,1024]{2,1,0:T(8,128)S(1)}, f32[2,8,1024]{2,1,0:T(8,128)S(1)}, u32[]{:S(2)}, u32[]{:S(2)}) collective-permute-start(f32[2,8,1024]{2,1,0:T(8,128)S(1)} %constant_dynamic-slice_fusion), channel_id=1, source_target_pairs={{0,4},{4,8},{8,12},{12,16},{16,20},{20,24},{24,28},{28,32},{32,36}... | collective-permute-start | bytes 196616 | tf_op jit(solution)/shard_map/ppermute | solution.py:35
  39.3 8.4 %collective-permute-start.5 = (f32[2,8,1024]{2,1,0:T(8,128)S(1)}, f32[2,8,1024]{2,1,0:T(8,128)S(1)}, u32[]{:S(2)}, u32[]{:S(2)}) collective-permute-start(f32[2,8,1024]{2,1,0:T(8,128)S(1)} %slice.454), channel_id=1, source_target_pairs={{4,0},{8,4},{12,8},{16,12},{20,16},{24,20},{28,24},{32,28},{36,32}... | collective-permute-start | bytes 196616 | tf_op jit(solution)/shard_map/ppermute | solution.py:35

commit v7 on v6

--- a/solution.py
+++ b/solution.py
@@ -1,6 +1,8 @@
 import jax
 import jax.numpy as jnp
 from jax import lax
+from jax.experimental import pallas as pl
+from jax.experimental.pallas import tpu as pltpu
 from jax.sharding import PartitionSpec as P
 
 STEPS = 2
@@ -203,6 +205,110 @@
     return coherence, curvature
 
 
+def attributes_kernel(flags_ref, grown_ref, coherence_ref, curvature_ref):
+    h = HALO
+    width = flags_ref[0]
+    first_row, last_row = flags_ref[1] != 0, flags_ref[2] != 0
+    first_col, last_col = flags_ref[3] != 0, flags_ref[4] != 0
+    grown = grown_ref[...]
+    n_rows, n_cols, samples = grown.shape
+    cols = n_cols - 2 * h
+
+    def masks_for(lo, hi):
+        shape = (hi - lo, n_cols, samples)
+        row = lax.broadcasted_iota(jnp.int32, shape, 0) + (lo - h)
+        col = lax.broadcasted_iota(jnp.int32, shape, 1) - h
+        sample = lax.broadcasted_iota(jnp.int32, shape, 2)
+        return [
+            (jnp.logical_not(last_row & (row == width - 1)), jnp.logical_not(first_row & (row == 0))),
+            (jnp.logical_not(last_col & (col == cols - 1)), jnp.logical_not(first_col & (col == 0))),
+            (sample < samples - 1, sample > 0),
+        ]
+
+    def near(source, lo, hi, at, which_axis, offset, opened):
+        centre = source[lo - at : hi - at]
+        if which_axis == 0:
+            moved_rows = source[lo - at + offset : hi - at + offset]
+        else:
+            length = source.shape[which_axis]
+            moved_rows = pltpu.roll(centre, (-offset) % length, which_axis)
+        return jnp.where(opened, moved_rows, centre)
+
+    lo, hi = 1, n_rows - 1
+    masks = masks_for(lo, hi)
+    grads = []
+    for which_axis in range(3):
+        up_open, down_open = masks[which_axis]
+        grads.append(
+            0.5
+            * (
+                near(grown, lo, hi, 0, which_axis, 1, up_open)
+                - near(grown, lo, hi, 0, which_axis, -1, down_open)
+            )
+        )
+    inner_lo, inner_hi = h, n_rows - h
+    inner = masks_for(inner_lo, inner_hi)
+    centre = grown[inner_lo:inner_hi]
+    seconds = []
+    for which_axis in range(2):
+        up_open, down_open = inner[which_axis]
+        seconds.append(
+            near(grown, inner_lo, inner_hi, 0, which_axis, 1, up_open)
+            + near(grown, inner_lo, inner_hi, 0, which_axis, -1, down_open)
+            - 2.0 * centre
+        )
+    combos = [(0, 0), (1, 1), (2, 2), (0, 1), (0, 2), (1, 2)]
+    tensor = []
+    for first_index, second_index in combos:
+        member = grads[first_index] * grads[second_index]
+        up_open, down_open = inner[0]
+        member = 0.25 * (
+            near(member, inner_lo, inner_hi, lo, 0, 1, up_open)
+            + 2.0 * member[inner_lo - lo : inner_hi - lo]
+            + near(member, inner_lo, inner_hi, lo, 0, -1, down_open)
+        )
+        for which_axis in (1, 2):
+            up_open, down_open = inner[which_axis]
+            member = 0.25 * (
+                near(member, inner_lo, inner_hi, inner_lo, which_axis, 1, up_open)
+                + 2.0 * member
+                + near(member, inner_lo, inner_hi, inner_lo, which_axis, -1, down_open)
+            )
+        tensor.append(member)
+    trace = tensor[0] + tensor[1] + tensor[2]
+    minors = (
+        tensor[0] * tensor[1]
+        - tensor[3] * tensor[3]
+        + tensor[0] * tensor[2]
+        - tensor[4] * tensor[4]
+        + tensor[1] * tensor[2]
+        - tensor[5] * tensor[5]
+    )
+    coherence = 1.0 - 3.0 * minors / (trace * trace + epsilon)
+    g_in = grads[0][inner_lo - lo : inner_hi - lo]
+    g_x = grads[1][inner_lo - lo : inner_hi - lo]
+    curvature = (seconds[0] + seconds[1]) / (1.0 + g_in * g_in + g_x * g_x) ** 1.5
+    out_shape = coherence_ref.shape
+    live = lax.broadcasted_iota(jnp.int32, out_shape, 0) < width
+    for value, out_ref in ((coherence, coherence_ref), (curvature, curvature_ref)):
+        value = pltpu.roll(value, n_cols - h, 1)[:, :cols]
+        out_ref[...] = jnp.where(live, value, 0.0)
+
+
+def attributes_call(grown, flags, rows, cols):
+    samples = grown.shape[-1]
+    out = jax.ShapeDtypeStruct((rows, cols, samples), jnp.float32)
+    return pl.pallas_call(
+        attributes_kernel,
+        out_shape=(out, out),
+        in_specs=[
+            pl.BlockSpec(memory_space=pltpu.SMEM),
+            pl.BlockSpec(memory_space=pltpu.VMEM),
+        ],
+        out_specs=(pl.BlockSpec(memory_space=pltpu.VMEM), pl.BlockSpec(memory_space=pltpu.VMEM)),
+    )(flags, grown)
+
+
 def on_device(survey, conduct, widths):
     h = HALO
     batch = lax.axis_index("segment")
@@ -222,8 +328,17 @@
 
     grown = with_rows(smooth, width, h)
     masks = face_masks(width, rows, cols, samples, h, h)
-    results = attributes(grown, masks)
-    return tuple(jnp.where(live, value[h : h + rows, h : h + cols], 0.0)[None] for value in results)
+    flags = jnp.stack(
+        [
+            width,
+            (lax.axis_index("inline") == 0).astype(jnp.int32),
+            (lax.axis_index("inline") == lax.axis_size("inline") - 1).astype(jnp.int32),
+            (lax.axis_index("xline") == 0).astype(jnp.int32),
+            (lax.axis_index("xline") == lax.axis_size("xline") - 1).astype(jnp.int32),
+        ]
+    )
+    results = attributes_call(grown, flags, rows, cols)
+    return tuple(value[None] for value in results)
 
 
 def solution(mesh):

time: 51.9 us -> 57.3 us (1.10)
  the two profiles are of different devices: /device:TPU:30 before, /device:TPU:6 now
where the time goes in v7:
time: 57.3 us; the launch traced here: 56.9 us
  starting transfers between devices  26.3 us (46%)
  waiting for transfers between devices  13.4 us (23%)
  local copies, waits for them, and re-layouts  6.02 us (11%)
  between operations  4.45 us (8%)
  other arithmetic  4.07 us (7%)
  Pallas kernels  2.65 us (5%)
    ppermute x4, starting transfers between devices, moved(): return lax.ppermute(value, 'inline', pairs)  21.5 us
    ppermute x4, waiting for transfers between devices, moved(): return lax.ppermute(value, 'inline', pairs)  9.81 us
    ppermute x2, starting transfers between devices, moved(): return lax.ppermute(value, 'xline', pairs)  4.79 us
    ppermute x2, waiting for transfers between devices, moved(): return lax.ppermute(value, 'xline', pairs)  3.57 us
    pallas_call x1, Pallas kernels, attributes_call(): pl.pallas_call(attributes_kernel, out_shape=(out, out), in_specs=[pl.Bloc...  2.65 us
    add x2, other arithmetic, relax_step(): return values + step_size * change  2.37 us
    dynamic_slice x2, local copies, waits for them, and re-layouts, on_device(): field = lax.dynamic_index_in_dim(survey, batch, 0, keepdims=False)  1.73 us
    another operation x1, local copies, waits for them, and re-layouts, on_device(): jnp.stack([width, (lax.axis_index('inline') == 0).astype(jnp.int32), (lax...  1.28 us
  transfers between devices with their start and end apart: 6, of which 4 were waited for; matrix products, arithmetic and copies ran while one was open for 4% of the time, Pallas kernels for 0%

profile of v7, /device:TPU:6, one launch (start us, length us, event | category | flops | bytes accessed | tf_op | source)
XLA Modules:
  0.0 56.9 jit_solution(8674566760259549849)
XLA Ops:
  0.7 0.9 %fusion.42 = f32[1,4,4,1024]{3,2,0,1:T(4,128)S(1)} fusion(f32[2,4,4,1024]{3,2,1,0:T(4,128)} %param.3, s32[]{:T(128)S(6)} %select_n.79), kind=kLoop, calls=%fused_computation.129 | loop fusion | bytes 131076 | tf_op jit(solution)/shard_map/jit(dynamic_index_in_dim)/dynamic_slice | solution.py:315
  1.5 0.8 %constant_dynamic-slice_fusion.2 = f32[1,4,4,1024]{3,2,1,0:T(4,128)S(1)} fusion(f32[2,4,4,1024]{3,2,1,0:T(4,128)} %param.3, s32[]{:T(128)S(6)} %select_n.79), kind=kLoop, calls=%fused_computation.120 | loop fusion | bytes 131076 | tf_op jit(solution)/shard_map/jit(dynamic_index_in_dim)/dynamic_slice | solution.py:315
  2.4 0.1 fusion.33
  2.6 0.1 reshape.90
  2.7 0.2 fusion.39
  3.0 3.5 %collective-permute-start = (f32[56,1024]{1,0:T(8,128)S(1)}, f32[56,1024]{1,0:T(8,128)S(1)}, u32[]{:S(2)}, u32[]{:S(2)}) collective-permute-start(f32[56,1024]{1,0:T(8,128)S(1)} %pad_maximum_fusion.1), channel_id=1, source_target_pairs={{0,1},{1,2},{2,3},{4,5},{5,6},{6,7},{8,9},{9,10},{10,11},{12,13},{... | collective-permute-start | bytes 688136 | tf_op jit(solution)/shard_map/ppermute | solution.py:40
  6.5 0.1 reshape.92
  6.7 1.3 %collective-permute-start.1 = (f32[56,1024]{1,0:T(8,128)S(1)}, f32[56,1024]{1,0:T(8,128)S(1)}, u32[]{:S(2)}, u32[]{:S(2)}) collective-permute-start(f32[56,1024]{1,0:T(8,128)S(1)} %pad_maximum_fusion.2), channel_id=1, source_target_pairs={{1,0},{2,1},{3,2},{5,4},{6,5},{7,6},{9,8},{10,9},{11,10},{13,12},{... | collective-permute-start | bytes 688136 | tf_op jit(solution)/shard_map/ppermute | solution.py:40
  8.1 0.6 %fusion.41 = (s32[1,1]{0,1:T(1,128)}, s32[1,1]{0,1:T(1,128)}) fusion(s32[2,1]{0,1:T(1,128)S(1)} %copy-done.2, s32[]{:T(128)S(6)} %select_n.79), kind=kLoop, calls=%fused_computation.128 | loop fusion | flops 1 | bytes 16 | tf_op jit(solution)/shard_map/sub | solution.py:115
  11.9 0.1 pad.133.clone
  12.1 3.6 %collective-permute-done.1 = f32[56,1024]{1,0:T(8,128)S(1)} collective-permute-done((f32[56,1024]{1,0:T(8,128)S(1)}, f32[56,1024]{1,0:T(8,128)S(1)}, u32[]{:S(2)}, u32[]{:S(2)}) %collective-permute-start.1) | collective-permute-done | bytes 229408 | tf_op jit(solution)/shard_map/ppermute | solution.py:40
  15.7 0.1 pad_maximum_fusion.5
  16.0 0.1 reshape.91
  16.1 0.1 reshape.93
  16.3 0.7 %concatenate.33 = f32[4,4,12,1024]{3,2,0,1:T(8,128)S(1)} concatenate(f32[4,4,1,1024]{3,2,0,1:T(1,128)S(1)} %copy.21, f32[4,4,3,1024]{3,2,0,1:T(4,128)S(1)} %copy.22, f32[4,4,4,1024]{3,2,0,1:T(4,128)S(1)} %pad_maximum_fusion, f32[4,4,3,1024]{3,2,0,1:T(4,128)S(1)} %copy.23, f32[4,4,1,1024]{3,2,0,1:T(1,128)S(1)} %broadcast_in_dim.133), dimensions={2} | concatenate | bytes 1572864 | tf_op jit(solution)/shard_map/concatenate | solution.py:103
  16.9 0.1 slice_bitcast_fusion.5
  17.2 11.7 %collective-permute-start.3 = (f32[54,1024]{1,0:T(8,128)S(1)}, f32[54,1024]{1,0:T(8,128)S(1)}, u32[]{:S(2)}, u32[]{:S(2)}) collective-permute-start(f32[54,1024]{1,0:T(8,128)S(1)} %pad_maximum_fusion.4), channel_id=1, source_target_pairs={{4,0},{8,4},{12,8},{16,12},{20,16},{24,20},{28,24},{32,28},{36,32}... | collective-permute-start | bytes 663560 | tf_op jit(solution)/shard_map/ppermute | solution.py:37
  28.9 1.9 %collective-permute-start.2 = (f32[54,1024]{1,0:T(8,128)S(1)}, f32[54,1024]{1,0:T(8,128)S(1)}, u32[]{:S(2)}, u32[]{:S(2)}) collective-permute-start(f32[54,1024]{1,0:T(8,128)S(1)} %pad_maximum_fusion.3), channel_id=1, source_target_pairs={{0,4},{4,8},{8,12},{12,16},{16,20},{20,24},{24,28},{28,32},{32,36}... | collective-permute-start | bytes 663560 | tf_op jit(solution)/shard_map/ppermute | solution.py:37
  30.9 1.6 %collective-permute-done.3 = f32[54,1024]{1,0:T(8,128)S(1)} collective-permute-done((f32[54,1024]{1,0:T(8,128)S(1)}, f32[54,1024]{1,0:T(8,128)S(1)}, u32[]{:S(2)}, u32[]{:S(2)}) %collective-permute-start.3) | collective-permute-done | bytes 221216 | tf_op jit(solution)/shard_map/ppermute | solution.py:37
  32.6 6.4 %collective-permute-done.2 = f32[54,1024]{1,0:T(8,128)S(1)} collective-permute-done((f32[54,1024]{1,0:T(8,128)S(1)}, f32[54,1024]{1,0:T(8,128)S(1)}, u32[]{:S(2)}, u32[]{:S(2)}) %collective-permute-start.2) | collective-permute-done | bytes 221216 | tf_op jit(solution)/shard_map/ppermute | solution.py:37
  39.1 0.3 maximum_maximum_fusion
  39.4 0.2 copy.24
  39.8 0.1 slice_bitcast_fusion.2
  39.9 1.2 %fusion.8 = f32[8,12,1024]{2,1,0:T(8,128)S(1)} fusion(f32[8,12,1024]{2,1,0:T(8,128)S(1)} %get-tuple-element.11, pred[12]{0:T(512)(128)(4,1)S(1)} %get-tuple-element.34, pred[12]{0:T(512)(128)(4,1)S(1)} %get-tuple-element.35, pred[8]{0:T(512)(128)(4,1)S(1)} %get-tuple-element.36, pred[8]{0:T(512)(128)(4,1)S(1)} %get-tuple-element.37, ...), kind=kLoop, calls=%fused_computation.39 | loop fusion | flops 4227072 | bytes 1968168 | tf_op jit(solution)/shard_map/add | solution.py:163
  41.1 1.2 %fusion.26 = f32[8,12,1024]{2,1,0:T(8,128)S(1)} fusion(f32[8,12,1024]{2,1,0:T(8,128)S(1)} %fusion.8, pred[12]{0:T(512)(128)(4,1)S(1)} %get-tuple-element.34, pred[12]{0:T(512)(128)(4,1)S(1)} %get-tuple-element.35, pred[8]{0:T(512)(128)(4,1)S(1)} %get-tuple-element.36, pred[8]{0:T(512)(128)(4,1)S(1)} %get-tuple-element.37, ...), kind=kLoop, calls=%fused_computation.57 | loop fusion | flops 4227072 | bytes 1968168 | tf_op jit(solution)/shard_map/add | solution.py:163
  42.4 1.9 %collective-permute-start.4 = (f32[2,8,1024]{2,1,0:T(8,128)S(1)}, f32[2,8,1024]{2,1,0:T(8,128)S(1)}, u32[]{:S(2)}, u32[]{:S(2)}) collective-permute-start(f32[2,8,1024]{2,1,0:T(8,128)S(1)} %constant_dynamic-slice_fusion), channel_id=1, source_target_pairs={{0,4},{4,8},{8,12},{12,16},{16,20},{20,24},{24,28},{28,32},{32,36}... | collective-permute-start | bytes 196616 | tf_op jit(solution)/shard_map/ppermute | solution.py:37
  44.3 1.3 %stack.60.flags_ref = s32[5]{0:T(128)} concatenate(s32[1]{0:T(128)} %bitcast, s32[1]{0:T(128)} %bitcast.1, s32[1]{0:T(128)} %bitcast.2, s32[1]{0:T(128)} %bitcast.3, s32[1]{0:T(128)} %bitcast.4), dimensions={0} | concatenate | bytes 40 | tf_op jit(solution)/shard_map/stack | solution.py:331
  45.6 6.0 %collective-permute-start.5 = (f32[2,8,1024]{2,1,0:T(8,128)S(1)}, f32[2,8,1024]{2,1,0:T(8,128)S(1)}, u32[]{:S(2)}, u32[]{:S(2)}) collective-permute-start(f32[2,8,1024]{2,1,0:T(8,128)S(1)} %slice.274), channel_id=1, source_target_pairs={{4,0},{8,4},{12,8},{16,12},{20,16},{24,20},{28,24},{32,28},{36,32}... | collective-permute-start | bytes 196616 | tf_op jit(solution)/shard_map/ppermute | solution.py:37
  51.7 0.1 maximum_maximum_fusion.1
  51.7 1.8 %collective-permute-done.5 = f32[2,8,1024]{2,1,0:T(8,128)S(1)} collective-permute-done((f32[2,8,1024]{2,1,0:T(8,128)S(1)}, f32[2,8,1024]{2,1,0:T(8,128)S(1)}, u32[]{:S(2)}, u32[]{:S(2)}) %collective-permute-start.5) | collective-permute-done | bytes 65568 | tf_op jit(solution)/shard_map/ppermute | solution.py:37
  53.5 0.7 %copy-done.1 = f32[8,8,1024]{2,1,0:T(8,128)} copy-done((f32[8,8,1024]{2,1,0:T(8,128)}, f32[8,8,1024]{2,1,0:T(8,128)S(1)}, u32[]{:S(2)}) %copy-start.1) | copy-done | bytes 262168
  54.2 2.6 %shard_map.50 = (f32[4,4,1024]{2,1,0:T(4,128)}, f32[4,4,1024]{2,1,0:T(4,128)}) custom-call(s32[5]{0:T(128)} %stack.60.flags_ref, f32[8,8,1024]{2,1,0:T(8,128)} %copy-done.1), custom_call_target="tpu_custom_call" | custom-call | tf_op jit(solution)/shard_map/pallas_call | solution.py:301
  (58 shorter events, 1.1 us)
Async XLA Ops:
  0.6 1.8 %copy-start = (bf16[3,2,4,4,1024]{4,3,2,1,0:T(4,128)(2,1)S(1)}, bf16[3,2,4,4,1024]{4,3,2,1,0:T(4,128)(2,1)}, u32[]{:S(2)}) copy-start(bf16[3,2,4,4,1024]{4,3,2,1,0:T(4,128)(2,1)} %param.4) | copy-start | bytes 589828
  2.5 5.5 %copy-start.2 = (s32[2,1]{0,1:T(1,128)S(1)}, s32[2,1]{0,1:T(1,128)}, u32[]{:S(2)}) copy-start(s32[2,1]{0,1:T(1,128)} %param.5) | copy-start | bytes 28
  3.0 9.0 %collective-permute-start = (f32[56,1024]{1,0:T(8,128)S(1)}, f32[56,1024]{1,0:T(8,128)S(1)}, u32[]{:S(2)}, u32[]{:S(2)}) collective-permute-start(f32[56,1024]{1,0:T(8,128)S(1)} %pad_maximum_fusion.1), channel_id=1, source_target_pairs={{0,1},{1,2},{2,3},{4,5},{5,6},{6,7},{8,9},{9,10},{10,11},{12,13},{... | collective-permute-start | bytes 688136 | tf_op jit(solution)/shard_map/ppermute | solution.py:40
  6.7 9.0 %collective-permute-start.1 = (f32[56,1024]{1,0:T(8,128)S(1)}, f32[56,1024]{1,0:T(8,128)S(1)}, u32[]{:S(2)}, u32[]{:S(2)}) collective-permute-start(f32[56,1024]{1,0:T(8,128)S(1)} %pad_maximum_fusion.2), channel_id=1, source_target_pairs={{1,0},{2,1},{3,2},{5,4},{6,5},{7,6},{9,8},{10,9},{11,10},{13,12},{... | collective-permute-start | bytes 688136 | tf_op jit(solution)/shard_map/ppermute | solution.py:40
  17.2 15.3 %collective-permute-start.3 = (f32[54,1024]{1,0:T(8,128)S(1)}, f32[54,1024]{1,0:T(8,128)S(1)}, u32[]{:S(2)}, u32[]{:S(2)}) collective-permute-start(f32[54,1024]{1,0:T(8,128)S(1)} %pad_maximum_fusion.4), channel_id=1, source_target_pairs={{4,0},{8,4},{12,8},{16,12},{20,16},{24,20},{28,24},{32,28},{36,32}... | collective-permute-start | bytes 663560 | tf_op jit(solution)/shard_map/ppermute | solution.py:37
  28.9 10.0 %collective-permute-start.2 = (f32[54,1024]{1,0:T(8,128)S(1)}, f32[54,1024]{1,0:T(8,128)S(1)}, u32[]{:S(2)}, u32[]{:S(2)}) collective-permute-start(f32[54,1024]{1,0:T(8,128)S(1)} %pad_maximum_fusion.3), channel_id=1, source_target_pairs={{0,4},{4,8},{8,12},{12,16},{16,20},{20,24},{24,28},{28,32},{32,36}... | collective-permute-start | bytes 663560 | tf_op jit(solution)/shard_map/ppermute | solution.py:37
  42.4 9.3 %collective-permute-start.4 = (f32[2,8,1024]{2,1,0:T(8,128)S(1)}, f32[2,8,1024]{2,1,0:T(8,128)S(1)}, u32[]{:S(2)}, u32[]{:S(2)}) collective-permute-start(f32[2,8,1024]{2,1,0:T(8,128)S(1)} %constant_dynamic-slice_fusion), channel_id=1, source_target_pairs={{0,4},{4,8},{8,12},{12,16},{16,20},{20,24},{24,28},{28,32},{32,36}... | collective-permute-start | bytes 196616 | tf_op jit(solution)/shard_map/ppermute | solution.py:37
  45.6 7.9 %collective-permute-start.5 = (f32[2,8,1024]{2,1,0:T(8,128)S(1)}, f32[2,8,1024]{2,1,0:T(8,128)S(1)}, u32[]{:S(2)}, u32[]{:S(2)}) collective-permute-start(f32[2,8,1024]{2,1,0:T(8,128)S(1)} %slice.274), channel_id=1, source_target_pairs={{4,0},{8,4},{12,8},{16,12},{20,16},{24,20},{28,24},{32,28},{36,32}... | collective-permute-start | bytes 196616 | tf_op jit(solution)/shard_map/ppermute | solution.py:37
  53.5 0.7 %copy-start.1 = (f32[8,8,1024]{2,1,0:T(8,128)}, f32[8,8,1024]{2,1,0:T(8,128)S(1)}, u32[]{:S(2)}) copy-start(f32[8,8,1024]{2,1,0:T(8,128)S(1)} %constant_dynamic-update-slice_fusion.grown_ref) | copy-start | bytes 786436

commit v8 on v6

--- a/solution.py
+++ b/solution.py
@@ -45,6 +45,16 @@
     return lax.ppermute(value, ("inline", "xline"), pairs)
 
 
+def exchanged(to_next, to_prev, axis):
+    count = lax.axis_size(axis)
+    even = lax.axis_index(axis) % 2 == 0
+    first = [(i, i ^ 1) for i in range(count) if i ^ 1 < count]
+    second = [(i, j) for a in range(1, count - 1, 2) for i, j in ((a, a + 1), (a + 1, a))]
+    got_first = lax.ppermute(jnp.where(even, to_next, to_prev), axis, first)
+    got_second = lax.ppermute(jnp.where(even, to_prev, to_next), axis, second)
+    return jnp.where(even, got_second, got_first), jnp.where(even, got_first, got_second)
+
+
 def with_columns(block, depth):
     ca = block.ndim - 2
     cols = block.shape[ca]
@@ -55,8 +65,9 @@
 
 def with_rows(block, width, depth):
     ra = block.ndim - 3
-    from_prev = moved(lax.dynamic_slice_in_dim(block, width - depth, depth, ra), 1, 0)
-    from_next = moved(lax.slice_in_dim(block, 0, depth, axis=ra), -1, 0)
+    from_prev, from_next = exchanged(
+        lax.dynamic_slice_in_dim(block, width - depth, depth, ra), lax.slice_in_dim(block, 0, depth, axis=ra), "inline"
+    )
     return placed_rows(block, from_prev, from_next, width, depth)
 
 
@@ -87,8 +98,9 @@
     far = jnp.stack([fields[0], fields[2]], 0)
     to_right = packed([fields[:, :, 1:], far[:, :, 0]])
     to_left = packed([fields[:, :, : cols - 1], far[:, :, cols - 1]])
-    from_left = unpacked(moved(to_right, 0, 1), [(n_f, rows, cols - 1, samples), (2, rows, samples)])
-    from_right = unpacked(moved(to_left, 0, -1), [(n_f, rows, cols - 1, samples), (2, rows, samples)])
+    got_left, got_right = exchanged(to_right, to_left, "xline")
+    from_left = unpacked(got_left, [(n_f, rows, cols - 1, samples), (2, rows, samples)])
+    from_right = unpacked(got_right, [(n_f, rows, cols - 1, samples), (2, rows, samples)])
 
     def edge(near, outer, outer_first):
         zero = jnp.zeros_like(outer[0])
@@ -123,8 +135,9 @@
         row_far = jnp.pad(jnp.pad(p_far, pad_mid), [(0, 2), (0, 0), (0, 0)])
         return row_near, row_far
 
-    prev_near, prev_far = rebuilt(moved(to_next, 1, 0))
-    next_near, next_far = rebuilt(moved(to_prev, -1, 0))
+    got_prev, got_next = exchanged(to_next, to_prev, "inline")
+    prev_near, prev_far = rebuilt(got_prev)
+    next_near, next_far = rebuilt(got_next)
     from_prev = jnp.stack([prev_far, prev_near], 1)
     from_next = jnp.stack([next_near, next_far], 1)
     return placed_rows(wide, from_prev, from_next, width, h)

time: 51.9 us -> 55.4 us (1.067)
  the two profiles are of different devices: /device:TPU:30 before, /device:TPU:14 now
where the time goes in v8:
time: 55.4 us; the launch traced here: 55 us
  starting transfers between devices  28.9 us (52%)
  waiting for transfers between devices  9.81 us (18%)
  other arithmetic  7.96 us (14%)
  local copies, waits for them, and re-layouts  4.37 us (8%)
  between operations  3.94 us (7%)
    ppermute x3, starting transfers between devices, exchanged(): got_second = lax.ppermute(jnp.where(even, to_prev, to_next), axis, second)  20.8 us
    ppermute x3, starting transfers between devices, exchanged(): got_first = lax.ppermute(jnp.where(even, to_next, to_prev), axis, first)  8.1 us
    ppermute x3, waiting for transfers between devices, exchanged(): got_second = lax.ppermute(jnp.where(even, to_prev, to_next), axis, second)  6.24 us
    ppermute x3, waiting for transfers between devices, exchanged(): got_first = lax.ppermute(jnp.where(even, to_next, to_prev), axis, first)  3.57 us
    add x2, other arithmetic, relax_step(): return values + step_size * change  2.36 us
    dynamic_slice x2, local copies, waits for them, and re-layouts, on_device(): field = lax.dynamic_index_in_dim(survey, batch, 0, keepdims=False)  1.73 us
    mul x4, other arithmetic, attributes(): 0.25 * (neighbor(member, which_axis, 1, up_open) + 2.0 * member + neighbo...  1.37 us
  transfers between devices with their start and end apart: 6, of which 3 were waited for; matrix products, arithmetic and copies ran while one was open for 3% of the time, Pallas kernels for 0%

profile of v8, /device:TPU:14, one launch (start us, length us, event | category | flops | bytes accessed | tf_op | source)
XLA Modules:
  0.0 55.0 jit_solution(9084152734193938423)
XLA Ops:
  0.7 0.9 %fusion.173 = f32[1,4,4,1024]{3,2,0,1:T(4,128)S(1)} fusion(f32[2,4,4,1024]{3,2,1,0:T(4,128)} %param.3, s32[]{:T(128)S(6)} %select_n.292), kind=kLoop, calls=%fused_computation.320 | loop fusion | bytes 131076 | tf_op jit(solution)/shard_map/jit(dynamic_index_in_dim)/dynamic_slice | solution.py:222
  1.5 0.8 %constant_dynamic-slice_fusion.1 = f32[1,4,4,1024]{3,2,1,0:T(4,128)S(1)} fusion(f32[2,4,4,1024]{3,2,1,0:T(4,128)} %param.3, s32[]{:T(128)S(6)} %select_n.292), kind=kLoop, calls=%fused_computation.304 | loop fusion | bytes 131076 | tf_op jit(solution)/shard_map/jit(dynamic_index_in_dim)/dynamic_slice | solution.py:222
  2.4 0.1 fusion.33
  2.6 0.1 reshape.98
  2.8 0.2 fusion.146
  3.0 0.1 reshape.99
  3.2 2.4 %collective-permute-start.1 = (f32[56,1024]{1,0:T(8,128)S(1)}, f32[56,1024]{1,0:T(8,128)S(1)}, u32[]{:S(2)}, u32[]{:S(2)}) collective-permute-start(f32[56,1024]{1,0:T(8,128)S(1)} %get-tuple-element.59), channel_id=1, source_target_pairs={{0,1},{1,0},{2,3},{3,2},{4,5},{5,4},{6,7},{7,6},{8,9},{9,8},{10,11... | collective-permute-start | bytes 688136 | tf_op jit(solution)/shard_map/ppermute | solution.py:53
  5.6 4.3 %collective-permute-start = (f32[56,1024]{1,0:T(8,128)S(1)}, f32[56,1024]{1,0:T(8,128)S(1)}, u32[]{:S(2)}, u32[]{:S(2)}) collective-permute-start(f32[56,1024]{1,0:T(8,128)S(1)} %get-tuple-element.60), channel_id=1, source_target_pairs={{1,2},{2,1},{5,6},{6,5},{9,10},{10,9},{13,14},{14,13},{17,18},{18,... | collective-permute-start | bytes 688136 | tf_op jit(solution)/shard_map/ppermute | solution.py:54
  10.0 0.6 %constant_dynamic-slice_fusion.2 = s32[1,1]{0,1:T(1,128)} fusion(s32[2,1]{0,1:T(1,128)S(1)} %copy-done.1, s32[]{:T(128)S(6)} %select_n.292), kind=kLoop, calls=%fused_computation.305 | loop fusion | bytes 12 | tf_op jit(solution)/shard_map/jit(dynamic_index_in_dim)/dynamic_slice | solution.py:224
  13.4 1.8 %collective-permute-done = f32[56,1024]{1,0:T(8,128)S(1)} collective-permute-done((f32[56,1024]{1,0:T(8,128)S(1)}, f32[56,1024]{1,0:T(8,128)S(1)}, u32[]{:S(2)}, u32[]{:S(2)}) %collective-permute-start) | collective-permute-done | bytes 229408 | tf_op jit(solution)/shard_map/ppermute | solution.py:54
  15.8 0.7 %concatenate.33 = f32[4,4,12,1024]{3,2,0,1:T(8,128)S(1)} concatenate(f32[4,4,1,1024]{3,2,0,1:T(1,128)S(1)} %copy.20, f32[4,4,3,1024]{3,2,0,1:T(4,128)S(1)} %copy.21, f32[4,4,4,1024]{3,2,0,1:T(4,128)S(1)} %pad_maximum_fusion, f32[4,4,3,1024]{3,2,0,1:T(4,128)S(1)} %copy.22, f32[4,4,1,1024]{3,2,0,1:T(1,128)S(1)} %copy.23), dimensions={2} | concatenate | bytes 1572864 | tf_op jit(solution)/shard_map/concatenate | solution.py:113
  16.8 3.8 %collective-permute-start.3 = (f32[54,1024]{1,0:T(8,128)S(1)}, f32[54,1024]{1,0:T(8,128)S(1)}, u32[]{:S(2)}, u32[]{:S(2)}) collective-permute-start(f32[54,1024]{1,0:T(8,128)S(1)} %get-tuple-element.55), channel_id=1, source_target_pairs={{0,4},{4,0},{8,12},{12,8},{16,20},{20,16},{24,28},{28,24},{32,36},... | collective-permute-start | bytes 663560 | tf_op jit(solution)/shard_map/ppermute | solution.py:53
  20.7 10.8 %collective-permute-start.2 = (f32[54,1024]{1,0:T(8,128)S(1)}, f32[54,1024]{1,0:T(8,128)S(1)}, u32[]{:S(2)}, u32[]{:S(2)}) collective-permute-start(f32[54,1024]{1,0:T(8,128)S(1)} %get-tuple-element.56), channel_id=1, source_target_pairs={{4,8},{8,4},{12,16},{16,12},{20,24},{24,20},{28,32},{32,28},{36,40... | collective-permute-start | bytes 663560 | tf_op jit(solution)/shard_map/ppermute | solution.py:54
  31.5 4.4 %collective-permute-done.2 = f32[54,1024]{1,0:T(8,128)S(1)} collective-permute-done((f32[54,1024]{1,0:T(8,128)S(1)}, f32[54,1024]{1,0:T(8,128)S(1)}, u32[]{:S(2)}, u32[]{:S(2)}) %collective-permute-start.2) | collective-permute-done | bytes 221216 | tf_op jit(solution)/shard_map/ppermute | solution.py:54
  36.2 0.3 maximum_maximum_fusion
  36.6 0.1 slice_bitcast_fusion.2
  36.7 1.2 %fusion.8 = f32[8,12,1024]{2,1,0:T(8,128)S(1)} fusion(f32[8,12,1024]{2,1,0:T(8,128)S(1)} %get-tuple-element.40, pred[12]{0:T(512)(128)(4,1)S(1)} %and_not_fusion.1, pred[12]{0:T(512)(128)(4,1)S(1)} %and_not_fusion.2, pred[8]{0:T(512)(128)(4,1)S(1)} %and_not_fusion.3, pred[8]{0:T(512)(128)(4,1)S(1)} %and_not_fusion.4, ...), kind=kLoop, calls=%fused_computation.39 | loop fusion | flops 4227072 | bytes 1968168 | tf_op jit(solution)/shard_map/add | solution.py:174
  37.9 1.2 %fusion.26 = f32[8,12,1024]{2,1,0:T(8,128)S(1)} fusion(f32[8,12,1024]{2,1,0:T(8,128)S(1)} %fusion.8, pred[12]{0:T(512)(128)(4,1)S(1)} %and_not_fusion.1, pred[12]{0:T(512)(128)(4,1)S(1)} %and_not_fusion.2, pred[8]{0:T(512)(128)(4,1)S(1)} %and_not_fusion.3, pred[8]{0:T(512)(128)(4,1)S(1)} %and_not_fusion.4, pred[1024]{0:T(1024)(128)(4,1)S(1)} %get-tuple-element.93, ...), kind=kLoop, calls=%fused_computation.57 | loop fusion | flops 4227072 | bytes 1968168 | tf_op jit(solution)/shard_map/add | solution.py:174
  39.2 5.8 %collective-permute-start.4 = (f32[2,8,1024]{2,1,0:T(8,128)S(1)}, f32[2,8,1024]{2,1,0:T(8,128)S(1)}, u32[]{:S(2)}, u32[]{:S(2)}) collective-permute-start(f32[2,8,1024]{2,1,0:T(8,128)S(1)} %get-tuple-element.48), channel_id=1, source_target_pairs={{4,8},{8,4},{12,16},{16,12},{20,24},{24,20},{28,32},{32,28},{36,40... | collective-permute-start | bytes 196616 | tf_op jit(solution)/shard_map/ppermute | solution.py:54
  44.9 1.9 %collective-permute-start.5 = (f32[2,8,1024]{2,1,0:T(8,128)S(1)}, f32[2,8,1024]{2,1,0:T(8,128)S(1)}, u32[]{:S(2)}, u32[]{:S(2)}) collective-permute-start(f32[2,8,1024]{2,1,0:T(8,128)S(1)} %get-tuple-element.47), channel_id=1, source_target_pairs={{0,4},{4,0},{8,12},{12,8},{16,20},{20,16},{24,28},{28,24},{32,36},... | collective-permute-start | bytes 196616 | tf_op jit(solution)/shard_map/ppermute | solution.py:53
  46.8 0.7 %iota_compare_fusion.4 = pred[4]{0:T(512)(128)(4,1)S(1)} fusion(s32[]{:T(128)} %bitcast), kind=kLoop, calls=%fused_computation.314 | loop fusion | flops 4 | bytes 8 | tf_op jit(solution)/shard_map/lt | solution.py:226
  47.5 3.6 %collective-permute-done.5 = f32[2,8,1024]{2,1,0:T(8,128)S(1)} collective-permute-done((f32[2,8,1024]{2,1,0:T(8,128)S(1)}, f32[2,8,1024]{2,1,0:T(8,128)S(1)}, u32[]{:S(2)}, u32[]{:S(2)}) %collective-permute-start.5) | collective-permute-done | bytes 65568 | tf_op jit(solution)/shard_map/ppermute | solution.py:53
  51.1 0.1 maximum_maximum_fusion.1
  51.2 0.2 fusion.149
  51.4 0.2 fusion.148
  51.6 0.2 broadcast_multiply_fusion.11
  51.9 0.5 broadcast_multiply_fusion.3
  52.4 0.3 broadcast_multiply_fusion
  52.6 0.4 broadcast_multiply_fusion.2
  53.1 0.3 fusion.87
  53.4 0.7 %fusion.64 = (f32[8,8,1024]{2,1,0:T(8,128)S(1)}, f32[8,8,1024]{2,1,0:T(8,128)S(1)}, f32[8,8,1024]{2,1,0:T(8,128)S(1)}, f32[8,8,1024]{2,1,0:T(8,128)S(1)}) fusion(f32[8,8,1024]{2,1,0:T(8,128)S(1)} %get-tuple-element.75, f32[8,8,1024]{2,1,0:T(8,128)S(1)} %get-tuple-element.76, pred[1024]{0:T(1024)(128)(4,1)S(1)} %get-tuple-element.93, ...), kind=kLoop, calls=%fused_computation.147 | loop fusion | flops 1900544 | bytes 3147776 | tf_op jit(solution)/shard_map/add | solution.py:207
  54.1 0.9 %fusion.134 = (f32[1,4,4,1024]{3,2,1,0:T(4,128)}, f32[1,4,4,1024]{3,2,1,0:T(4,128)}) fusion(f32[8,8,1024]{2,1,0:T(8,128)S(1)} %get-tuple-element.50, f32[8,8,1024]{2,1,0:T(8,128)S(1)} %get-tuple-element.52, f32[8,8,1024]{2,1,0:T(8,128)S(1)} %get-tuple-element.13, f32[8,8,1024]{2,1,0:T(8,128)S(1)} %get-tuple-element.14, ...), kind=kLoop, calls=%fused_computation.256 | loop fusion | flops 393216 | bytes 983044 | tf_op jit(solution)/shard_map/broadcast_in_dim | solution.py:239
  (69 shorter events, 1.6 us)
Async XLA Ops:
  0.6 1.8 %copy-start = (bf16[3,2,4,4,1024]{4,3,2,1,0:T(4,128)(2,1)S(1)}, bf16[3,2,4,4,1024]{4,3,2,1,0:T(4,128)(2,1)}, u32[]{:S(2)}) copy-start(bf16[3,2,4,4,1024]{4,3,2,1,0:T(4,128)(2,1)} %param.4) | copy-start | bytes 589828
  2.5 7.5 %copy-start.1 = (s32[2,1]{0,1:T(1,128)S(1)}, s32[2,1]{0,1:T(1,128)}, u32[]{:S(2)}) copy-start(s32[2,1]{0,1:T(1,128)} %param.5) | copy-start | bytes 28
  3.2 10.1 %collective-permute-start.1 = (f32[56,1024]{1,0:T(8,128)S(1)}, f32[56,1024]{1,0:T(8,128)S(1)}, u32[]{:S(2)}, u32[]{:S(2)}) collective-permute-start(f32[56,1024]{1,0:T(8,128)S(1)} %get-tuple-element.59), channel_id=1, source_target_pairs={{0,1},{1,0},{2,3},{3,2},{4,5},{5,4},{6,7},{7,6},{8,9},{9,8},{10,11... | collective-permute-start | bytes 688136 | tf_op jit(solution)/shard_map/ppermute | solution.py:53
  5.6 9.6 %collective-permute-start = (f32[56,1024]{1,0:T(8,128)S(1)}, f32[56,1024]{1,0:T(8,128)S(1)}, u32[]{:S(2)}, u32[]{:S(2)}) collective-permute-start(f32[56,1024]{1,0:T(8,128)S(1)} %get-tuple-element.60), channel_id=1, source_target_pairs={{1,2},{2,1},{5,6},{6,5},{9,10},{10,9},{13,14},{14,13},{17,18},{18,... | collective-permute-start | bytes 688136 | tf_op jit(solution)/shard_map/ppermute | solution.py:54
  16.8 14.6 %collective-permute-start.3 = (f32[54,1024]{1,0:T(8,128)S(1)}, f32[54,1024]{1,0:T(8,128)S(1)}, u32[]{:S(2)}, u32[]{:S(2)}) collective-permute-start(f32[54,1024]{1,0:T(8,128)S(1)} %get-tuple-element.55), channel_id=1, source_target_pairs={{0,4},{4,0},{8,12},{12,8},{16,20},{20,16},{24,28},{28,24},{32,36},... | collective-permute-start | bytes 663560 | tf_op jit(solution)/shard_map/ppermute | solution.py:53
  20.7 15.2 %collective-permute-start.2 = (f32[54,1024]{1,0:T(8,128)S(1)}, f32[54,1024]{1,0:T(8,128)S(1)}, u32[]{:S(2)}, u32[]{:S(2)}) collective-permute-start(f32[54,1024]{1,0:T(8,128)S(1)} %get-tuple-element.56), channel_id=1, source_target_pairs={{4,8},{8,4},{12,16},{16,12},{20,24},{24,20},{28,32},{32,28},{36,40... | collective-permute-start | bytes 663560 | tf_op jit(solution)/shard_map/ppermute | solution.py:54
  39.2 8.3 %collective-permute-start.4 = (f32[2,8,1024]{2,1,0:T(8,128)S(1)}, f32[2,8,1024]{2,1,0:T(8,128)S(1)}, u32[]{:S(2)}, u32[]{:S(2)}) collective-permute-start(f32[2,8,1024]{2,1,0:T(8,128)S(1)} %get-tuple-element.48), channel_id=1, source_target_pairs={{4,8},{8,4},{12,16},{16,12},{20,24},{24,20},{28,32},{32,28},{36,40... | collective-permute-start | bytes 196616 | tf_op jit(solution)/shard_map/ppermute | solution.py:54
  44.9 6.2 %collective-permute-start.5 = (f32[2,8,1024]{2,1,0:T(8,128)S(1)}, f32[2,8,1024]{2,1,0:T(8,128)S(1)}, u32[]{:S(2)}, u32[]{:S(2)}) collective-permute-start(f32[2,8,1024]{2,1,0:T(8,128)S(1)} %get-tuple-element.47), channel_id=1, source_target_pairs={{0,4},{4,0},{8,12},{12,8},{16,20},{20,16},{24,28},{28,24},{32,36},... | collective-permute-start | bytes 196616 | tf_op jit(solution)/shard_map/ppermute | solution.py:53

commit v9 on v6

--- a/solution.py
+++ b/solution.py
@@ -149,44 +149,74 @@
     ]
 
 
-def relax_step(values, coeffs, masks):
-    change = jnp.zeros_like(values)
+def near(source, lo, hi, at, which_axis, offset, opened):
+    centre = source[lo - at : hi - at]
+    if which_axis == 0:
+        return jnp.where(opened, source[lo - at + offset : hi - at + offset], centre)
+    return jnp.where(opened, shifted(centre, which_axis, offset), centre)
+
+
+def rows_of(masks, lo, hi):
+    rows = masks[0]
+    return [(rows[0][lo:hi], rows[1][lo:hi])] + list(masks[1:])
+
+
+def relax_rows(values, coeffs, masks, lo, hi, at):
+    opened = rows_of(masks, lo, hi)
+    centre = values[lo - at : hi - at]
+    change = jnp.zeros_like(centre)
     for which_axis in range(3):
         kk = coeffs[which_axis]
-        up_open, down_open = masks[which_axis]
-        for offset, opened in ((1, up_open), (-1, down_open)):
-            change = change + 0.5 * (kk + neighbor(kk, which_axis, offset, opened)) * (
-                neighbor(values, which_axis, offset, opened) - values
+        k_centre = kk[lo - at : hi - at]
+        up_open, down_open = opened[which_axis]
+        for offset, mask in ((1, up_open), (-1, down_open)):
+            change = change + 0.5 * (k_centre + near(kk, lo, hi, at, which_axis, offset, mask)) * (
+                near(values, lo, hi, at, which_axis, offset, mask) - centre
             )
-    return values + step_size * change
-
-
-def attributes(grown, masks):
+    return centre + step_size * change
+
+
+def attributes(grown, masks, h):
+    n_rows = grown.shape[0]
+    lo, hi = 1, n_rows - 1
+    outer = rows_of(masks, lo, hi)
     grads = []
     for which_axis in range(3):
-        up_open, down_open = masks[which_axis]
+        up_open, down_open = outer[which_axis]
         grads.append(
             0.5
-            * (neighbor(grown, which_axis, 1, up_open) - neighbor(grown, which_axis, -1, down_open))
+            * (
+                near(grown, lo, hi, 0, which_axis, 1, up_open)
+                - near(grown, lo, hi, 0, which_axis, -1, down_open)
+            )
         )
+    inner_lo, inner_hi = h, n_rows - h
+    inner = rows_of(masks, inner_lo, inner_hi)
+    centre = grown[inner_lo:inner_hi]
     seconds = []
     for which_axis in range(2):
-        up_open, down_open = masks[which_axis]
+        up_open, down_open = inner[which_axis]
         seconds.append(
-            neighbor(grown, which_axis, 1, up_open)
-            + neighbor(grown, which_axis, -1, down_open)
-            - 2.0 * grown
+            near(grown, inner_lo, inner_hi, 0, which_axis, 1, up_open)
+            + near(grown, inner_lo, inner_hi, 0, which_axis, -1, down_open)
+            - 2.0 * centre
         )
     combos = [(0, 0), (1, 1), (2, 2), (0, 1), (0, 2), (1, 2)]
     tensor = []
     for first_index, second_index in combos:
         member = grads[first_index] * grads[second_index]
-        for which_axis in range(3):
-            up_open, down_open = masks[which_axis]
+        up_open, down_open = inner[0]
+        member = 0.25 * (
+            near(member, inner_lo, inner_hi, lo, 0, 1, up_open)
+            + 2.0 * member[inner_lo - lo : inner_hi - lo]
+            + near(member, inner_lo, inner_hi, lo, 0, -1, down_open)
+        )
+        for which_axis in (1, 2):
+            up_open, down_open = inner[which_axis]
             member = 0.25 * (
-                neighbor(member, which_axis, 1, up_open)
+                near(member, inner_lo, inner_hi, inner_lo, which_axis, 1, up_open)
                 + 2.0 * member
-                + neighbor(member, which_axis, -1, down_open)
+                + near(member, inner_lo, inner_hi, inner_lo, which_axis, -1, down_open)
             )
         tensor.append(member)
     trace = tensor[0] + tensor[1] + tensor[2]
@@ -199,7 +229,9 @@
         - tensor[5] * tensor[5]
     )
     coherence = 1.0 - 3.0 * minors / (trace * trace + epsilon)
-    curvature = (seconds[0] + seconds[1]) / (1.0 + grads[0] * grads[0] + grads[1] * grads[1]) ** 1.5
+    g_in = grads[0][inner_lo - lo : inner_hi - lo]
+    g_x = grads[1][inner_lo - lo : inner_hi - lo]
+    curvature = (seconds[0] + seconds[1]) / (1.0 + g_in * g_in + g_x * g_x) ** 1.5
     return coherence, curvature
 
 
@@ -216,14 +248,18 @@
     grown = diffusion_rows(wide, width, cols)
     masks = face_masks(width, rows, cols, samples, h, cols)
     values, coeffs_grown = grown[0], grown[1:]
+    n_rows = values.shape[0]
+    at = 0
     for repeat in range(STEPS):
-        values = relax_step(values, coeffs_grown, masks)
-    smooth = values[h : h + rows, cols - h : 2 * cols + h]
+        lo, hi = repeat + 1, n_rows - repeat - 1
+        values = relax_rows(values, coeffs_grown[:, lo - 1 :], masks, lo, hi, at)
+        at = lo
+    smooth = values[h - at : h - at + rows, cols - h : 2 * cols + h]
 
     grown = with_rows(smooth, width, h)
     masks = face_masks(width, rows, cols, samples, h, h)
-    results = attributes(grown, masks)
-    return tuple(jnp.where(live, value[h : h + rows, h : h + cols], 0.0)[None] for value in results)
+    results = attributes(grown, masks, h)
+    return tuple(jnp.where(live, value[:, h : h + cols], 0.0)[None] for value in results)
 
 
 def solution(mesh):

time: 51.9 us -> 54.9 us (1.058)
  the two profiles are of different devices: /device:TPU:30 before, /device:TPU:6 now
where the time goes in v9:
time: 54.9 us; the launch traced here: 54.6 us
  starting transfers between devices  26.3 us (48%)
  waiting for transfers between devices  13.6 us (25%)
  other arithmetic  5.89 us (11%)
  local copies, waits for them, and re-layouts  4.91 us (9%)
  between operations  3.87 us (7%)
    ppermute x4, starting transfers between devices, moved(): return lax.ppermute(value, 'inline', pairs)  21.5 us
    ppermute x4, waiting for transfers between devices, moved(): return lax.ppermute(value, 'inline', pairs)  9.81 us
    ppermute x2, starting transfers between devices, moved(): return lax.ppermute(value, 'xline', pairs)  4.79 us
    ppermute x2, waiting for transfers between devices, moved(): return lax.ppermute(value, 'xline', pairs)  3.8 us
    dynamic_slice x2, local copies, waits for them, and re-layouts, on_device(): field = lax.dynamic_index_in_dim(survey, batch, 0, keepdims=False)  1.73 us
    add x2, other arithmetic, relax_rows(): return centre + step_size * change  1.54 us
  transfers between devices with their start and end apart: 6, of which 4 were waited for; matrix products, arithmetic and copies ran while one was open for 4% of the time, Pallas kernels for 0%

profile of v9, /device:TPU:6, one launch (start us, length us, event | category | flops | bytes accessed | tf_op | source)
XLA Modules:
  0.0 54.6 jit_solution(8748581041536389904)
XLA Ops:
  0.7 0.9 %fusion.168 = f32[1,4,4,1024]{3,2,0,1:T(4,128)S(1)} fusion(f32[2,4,4,1024]{3,2,1,0:T(4,128)} %param.3, s32[]{:T(128)S(6)} %select_n.245), kind=kLoop, calls=%fused_computation.319 | loop fusion | bytes 131076 | tf_op jit(solution)/shard_map/jit(dynamic_index_in_dim)/dynamic_slice | solution.py:241
  1.5 0.8 %constant_dynamic-slice_fusion.2 = f32[1,4,4,1024]{3,2,1,0:T(4,128)S(1)} fusion(f32[2,4,4,1024]{3,2,1,0:T(4,128)} %param.3, s32[]{:T(128)S(6)} %select_n.245), kind=kLoop, calls=%fused_computation.304 | loop fusion | bytes 131076 | tf_op jit(solution)/shard_map/jit(dynamic_index_in_dim)/dynamic_slice | solution.py:241
  2.4 0.1 fusion.20
  2.6 0.1 reshape.107
  2.7 0.2 fusion.144
  3.0 3.5 %collective-permute-start = (f32[56,1024]{1,0:T(8,128)S(1)}, f32[56,1024]{1,0:T(8,128)S(1)}, u32[]{:S(2)}, u32[]{:S(2)}) collective-permute-start(f32[56,1024]{1,0:T(8,128)S(1)} %pad_maximum_fusion.1), channel_id=1, source_target_pairs={{0,1},{1,2},{2,3},{4,5},{5,6},{6,7},{8,9},{9,10},{10,11},{12,13},{... | collective-permute-start | bytes 688136 | tf_op jit(solution)/shard_map/ppermute | solution.py:38
  6.5 0.1 reshape.109
  6.7 1.3 %collective-permute-start.1 = (f32[56,1024]{1,0:T(8,128)S(1)}, f32[56,1024]{1,0:T(8,128)S(1)}, u32[]{:S(2)}, u32[]{:S(2)}) collective-permute-start(f32[56,1024]{1,0:T(8,128)S(1)} %pad_maximum_fusion.2), channel_id=1, source_target_pairs={{1,0},{2,1},{3,2},{5,4},{6,5},{7,6},{9,8},{10,9},{11,10},{13,12},{... | collective-permute-start | bytes 688136 | tf_op jit(solution)/shard_map/ppermute | solution.py:38
  8.0 0.6 %constant_dynamic-slice_fusion.3 = s32[1,1]{0,1:T(1,128)} fusion(s32[2,1]{0,1:T(1,128)S(1)} %copy-done.1, s32[]{:T(128)S(6)} %select_n.245), kind=kLoop, calls=%fused_computation.305 | loop fusion | bytes 12 | tf_op jit(solution)/shard_map/jit(dynamic_index_in_dim)/dynamic_slice | solution.py:243
  11.8 3.8 %collective-permute-done.1 = f32[56,1024]{1,0:T(8,128)S(1)} collective-permute-done((f32[56,1024]{1,0:T(8,128)S(1)}, f32[56,1024]{1,0:T(8,128)S(1)}, u32[]{:S(2)}, u32[]{:S(2)}) %collective-permute-start.1) | collective-permute-done | bytes 229408 | tf_op jit(solution)/shard_map/ppermute | solution.py:38
  16.2 0.7 %concatenate.33 = f32[4,4,12,1024]{3,2,0,1:T(8,128)S(1)} concatenate(f32[4,4,1,1024]{3,2,0,1:T(1,128)S(1)} %copy.19, f32[4,4,3,1024]{3,2,0,1:T(4,128)S(1)} %copy.20, f32[4,4,4,1024]{3,2,0,1:T(4,128)S(1)} %pad_maximum_fusion, f32[4,4,3,1024]{3,2,0,1:T(4,128)S(1)} %copy.21, f32[4,4,1,1024]{3,2,0,1:T(1,128)S(1)} %copy.22), dimensions={2} | concatenate | bytes 1572864 | tf_op jit(solution)/shard_map/concatenate | solution.py:101
  17.1 11.7 %collective-permute-start.3 = (f32[54,1024]{1,0:T(8,128)S(1)}, f32[54,1024]{1,0:T(8,128)S(1)}, u32[]{:S(2)}, u32[]{:S(2)}) collective-permute-start(f32[54,1024]{1,0:T(8,128)S(1)} %pad_maximum_fusion.4), channel_id=1, source_target_pairs={{4,0},{8,4},{12,8},{16,12},{20,16},{24,20},{28,24},{32,28},{36,32}... | collective-permute-start | bytes 663560 | tf_op jit(solution)/shard_map/ppermute | solution.py:35
  28.8 1.9 %collective-permute-start.2 = (f32[54,1024]{1,0:T(8,128)S(1)}, f32[54,1024]{1,0:T(8,128)S(1)}, u32[]{:S(2)}, u32[]{:S(2)}) collective-permute-start(f32[54,1024]{1,0:T(8,128)S(1)} %pad_maximum_fusion.3), channel_id=1, source_target_pairs={{0,4},{4,8},{8,12},{12,16},{16,20},{20,24},{24,28},{28,32},{32,36}... | collective-permute-start | bytes 663560 | tf_op jit(solution)/shard_map/ppermute | solution.py:35
  30.8 1.6 %collective-permute-done.3 = f32[54,1024]{1,0:T(8,128)S(1)} collective-permute-done((f32[54,1024]{1,0:T(8,128)S(1)}, f32[54,1024]{1,0:T(8,128)S(1)}, u32[]{:S(2)}, u32[]{:S(2)}) %collective-permute-start.3) | collective-permute-done | bytes 221216 | tf_op jit(solution)/shard_map/ppermute | solution.py:35
  32.5 6.4 %collective-permute-done.2 = f32[54,1024]{1,0:T(8,128)S(1)} collective-permute-done((f32[54,1024]{1,0:T(8,128)S(1)}, f32[54,1024]{1,0:T(8,128)S(1)}, u32[]{:S(2)}, u32[]{:S(2)}) %collective-permute-start.2) | collective-permute-done | bytes 221216 | tf_op jit(solution)/shard_map/ppermute | solution.py:35
  39.1 0.3 maximum_maximum_fusion
  39.4 0.1 slice_bitcast_fusion
  39.6 0.9 %fusion.8 = f32[6,12,1024]{2,1,0:T(8,128)S(1)} fusion(f32[6,12,1024]{2,1,0:T(8,128)S(1)} %get-tuple-element.41, f32[6,12,1024]{2,1,0:T(8,128)S(1)} %get-tuple-element.40, f32[6,12,1024]{2,1,0:T(8,128)S(1)} %get-tuple-element.39, f32[4,8,12,1024]{3,2,0,1:T(8,128)S(1)} %maximum_dynamic-update-slice_fusion, pred[12]{0:T(512)(128)(4,1)S(1)} %get-tuple-element.91, ...), kind=kLoop, calls=%fused_computation.29 | loop fusion | flops 3170304 | bytes 2656292 | tf_op jit(solution)/shard_map/add | solution.py:176
  40.6 0.6 %fusion.29 = f32[4,12,1024]{2,1,0:T(8,128)S(1)} fusion(f32[4,12,1024]{2,1,0:T(8,128)S(1)} %slice.686, f32[4,12,1024]{2,1,0:T(8,128)S(1)} %get-tuple-element.38, f32[4,12,1024]{2,1,0:T(8,128)S(1)} %get-tuple-element.37, f32[6,12,1024]{2,1,0:T(8,128)S(1)} %fusion.8, f32[4,8,12,1024]{3,2,0,1:T(8,128)S(1)} %maximum_dynamic-update-slice_fusion, ...), kind=kLoop, calls=%fused_computation.78 | loop fusion | flops 2113536 | bytes 1771552 | tf_op jit(solution)/shard_map/add | solution.py:176
  41.2 1.9 %collective-permute-start.4 = (f32[2,8,1024]{2,1,0:T(8,128)S(1)}, f32[2,8,1024]{2,1,0:T(8,128)S(1)}, u32[]{:S(2)}, u32[]{:S(2)}) collective-permute-start(f32[2,8,1024]{2,1,0:T(8,128)S(1)} %constant_dynamic-slice_fusion), channel_id=1, source_target_pairs={{0,4},{4,8},{8,12},{12,16},{16,20},{20,24},{24,28},{28,32},{32,36}... | collective-permute-start | bytes 196616 | tf_op jit(solution)/shard_map/ppermute | solution.py:35
  43.2 0.7 %iota_compare_fusion.4 = pred[4]{0:T(512)(128)(4,1)S(1)} fusion(s32[]{:T(128)} %bitcast), kind=kLoop, calls=%fused_computation.314 | loop fusion | flops 4 | bytes 8 | tf_op jit(solution)/shard_map/lt | solution.py:245
  43.8 6.0 %collective-permute-start.5 = (f32[2,8,1024]{2,1,0:T(8,128)S(1)}, f32[2,8,1024]{2,1,0:T(8,128)S(1)}, u32[]{:S(2)}, u32[]{:S(2)}) collective-permute-start(f32[2,8,1024]{2,1,0:T(8,128)S(1)} %slice.695), channel_id=1, source_target_pairs={{4,0},{8,4},{12,8},{16,12},{20,16},{24,20},{28,24},{32,28},{36,32}... | collective-permute-start | bytes 196616 | tf_op jit(solution)/shard_map/ppermute | solution.py:35
  50.0 1.8 %collective-permute-done.5 = f32[2,8,1024]{2,1,0:T(8,128)S(1)} collective-permute-done((f32[2,8,1024]{2,1,0:T(8,128)S(1)}, f32[2,8,1024]{2,1,0:T(8,128)S(1)}, u32[]{:S(2)}, u32[]{:S(2)}) %collective-permute-start.5) | collective-permute-done | bytes 65568 | tf_op jit(solution)/shard_map/ppermute | solution.py:35
  51.8 0.1 fusion.151
  52.0 0.2 fusion.156
  52.3 0.1 broadcast_multiply_fusion.11
  52.4 0.3 broadcast_multiply_fusion.3
  52.7 0.1 broadcast_multiply_fusion
  52.8 0.2 broadcast_multiply_fusion.2
  53.1 0.2 fusion.79
  53.3 0.4 fusion.68
  53.6 1.0 %fusion.129 = (f32[1,4,4,1024]{3,2,1,0:T(4,128)}, f32[1,4,4,1024]{3,2,1,0:T(4,128)}) fusion(f32[4,8,1024]{2,1,0:T(8,128)S(1)} %slice.727, f32[4,8,1024]{2,1,0:T(8,128)S(1)} %slice.726, f32[4,8,1024]{2,1,0:T(8,128)S(1)} %get-tuple-element.60, f32[4,8,1024]{2,1,0:T(8,128)S(1)} %get-tuple-element.59, f32[4,8,1024]{2,1,0:T(8,128)S(1)} %get-tuple-element.51, ...), kind=kLoop, calls=%fused_computation.246 | loop fusion | flops 491520 | bytes 983060 | tf_op jit(solution)/shard_map/broadcast_in_dim | solution.py:262
  (75 shorter events, 2.2 us)
Async XLA Ops:
  0.6 1.8 %copy-start = (bf16[3,2,4,4,1024]{4,3,2,1,0:T(4,128)(2,1)S(1)}, bf16[3,2,4,4,1024]{4,3,2,1,0:T(4,128)(2,1)}, u32[]{:S(2)}) copy-start(bf16[3,2,4,4,1024]{4,3,2,1,0:T(4,128)(2,1)} %param.4) | copy-start | bytes 589828
  2.4 5.6 %copy-start.1 = (s32[2,1]{0,1:T(1,128)S(1)}, s32[2,1]{0,1:T(1,128)}, u32[]{:S(2)}) copy-start(s32[2,1]{0,1:T(1,128)} %param.5) | copy-start | bytes 28
  3.0 8.9 %collective-permute-start = (f32[56,1024]{1,0:T(8,128)S(1)}, f32[56,1024]{1,0:T(8,128)S(1)}, u32[]{:S(2)}, u32[]{:S(2)}) collective-permute-start(f32[56,1024]{1,0:T(8,128)S(1)} %pad_maximum_fusion.1), channel_id=1, source_target_pairs={{0,1},{1,2},{2,3},{4,5},{5,6},{6,7},{8,9},{9,10},{10,11},{12,13},{... | collective-permute-start | bytes 688136 | tf_op jit(solution)/shard_map/ppermute | solution.py:38
  6.7 9.0 %collective-permute-start.1 = (f32[56,1024]{1,0:T(8,128)S(1)}, f32[56,1024]{1,0:T(8,128)S(1)}, u32[]{:S(2)}, u32[]{:S(2)}) collective-permute-start(f32[56,1024]{1,0:T(8,128)S(1)} %pad_maximum_fusion.2), channel_id=1, source_target_pairs={{1,0},{2,1},{3,2},{5,4},{6,5},{7,6},{9,8},{10,9},{11,10},{13,12},{... | collective-permute-start | bytes 688136 | tf_op jit(solution)/shard_map/ppermute | solution.py:38
  17.1 15.3 %collective-permute-start.3 = (f32[54,1024]{1,0:T(8,128)S(1)}, f32[54,1024]{1,0:T(8,128)S(1)}, u32[]{:S(2)}, u32[]{:S(2)}) collective-permute-start(f32[54,1024]{1,0:T(8,128)S(1)} %pad_maximum_fusion.4), channel_id=1, source_target_pairs={{4,0},{8,4},{12,8},{16,12},{20,16},{24,20},{28,24},{32,28},{36,32}... | collective-permute-start | bytes 663560 | tf_op jit(solution)/shard_map/ppermute | solution.py:35
  28.8 10.0 %collective-permute-start.2 = (f32[54,1024]{1,0:T(8,128)S(1)}, f32[54,1024]{1,0:T(8,128)S(1)}, u32[]{:S(2)}, u32[]{:S(2)}) collective-permute-start(f32[54,1024]{1,0:T(8,128)S(1)} %pad_maximum_fusion.3), channel_id=1, source_target_pairs={{0,4},{4,8},{8,12},{12,16},{16,20},{20,24},{24,28},{28,32},{32,36}... | collective-permute-start | bytes 663560 | tf_op jit(solution)/shard_map/ppermute | solution.py:35
  41.2 8.6 %collective-permute-start.4 = (f32[2,8,1024]{2,1,0:T(8,128)S(1)}, f32[2,8,1024]{2,1,0:T(8,128)S(1)}, u32[]{:S(2)}, u32[]{:S(2)}) collective-permute-start(f32[2,8,1024]{2,1,0:T(8,128)S(1)} %constant_dynamic-slice_fusion), channel_id=1, source_target_pairs={{0,4},{4,8},{8,12},{12,16},{16,20},{20,24},{24,28},{28,32},{32,36}... | collective-permute-start | bytes 196616 | tf_op jit(solution)/shard_map/ppermute | solution.py:35
  43.8 7.9 %collective-permute-start.5 = (f32[2,8,1024]{2,1,0:T(8,128)S(1)}, f32[2,8,1024]{2,1,0:T(8,128)S(1)}, u32[]{:S(2)}, u32[]{:S(2)}) collective-permute-start(f32[2,8,1024]{2,1,0:T(8,128)S(1)} %slice.695), channel_id=1, source_target_pairs={{4,0},{8,4},{12,8},{16,12},{20,16},{24,20},{28,24},{32,28},{36,32}... | collective-permute-start | bytes 196616 | tf_op jit(solution)/shard_map/ppermute | solution.py:35

commit v10 on v6

--- a/solution.py
+++ b/solution.py
@@ -149,16 +149,31 @@
     ]
 
 
-def relax_step(values, coeffs, masks):
-    change = jnp.zeros_like(values)
+def near(source, lo, hi, at, which_axis, offset, opened):
+    centre = source[lo - at : hi - at]
+    if which_axis == 0:
+        return jnp.where(opened, source[lo - at + offset : hi - at + offset], centre)
+    return jnp.where(opened, shifted(centre, which_axis, offset), centre)
+
+
+def rows_of(masks, lo, hi):
+    rows = masks[0]
+    return [(rows[0][lo:hi], rows[1][lo:hi])] + list(masks[1:])
+
+
+def relax_rows(values, coeffs, masks, lo, hi, at):
+    opened = rows_of(masks, lo, hi)
+    centre = values[lo - at : hi - at]
+    change = jnp.zeros_like(centre)
     for which_axis in range(3):
         kk = coeffs[which_axis]
-        up_open, down_open = masks[which_axis]
-        for offset, opened in ((1, up_open), (-1, down_open)):
-            change = change + 0.5 * (kk + neighbor(kk, which_axis, offset, opened)) * (
-                neighbor(values, which_axis, offset, opened) - values
+        k_centre = kk[lo - at : hi - at]
+        up_open, down_open = opened[which_axis]
+        for offset, mask in ((1, up_open), (-1, down_open)):
+            change = change + 0.5 * (k_centre + near(kk, lo, hi, at, which_axis, offset, mask)) * (
+                near(values, lo, hi, at, which_axis, offset, mask) - centre
             )
-    return values + step_size * change
+    return centre + step_size * change
 
 
 def attributes(grown, masks):
@@ -216,9 +231,13 @@
     grown = diffusion_rows(wide, width, cols)
     masks = face_masks(width, rows, cols, samples, h, cols)
     values, coeffs_grown = grown[0], grown[1:]
+    n_rows = values.shape[0]
+    at = 0
     for repeat in range(STEPS):
-        values = relax_step(values, coeffs_grown, masks)
-    smooth = values[h : h + rows, cols - h : 2 * cols + h]
+        lo, hi = repeat + 1, n_rows - repeat - 1
+        values = relax_rows(values, coeffs_grown[:, lo - 1 :], masks, lo, hi, at)
+        at = lo
+    smooth = values[h - at : h - at + rows, cols - h : 2 * cols + h]
 
     grown = with_rows(smooth, width, h)
     masks = face_masks(width, rows, cols, samples, h, h)

time: 51.9 us -> 51.1 us (0.985)
  other arithmetic: 7.84 us -> 7.01 us
    add x2, other arithmetic: 2.36 us -> 1.54 us  [relax_rows(): return centre + step_size * change]
  transfers between devices with their start and end apart: 6 -> 6, of which waited for: 4 -> 4; matrix products, arithmetic and copies ran while one was open for 3% -> 4% of each run, Pallas kernels for 0% -> 0%
where the time goes in v10:
time: 51.1 us; the launch traced here: 50.8 us
  starting transfers between devices  26 us (51%)
  waiting for transfers between devices  9.32 us (18%)
  other arithmetic  7.01 us (14%)
  local copies, waits for them, and re-layouts  4.67 us (9%)
  between operations  3.83 us (7%)
    ppermute x4, starting transfers between devices, moved(): return lax.ppermute(value, 'inline', pairs)  22 us
    ppermute x4, waiting for transfers between devices, moved(): return lax.ppermute(value, 'inline', pairs)  5.37 us
    ppermute x2, waiting for transfers between devices, moved(): return lax.ppermute(value, 'xline', pairs)  3.96 us
    ppermute x2, starting transfers between devices, moved(): return lax.ppermute(value, 'xline', pairs)  3.95 us
    dynamic_slice x2, local copies, waits for them, and re-layouts, on_device(): field = lax.dynamic_index_in_dim(survey, batch, 0, keepdims=False)  1.73 us
    add x2, other arithmetic, relax_rows(): return centre + step_size * change  1.54 us
    mul x4, other arithmetic, attributes(): 0.25 * (neighbor(member, which_axis, 1, up_open) + 2.0 * member + neighbo...  1.37 us
  transfers between devices with their start and end apart: 6, of which 4 were waited for; matrix products, arithmetic and copies ran while one was open for 4% of the time, Pallas kernels for 0%

profile of v10, /device:TPU:30, one launch (start us, length us, event | category | flops | bytes accessed | tf_op | source)
XLA Modules:
  0.0 50.8 jit_solution(3308892013042556906)
XLA Ops:
  0.7 0.9 %constant_dynamic-slice_fusion.2 = f32[1,4,4,1024]{3,2,1,0:T(4,128)S(1)} fusion(f32[2,4,4,1024]{3,2,1,0:T(4,128)} %param.3, s32[]{:T(128)S(6)} %select_n.234), kind=kLoop, calls=%fused_computation.309 | loop fusion | bytes 131076 | tf_op jit(solution)/shard_map/jit(dynamic_index_in_dim)/dynamic_slice | solution.py:224
  1.5 0.8 %fusion.177 = f32[1,4,4,1024]{3,2,0,1:T(4,128)S(1)} fusion(f32[2,4,4,1024]{3,2,1,0:T(4,128)} %param.3, s32[]{:T(128)S(6)} %select_n.234), kind=kLoop, calls=%fused_computation.325 | loop fusion | bytes 131076 | tf_op jit(solution)/shard_map/jit(dynamic_index_in_dim)/dynamic_slice | solution.py:224
  2.5 0.2 fusion.150
  2.7 0.1 fusion.20
  2.8 0.1 reshape.121
  3.0 2.7 %collective-permute-start.1 = (f32[56,1024]{1,0:T(8,128)S(1)}, f32[56,1024]{1,0:T(8,128)S(1)}, u32[]{:S(2)}, u32[]{:S(2)}) collective-permute-start(f32[56,1024]{1,0:T(8,128)S(1)} %pad_maximum_fusion.2), channel_id=1, source_target_pairs={{1,0},{2,1},{3,2},{5,4},{6,5},{7,6},{9,8},{10,9},{11,10},{13,12},{... | collective-permute-start | bytes 688136 | tf_op jit(solution)/shard_map/ppermute | solution.py:38
  5.7 0.1 reshape.119
  5.8 1.3 %collective-permute-start = (f32[56,1024]{1,0:T(8,128)S(1)}, f32[56,1024]{1,0:T(8,128)S(1)}, u32[]{:S(2)}, u32[]{:S(2)}) collective-permute-start(f32[56,1024]{1,0:T(8,128)S(1)} %pad_maximum_fusion.1), channel_id=1, source_target_pairs={{0,1},{1,2},{2,3},{4,5},{5,6},{6,7},{8,9},{9,10},{10,11},{12,13},{... | collective-permute-start | bytes 688136 | tf_op jit(solution)/shard_map/ppermute | solution.py:38
  7.2 0.6 %constant_dynamic-slice_fusion.3 = s32[1,1]{0,1:T(1,128)} fusion(s32[2,1]{0,1:T(1,128)S(1)} %copy-done.1, s32[]{:T(128)S(6)} %select_n.234), kind=kLoop, calls=%fused_computation.310 | loop fusion | bytes 12 | tf_op jit(solution)/shard_map/jit(dynamic_index_in_dim)/dynamic_slice | solution.py:226
  10.8 4.0 %collective-permute-done = f32[56,1024]{1,0:T(8,128)S(1)} collective-permute-done((f32[56,1024]{1,0:T(8,128)S(1)}, f32[56,1024]{1,0:T(8,128)S(1)}, u32[]{:S(2)}, u32[]{:S(2)}) %collective-permute-start) | collective-permute-done | bytes 229408 | tf_op jit(solution)/shard_map/ppermute | solution.py:38
  15.3 0.7 %concatenate.33 = f32[4,4,12,1024]{3,2,0,1:T(8,128)S(1)} concatenate(f32[4,4,1,1024]{3,2,0,1:T(1,128)S(1)} %copy.19, f32[4,4,3,1024]{3,2,0,1:T(4,128)S(1)} %copy.20, f32[4,4,4,1024]{3,2,0,1:T(4,128)S(1)} %pad_maximum_fusion, f32[4,4,3,1024]{3,2,0,1:T(4,128)S(1)} %copy.21, f32[4,4,1,1024]{3,2,0,1:T(1,128)S(1)} %copy.22), dimensions={2} | concatenate | bytes 1572864 | tf_op jit(solution)/shard_map/concatenate | solution.py:101
  16.3 3.8 %collective-permute-start.2 = (f32[54,1024]{1,0:T(8,128)S(1)}, f32[54,1024]{1,0:T(8,128)S(1)}, u32[]{:S(2)}, u32[]{:S(2)}) collective-permute-start(f32[54,1024]{1,0:T(8,128)S(1)} %pad_maximum_fusion.3), channel_id=1, source_target_pairs={{0,4},{4,8},{8,12},{12,16},{16,20},{20,24},{24,28},{28,32},{32,36}... | collective-permute-start | bytes 663560 | tf_op jit(solution)/shard_map/ppermute | solution.py:35
  20.2 9.8 %collective-permute-start.3 = (f32[54,1024]{1,0:T(8,128)S(1)}, f32[54,1024]{1,0:T(8,128)S(1)}, u32[]{:S(2)}, u32[]{:S(2)}) collective-permute-start(f32[54,1024]{1,0:T(8,128)S(1)} %pad_maximum_fusion.4), channel_id=1, source_target_pairs={{4,0},{8,4},{12,8},{16,12},{20,16},{24,20},{28,24},{32,28},{36,32}... | collective-permute-start | bytes 663560 | tf_op jit(solution)/shard_map/ppermute | solution.py:35
  30.0 2.4 %collective-permute-done.2 = f32[54,1024]{1,0:T(8,128)S(1)} collective-permute-done((f32[54,1024]{1,0:T(8,128)S(1)}, f32[54,1024]{1,0:T(8,128)S(1)}, u32[]{:S(2)}, u32[]{:S(2)}) %collective-permute-start.2) | collective-permute-done | bytes 221216 | tf_op jit(solution)/shard_map/ppermute | solution.py:35
  32.4 1.2 %collective-permute-done.3 = f32[54,1024]{1,0:T(8,128)S(1)} collective-permute-done((f32[54,1024]{1,0:T(8,128)S(1)}, f32[54,1024]{1,0:T(8,128)S(1)}, u32[]{:S(2)}, u32[]{:S(2)}) %collective-permute-start.3) | collective-permute-done | bytes 221216 | tf_op jit(solution)/shard_map/ppermute | solution.py:35
  33.7 0.3 maximum_maximum_fusion
  34.2 0.1 slice_bitcast_fusion
  34.3 0.9 %fusion.8 = f32[6,12,1024]{2,1,0:T(8,128)S(1)} fusion(f32[6,12,1024]{2,1,0:T(8,128)S(1)} %get-tuple-element.43, f32[6,12,1024]{2,1,0:T(8,128)S(1)} %get-tuple-element.42, f32[6,12,1024]{2,1,0:T(8,128)S(1)} %get-tuple-element.41, f32[4,8,12,1024]{3,2,0,1:T(8,128)S(1)} %maximum_dynamic-update-slice_fusion, pred[12]{0:T(512)(128)(4,1)S(1)} %get-tuple-element.88, ...), kind=kLoop, calls=%fused_computation.43 | loop fusion | flops 3170304 | bytes 2656292 | tf_op jit(solution)/shard_map/add | solution.py:176
  35.3 0.6 %fusion.92 = f32[4,12,1024]{2,1,0:T(8,128)S(1)} fusion(f32[4,12,1024]{2,1,0:T(8,128)S(1)} %slice.609, f32[4,12,1024]{2,1,0:T(8,128)S(1)} %get-tuple-element.40, f32[4,12,1024]{2,1,0:T(8,128)S(1)} %get-tuple-element.39, f32[6,12,1024]{2,1,0:T(8,128)S(1)} %fusion.8, f32[4,8,12,1024]{3,2,0,1:T(8,128)S(1)} %maximum_dynamic-update-slice_fusion, ...), kind=kLoop, calls=%fused_computation.181 | loop fusion | flops 2113536 | bytes 1771552 | tf_op jit(solution)/shard_map/add | solution.py:176
  36.0 1.9 %collective-permute-start.4 = (f32[2,8,1024]{2,1,0:T(8,128)S(1)}, f32[2,8,1024]{2,1,0:T(8,128)S(1)}, u32[]{:S(2)}, u32[]{:S(2)}) collective-permute-start(f32[2,8,1024]{2,1,0:T(8,128)S(1)} %constant_dynamic-slice_fusion), channel_id=1, source_target_pairs={{0,4},{4,8},{8,12},{12,16},{16,20},{20,24},{24,28},{28,32},{32,36}... | collective-permute-start | bytes 196616 | tf_op jit(solution)/shard_map/ppermute | solution.py:35
  37.9 0.7 %iota_compare_fusion.4 = pred[4]{0:T(512)(128)(4,1)S(1)} fusion(s32[]{:T(128)} %bitcast), kind=kLoop, calls=%fused_computation.319 | loop fusion | flops 4 | bytes 8 | tf_op jit(solution)/shard_map/lt | solution.py:228
  38.6 6.5 %collective-permute-start.5 = (f32[2,8,1024]{2,1,0:T(8,128)S(1)}, f32[2,8,1024]{2,1,0:T(8,128)S(1)}, u32[]{:S(2)}, u32[]{:S(2)}) collective-permute-start(f32[2,8,1024]{2,1,0:T(8,128)S(1)} %slice.618), channel_id=1, source_target_pairs={{4,0},{8,4},{12,8},{16,12},{20,16},{24,20},{28,24},{32,28},{36,32}... | collective-permute-start | bytes 196616 | tf_op jit(solution)/shard_map/ppermute | solution.py:35
  45.2 1.8 %collective-permute-done.5 = f32[2,8,1024]{2,1,0:T(8,128)S(1)} collective-permute-done((f32[2,8,1024]{2,1,0:T(8,128)S(1)}, f32[2,8,1024]{2,1,0:T(8,128)S(1)}, u32[]{:S(2)}, u32[]{:S(2)}) %collective-permute-start.5) | collective-permute-done | bytes 65568 | tf_op jit(solution)/shard_map/ppermute | solution.py:35
  47.0 0.2 fusion.153
  47.2 0.2 fusion.152
  47.5 0.2 broadcast_multiply_fusion.1
  47.6 0.5 broadcast_multiply_fusion.3
  48.1 0.3 broadcast_multiply_fusion
  48.4 0.4 broadcast_multiply_fusion.2
  48.9 0.3 fusion.74
  49.2 0.7 %fusion.51 = (f32[8,8,1024]{2,1,0:T(8,128)S(1)}, f32[8,8,1024]{2,1,0:T(8,128)S(1)}, f32[8,8,1024]{2,1,0:T(8,128)S(1)}, f32[8,8,1024]{2,1,0:T(8,128)S(1)}) fusion(f32[8,8,1024]{2,1,0:T(8,128)S(1)} %get-tuple-element.66, f32[8,8,1024]{2,1,0:T(8,128)S(1)} %get-tuple-element.67, pred[1024]{0:T(1024)(128)(4,1)S(1)} %get-tuple-element.86, ...), kind=kLoop, calls=%fused_computation.140 | loop fusion | flops 1900544 | bytes 3147776 | tf_op jit(solution)/shard_map/add | solution.py:209
  49.9 0.9 %fusion.138 = (f32[1,4,4,1024]{3,2,1,0:T(4,128)}, f32[1,4,4,1024]{3,2,1,0:T(4,128)}) fusion(f32[8,8,1024]{2,1,0:T(8,128)S(1)} %get-tuple-element.49, f32[8,8,1024]{2,1,0:T(8,128)S(1)} %get-tuple-element.51, f32[8,8,1024]{2,1,0:T(8,128)S(1)} %get-tuple-element.13, f32[8,8,1024]{2,1,0:T(8,128)S(1)} %get-tuple-element.14, ...), kind=kLoop, calls=%fused_computation.267 | loop fusion | flops 393216 | bytes 983044 | tf_op jit(solution)/shard_map/broadcast_in_dim | solution.py:245
  (67 shorter events, 1.9 us)
Async XLA Ops:
  0.6 1.8 %copy-start = (bf16[3,2,4,4,1024]{4,3,2,1,0:T(4,128)(2,1)S(1)}, bf16[3,2,4,4,1024]{4,3,2,1,0:T(4,128)(2,1)}, u32[]{:S(2)}) copy-start(bf16[3,2,4,4,1024]{4,3,2,1,0:T(4,128)(2,1)} %param.4) | copy-start | bytes 589828
  2.4 4.7 %copy-start.1 = (s32[2,1]{0,1:T(1,128)S(1)}, s32[2,1]{0,1:T(1,128)}, u32[]{:S(2)}) copy-start(s32[2,1]{0,1:T(1,128)} %param.5) | copy-start | bytes 28
  3.0 7.9 %collective-permute-start.1 = (f32[56,1024]{1,0:T(8,128)S(1)}, f32[56,1024]{1,0:T(8,128)S(1)}, u32[]{:S(2)}, u32[]{:S(2)}) collective-permute-start(f32[56,1024]{1,0:T(8,128)S(1)} %pad_maximum_fusion.2), channel_id=1, source_target_pairs={{1,0},{2,1},{3,2},{5,4},{6,5},{7,6},{9,8},{10,9},{11,10},{13,12},{... | collective-permute-start | bytes 688136 | tf_op jit(solution)/shard_map/ppermute | solution.py:38
  5.8 9.0 %collective-permute-start = (f32[56,1024]{1,0:T(8,128)S(1)}, f32[56,1024]{1,0:T(8,128)S(1)}, u32[]{:S(2)}, u32[]{:S(2)}) collective-permute-start(f32[56,1024]{1,0:T(8,128)S(1)} %pad_maximum_fusion.1), channel_id=1, source_target_pairs={{0,1},{1,2},{2,3},{4,5},{5,6},{6,7},{8,9},{9,10},{10,11},{12,13},{... | collective-permute-start | bytes 688136 | tf_op jit(solution)/shard_map/ppermute | solution.py:38
  16.3 16.1 %collective-permute-start.2 = (f32[54,1024]{1,0:T(8,128)S(1)}, f32[54,1024]{1,0:T(8,128)S(1)}, u32[]{:S(2)}, u32[]{:S(2)}) collective-permute-start(f32[54,1024]{1,0:T(8,128)S(1)} %pad_maximum_fusion.3), channel_id=1, source_target_pairs={{0,4},{4,8},{8,12},{12,16},{16,20},{20,24},{24,28},{28,32},{32,36}... | collective-permute-start | bytes 663560 | tf_op jit(solution)/shard_map/ppermute | solution.py:35
  20.2 13.4 %collective-permute-start.3 = (f32[54,1024]{1,0:T(8,128)S(1)}, f32[54,1024]{1,0:T(8,128)S(1)}, u32[]{:S(2)}, u32[]{:S(2)}) collective-permute-start(f32[54,1024]{1,0:T(8,128)S(1)} %pad_maximum_fusion.4), channel_id=1, source_target_pairs={{4,0},{8,4},{12,8},{16,12},{20,16},{24,20},{28,24},{32,28},{36,32}... | collective-permute-start | bytes 663560 | tf_op jit(solution)/shard_map/ppermute | solution.py:35
  36.0 9.1 %collective-permute-start.4 = (f32[2,8,1024]{2,1,0:T(8,128)S(1)}, f32[2,8,1024]{2,1,0:T(8,128)S(1)}, u32[]{:S(2)}, u32[]{:S(2)}) collective-permute-start(f32[2,8,1024]{2,1,0:T(8,128)S(1)} %constant_dynamic-slice_fusion), channel_id=1, source_target_pairs={{0,4},{4,8},{8,12},{12,16},{16,20},{20,24},{24,28},{28,32},{32,36}... | collective-permute-start | bytes 196616 | tf_op jit(solution)/shard_map/ppermute | solution.py:35
  38.6 8.4 %collective-permute-start.5 = (f32[2,8,1024]{2,1,0:T(8,128)S(1)}, f32[2,8,1024]{2,1,0:T(8,128)S(1)}, u32[]{:S(2)}, u32[]{:S(2)}) collective-permute-start(f32[2,8,1024]{2,1,0:T(8,128)S(1)} %slice.618), channel_id=1, source_target_pairs={{4,0},{8,4},{12,8},{16,12},{20,16},{24,20},{28,24},{32,28},{36,32}... | collective-permute-start | bytes 196616 | tf_op jit(solution)/shard_map/ppermute | solution.py:35

commit v11 on v10

--- a/solution.py
+++ b/solution.py
@@ -221,7 +221,7 @@
 def on_device(survey, conduct, widths):
     h = HALO
     batch = lax.axis_index("segment")
-    field = lax.dynamic_index_in_dim(survey, batch, 0, keepdims=False)
+    field = lax.optimization_barrier(lax.dynamic_index_in_dim(survey, batch, 0, keepdims=False))
     coeffs = lax.dynamic_index_in_dim(conduct, batch, 1, keepdims=False).astype(jnp.float32)
     width = lax.dynamic_index_in_dim(widths[:, 0], batch, 0, keepdims=False)
     rows, cols, samples = field.shape

time: 51.1 us -> 51.2 us (level)
    dynamic_slice x2 -> x0, local copies, waits for them, and re-layouts: 1.73 us -> none  [on_device(): field = lax.dynamic_index_in_dim(survey, batch, 0, keepdims=False)]
    unnamed x4, local copies, waits for them, and re-layouts: 0.02 us -> 0.93 us
    squeeze x0 -> x1, local copies, waits for them, and re-layouts: none -> 0.85 us  [on_device(): lax.dynamic_index_in_dim(survey, batch, 0, keepdims=False)]
where the time goes in v11:
time: 51.2 us; the launch traced here: 50.8 us
  starting transfers between devices  26 us (51%)
  waiting for transfers between devices  9.32 us (18%)
  other arithmetic  7 us (14%)
  local copies, waits for them, and re-layouts  4.7 us (9%)
  between operations  3.82 us (7%)
    ppermute x4, starting transfers between devices, moved(): return lax.ppermute(value, 'inline', pairs)  22 us
    ppermute x4, waiting for transfers between devices, moved(): return lax.ppermute(value, 'inline', pairs)  5.37 us
    ppermute x2, waiting for transfers between devices, moved(): return lax.ppermute(value, 'xline', pairs)  3.96 us
    ppermute x2, starting transfers between devices, moved(): return lax.ppermute(value, 'xline', pairs)  3.95 us
    add x2, other arithmetic, relax_rows(): return centre + step_size * change  1.54 us
    mul x4, other arithmetic, attributes(): 0.25 * (neighbor(member, which_axis, 1, up_open) + 2.0 * member + neighbo...  1.37 us
  transfers between devices with their start and end apart: 6, of which 4 were waited for; matrix products, arithmetic and copies ran while one was open for 4% of the time, Pallas kernels for 0%

profile of v11, /device:TPU:30, one launch (start us, length us, event | category | flops | bytes accessed | tf_op | source)
XLA Modules:
  0.0 50.8 jit_solution(9407934263251223107)
XLA Ops:
  0.7 0.9 %copy-done = bf16[3,2,4,4,1024]{4,3,2,1,0:T(4,128)(2,1)S(1)} copy-done((bf16[3,2,4,4,1024]{4,3,2,1,0:T(4,128)(2,1)S(1)}, bf16[3,2,4,4,1024]{4,3,2,1,0:T(4,128)(2,1)}, u32[]{:S(2)}) %copy-start) | copy-done | bytes 196632
  1.6 0.9 %dynamic-slice_bitcast_fusion.2 = f32[4,4,1024]{2,1,0:T(4,128)S(1)} fusion(f32[2,4,4,1024]{3,2,1,0:T(4,128)} %param.3, s32[]{:T(128)S(6)} %select_n.234), kind=kLoop, calls=%fused_computation.292 | loop fusion | bytes 131076 | tf_op jit(solution)/shard_map/jit(dynamic_index_in_dim)/squeeze | solution.py:224
  2.5 0.2 fusion.150
  2.7 0.1 fusion.20
  2.8 0.1 reshape.121
  3.0 2.7 %collective-permute-start.1 = (f32[56,1024]{1,0:T(8,128)S(1)}, f32[56,1024]{1,0:T(8,128)S(1)}, u32[]{:S(2)}, u32[]{:S(2)}) collective-permute-start(f32[56,1024]{1,0:T(8,128)S(1)} %pad_maximum_fusion.2), channel_id=1, source_target_pairs={{1,0},{2,1},{3,2},{5,4},{6,5},{7,6},{9,8},{10,9},{11,10},{13,12},{... | collective-permute-start | bytes 688136 | tf_op jit(solution)/shard_map/ppermute | solution.py:38
  5.7 0.1 reshape.119
  5.9 1.3 %collective-permute-start = (f32[56,1024]{1,0:T(8,128)S(1)}, f32[56,1024]{1,0:T(8,128)S(1)}, u32[]{:S(2)}, u32[]{:S(2)}) collective-permute-start(f32[56,1024]{1,0:T(8,128)S(1)} %pad_maximum_fusion.1), channel_id=1, source_target_pairs={{0,1},{1,2},{2,3},{4,5},{5,6},{6,7},{8,9},{9,10},{10,11},{12,13},{... | collective-permute-start | bytes 688136 | tf_op jit(solution)/shard_map/ppermute | solution.py:38
  7.2 0.6 %constant_dynamic-slice_fusion.2 = s32[1,1]{0,1:T(1,128)} fusion(s32[2,1]{0,1:T(1,128)S(1)} %copy-done.1, s32[]{:T(128)S(6)} %select_n.234), kind=kLoop, calls=%fused_computation.310 | loop fusion | bytes 12 | tf_op jit(solution)/shard_map/jit(dynamic_index_in_dim)/dynamic_slice | solution.py:226
  10.9 4.0 %collective-permute-done = f32[56,1024]{1,0:T(8,128)S(1)} collective-permute-done((f32[56,1024]{1,0:T(8,128)S(1)}, f32[56,1024]{1,0:T(8,128)S(1)}, u32[]{:S(2)}, u32[]{:S(2)}) %collective-permute-start) | collective-permute-done | bytes 229408 | tf_op jit(solution)/shard_map/ppermute | solution.py:38
  15.4 0.7 %concatenate.33 = f32[4,4,12,1024]{3,2,0,1:T(8,128)S(1)} concatenate(f32[4,4,1,1024]{3,2,0,1:T(1,128)S(1)} %copy.19, f32[4,4,3,1024]{3,2,0,1:T(4,128)S(1)} %copy.20, f32[4,4,4,1024]{3,2,0,1:T(4,128)S(1)} %pad_maximum_fusion, f32[4,4,3,1024]{3,2,0,1:T(4,128)S(1)} %copy.21, f32[4,4,1,1024]{3,2,0,1:T(1,128)S(1)} %copy.22), dimensions={2} | concatenate | bytes 1572864 | tf_op jit(solution)/shard_map/concatenate | solution.py:101
  16.3 3.8 %collective-permute-start.2 = (f32[54,1024]{1,0:T(8,128)S(1)}, f32[54,1024]{1,0:T(8,128)S(1)}, u32[]{:S(2)}, u32[]{:S(2)}) collective-permute-start(f32[54,1024]{1,0:T(8,128)S(1)} %pad_maximum_fusion.3), channel_id=1, source_target_pairs={{0,4},{4,8},{8,12},{12,16},{16,20},{20,24},{24,28},{28,32},{32,36}... | collective-permute-start | bytes 663560 | tf_op jit(solution)/shard_map/ppermute | solution.py:35
  20.2 9.8 %collective-permute-start.3 = (f32[54,1024]{1,0:T(8,128)S(1)}, f32[54,1024]{1,0:T(8,128)S(1)}, u32[]{:S(2)}, u32[]{:S(2)}) collective-permute-start(f32[54,1024]{1,0:T(8,128)S(1)} %pad_maximum_fusion.4), channel_id=1, source_target_pairs={{4,0},{8,4},{12,8},{16,12},{20,16},{24,20},{28,24},{32,28},{36,32}... | collective-permute-start | bytes 663560 | tf_op jit(solution)/shard_map/ppermute | solution.py:35
  30.0 2.4 %collective-permute-done.2 = f32[54,1024]{1,0:T(8,128)S(1)} collective-permute-done((f32[54,1024]{1,0:T(8,128)S(1)}, f32[54,1024]{1,0:T(8,128)S(1)}, u32[]{:S(2)}, u32[]{:S(2)}) %collective-permute-start.2) | collective-permute-done | bytes 221216 | tf_op jit(solution)/shard_map/ppermute | solution.py:35
  32.4 1.2 %collective-permute-done.3 = f32[54,1024]{1,0:T(8,128)S(1)} collective-permute-done((f32[54,1024]{1,0:T(8,128)S(1)}, f32[54,1024]{1,0:T(8,128)S(1)}, u32[]{:S(2)}, u32[]{:S(2)}) %collective-permute-start.3) | collective-permute-done | bytes 221216 | tf_op jit(solution)/shard_map/ppermute | solution.py:35
  33.7 0.3 maximum_maximum_fusion
  34.2 0.1 slice_bitcast_fusion
  34.4 0.9 %fusion.8 = f32[6,12,1024]{2,1,0:T(8,128)S(1)} fusion(f32[6,12,1024]{2,1,0:T(8,128)S(1)} %get-tuple-element.43, f32[6,12,1024]{2,1,0:T(8,128)S(1)} %get-tuple-element.42, f32[6,12,1024]{2,1,0:T(8,128)S(1)} %get-tuple-element.41, f32[4,8,12,1024]{3,2,0,1:T(8,128)S(1)} %maximum_dynamic-update-slice_fusion, pred[12]{0:T(512)(128)(4,1)S(1)} %get-tuple-element.88, ...), kind=kLoop, calls=%fused_computation.43 | loop fusion | flops 3170304 | bytes 2656292 | tf_op jit(solution)/shard_map/add | solution.py:176
  35.3 0.6 %fusion.92 = f32[4,12,1024]{2,1,0:T(8,128)S(1)} fusion(f32[4,12,1024]{2,1,0:T(8,128)S(1)} %slice.609, f32[4,12,1024]{2,1,0:T(8,128)S(1)} %get-tuple-element.40, f32[4,12,1024]{2,1,0:T(8,128)S(1)} %get-tuple-element.39, f32[6,12,1024]{2,1,0:T(8,128)S(1)} %fusion.8, f32[4,8,12,1024]{3,2,0,1:T(8,128)S(1)} %maximum_dynamic-update-slice_fusion, ...), kind=kLoop, calls=%fused_computation.181 | loop fusion | flops 2113536 | bytes 1771552 | tf_op jit(solution)/shard_map/add | solution.py:176
  36.0 1.9 %collective-permute-start.4 = (f32[2,8,1024]{2,1,0:T(8,128)S(1)}, f32[2,8,1024]{2,1,0:T(8,128)S(1)}, u32[]{:S(2)}, u32[]{:S(2)}) collective-permute-start(f32[2,8,1024]{2,1,0:T(8,128)S(1)} %constant_dynamic-slice_fusion), channel_id=1, source_target_pairs={{0,4},{4,8},{8,12},{12,16},{16,20},{20,24},{24,28},{28,32},{32,36}... | collective-permute-start | bytes 196616 | tf_op jit(solution)/shard_map/ppermute | solution.py:35
  37.9 0.7 %iota_compare_fusion.4 = pred[4]{0:T(512)(128)(4,1)S(1)} fusion(s32[]{:T(128)} %bitcast), kind=kLoop, calls=%fused_computation.319 | loop fusion | flops 4 | bytes 8 | tf_op jit(solution)/shard_map/lt | solution.py:228
  38.6 6.5 %collective-permute-start.5 = (f32[2,8,1024]{2,1,0:T(8,128)S(1)}, f32[2,8,1024]{2,1,0:T(8,128)S(1)}, u32[]{:S(2)}, u32[]{:S(2)}) collective-permute-start(f32[2,8,1024]{2,1,0:T(8,128)S(1)} %slice.618), channel_id=1, source_target_pairs={{4,0},{8,4},{12,8},{16,12},{20,16},{24,20},{28,24},{32,28},{36,32}... | collective-permute-start | bytes 196616 | tf_op jit(solution)/shard_map/ppermute | solution.py:35
  45.2 1.8 %collective-permute-done.5 = f32[2,8,1024]{2,1,0:T(8,128)S(1)} collective-permute-done((f32[2,8,1024]{2,1,0:T(8,128)S(1)}, f32[2,8,1024]{2,1,0:T(8,128)S(1)}, u32[]{:S(2)}, u32[]{:S(2)}) %collective-permute-start.5) | collective-permute-done | bytes 65568 | tf_op jit(solution)/shard_map/ppermute | solution.py:35
  47.0 0.2 fusion.153
  47.2 0.2 fusion.152
  47.5 0.2 broadcast_multiply_fusion.1
  47.6 0.5 broadcast_multiply_fusion.3
  48.2 0.3 broadcast_multiply_fusion
  48.4 0.4 broadcast_multiply_fusion.2
  48.9 0.3 fusion.74
  49.2 0.7 %fusion.51 = (f32[8,8,1024]{2,1,0:T(8,128)S(1)}, f32[8,8,1024]{2,1,0:T(8,128)S(1)}, f32[8,8,1024]{2,1,0:T(8,128)S(1)}, f32[8,8,1024]{2,1,0:T(8,128)S(1)}) fusion(f32[8,8,1024]{2,1,0:T(8,128)S(1)} %get-tuple-element.66, f32[8,8,1024]{2,1,0:T(8,128)S(1)} %get-tuple-element.67, pred[1024]{0:T(1024)(128)(4,1)S(1)} %get-tuple-element.86, ...), kind=kLoop, calls=%fused_computation.140 | loop fusion | flops 1900544 | bytes 3147776 | tf_op jit(solution)/shard_map/add | solution.py:209
  49.9 0.9 %fusion.138 = (f32[1,4,4,1024]{3,2,1,0:T(4,128)}, f32[1,4,4,1024]{3,2,1,0:T(4,128)}) fusion(f32[8,8,1024]{2,1,0:T(8,128)S(1)} %get-tuple-element.49, f32[8,8,1024]{2,1,0:T(8,128)S(1)} %get-tuple-element.51, f32[8,8,1024]{2,1,0:T(8,128)S(1)} %get-tuple-element.13, f32[8,8,1024]{2,1,0:T(8,128)S(1)} %get-tuple-element.14, ...), kind=kLoop, calls=%fused_computation.267 | loop fusion | flops 393216 | bytes 983044 | tf_op jit(solution)/shard_map/broadcast_in_dim | solution.py:245
  (66 shorter events, 1.9 us)
Async XLA Ops:
  0.6 0.9 %copy-start = (bf16[3,2,4,4,1024]{4,3,2,1,0:T(4,128)(2,1)S(1)}, bf16[3,2,4,4,1024]{4,3,2,1,0:T(4,128)(2,1)}, u32[]{:S(2)}) copy-start(bf16[3,2,4,4,1024]{4,3,2,1,0:T(4,128)(2,1)} %param.4) | copy-start | bytes 589828
  1.6 5.6 %copy-start.1 = (s32[2,1]{0,1:T(1,128)S(1)}, s32[2,1]{0,1:T(1,128)}, u32[]{:S(2)}) copy-start(s32[2,1]{0,1:T(1,128)} %param.5) | copy-start | bytes 28
  3.0 7.9 %collective-permute-start.1 = (f32[56,1024]{1,0:T(8,128)S(1)}, f32[56,1024]{1,0:T(8,128)S(1)}, u32[]{:S(2)}, u32[]{:S(2)}) collective-permute-start(f32[56,1024]{1,0:T(8,128)S(1)} %pad_maximum_fusion.2), channel_id=1, source_target_pairs={{1,0},{2,1},{3,2},{5,4},{6,5},{7,6},{9,8},{10,9},{11,10},{13,12},{... | collective-permute-start | bytes 688136 | tf_op jit(solution)/shard_map/ppermute | solution.py:38
  5.9 9.0 %collective-permute-start = (f32[56,1024]{1,0:T(8,128)S(1)}, f32[56,1024]{1,0:T(8,128)S(1)}, u32[]{:S(2)}, u32[]{:S(2)}) collective-permute-start(f32[56,1024]{1,0:T(8,128)S(1)} %pad_maximum_fusion.1), channel_id=1, source_target_pairs={{0,1},{1,2},{2,3},{4,5},{5,6},{6,7},{8,9},{9,10},{10,11},{12,13},{... | collective-permute-start | bytes 688136 | tf_op jit(solution)/shard_map/ppermute | solution.py:38
  16.3 16.1 %collective-permute-start.2 = (f32[54,1024]{1,0:T(8,128)S(1)}, f32[54,1024]{1,0:T(8,128)S(1)}, u32[]{:S(2)}, u32[]{:S(2)}) collective-permute-start(f32[54,1024]{1,0:T(8,128)S(1)} %pad_maximum_fusion.3), channel_id=1, source_target_pairs={{0,4},{4,8},{8,12},{12,16},{16,20},{20,24},{24,28},{28,32},{32,36}... | collective-permute-start | bytes 663560 | tf_op jit(solution)/shard_map/ppermute | solution.py:35
  20.2 13.4 %collective-permute-start.3 = (f32[54,1024]{1,0:T(8,128)S(1)}, f32[54,1024]{1,0:T(8,128)S(1)}, u32[]{:S(2)}, u32[]{:S(2)}) collective-permute-start(f32[54,1024]{1,0:T(8,128)S(1)} %pad_maximum_fusion.4), channel_id=1, source_target_pairs={{4,0},{8,4},{12,8},{16,12},{20,16},{24,20},{28,24},{32,28},{36,32}... | collective-permute-start | bytes 663560 | tf_op jit(solution)/shard_map/ppermute | solution.py:35
  36.0 9.1 %collective-permute-start.4 = (f32[2,8,1024]{2,1,0:T(8,128)S(1)}, f32[2,8,1024]{2,1,0:T(8,128)S(1)}, u32[]{:S(2)}, u32[]{:S(2)}) collective-permute-start(f32[2,8,1024]{2,1,0:T(8,128)S(1)} %constant_dynamic-slice_fusion), channel_id=1, source_target_pairs={{0,4},{4,8},{8,12},{12,16},{16,20},{20,24},{24,28},{28,32},{32,36}... | collective-permute-start | bytes 196616 | tf_op jit(solution)/shard_map/ppermute | solution.py:35
  38.6 8.4 %collective-permute-start.5 = (f32[2,8,1024]{2,1,0:T(8,128)S(1)}, f32[2,8,1024]{2,1,0:T(8,128)S(1)}, u32[]{:S(2)}, u32[]{:S(2)}) collective-permute-start(f32[2,8,1024]{2,1,0:T(8,128)S(1)} %slice.618), channel_id=1, source_target_pairs={{4,0},{8,4},{12,8},{16,12},{20,16},{24,20},{28,24},{32,28},{36,32}... | collective-permute-start | bytes 196616 | tf_op jit(solution)/shard_map/ppermute | solution.py:35

commit v12 on v10

--- a/solution.py
+++ b/solution.py
@@ -214,7 +214,8 @@
         - tensor[5] * tensor[5]
     )
     coherence = 1.0 - 3.0 * minors / (trace * trace + epsilon)
-    curvature = (seconds[0] + seconds[1]) / (1.0 + grads[0] * grads[0] + grads[1] * grads[1]) ** 1.5
+    base = 1.0 + grads[0] * grads[0] + grads[1] * grads[1]
+    curvature = (seconds[0] + seconds[1]) / (base * jnp.sqrt(base))
     return coherence, curvature
 
 

time: 51.1 us -> 51.1 us (level)
  no operation moved by 1% of the time
where the time goes in v12:
time: 51.1 us; the launch traced here: 50.8 us
  starting transfers between devices  26 us (51%)
  waiting for transfers between devices  9.32 us (18%)
  other arithmetic  7 us (14%)
  local copies, waits for them, and re-layouts  4.67 us (9%)
  between operations  3.83 us (7%)
    ppermute x4, starting transfers between devices, moved(): return lax.ppermute(value, 'inline', pairs)  22 us
    ppermute x4, waiting for transfers between devices, moved(): return lax.ppermute(value, 'inline', pairs)  5.37 us
    ppermute x2, waiting for transfers between devices, moved(): return lax.ppermute(value, 'xline', pairs)  3.96 us
    ppermute x2, starting transfers between devices, moved(): return lax.ppermute(value, 'xline', pairs)  3.95 us
    dynamic_slice x2, local copies, waits for them, and re-layouts, on_device(): field = lax.dynamic_index_in_dim(survey, batch, 0, keepdims=False)  1.73 us
    add x2, other arithmetic, relax_rows(): return centre + step_size * change  1.54 us
    mul x4, other arithmetic, attributes(): 0.25 * (neighbor(member, which_axis, 1, up_open) + 2.0 * member + neighbo...  1.37 us
  transfers between devices with their start and end apart: 6, of which 4 were waited for; matrix products, arithmetic and copies ran while one was open for 4% of the time, Pallas kernels for 0%

profile of v12, /device:TPU:30, one launch (start us, length us, event | category | flops | bytes accessed | tf_op | source)
XLA Modules:
  0.0 50.8 jit_solution(15727773547488921244)
XLA Ops:
  0.7 0.9 %constant_dynamic-slice_fusion.2 = f32[1,4,4,1024]{3,2,1,0:T(4,128)S(1)} fusion(f32[2,4,4,1024]{3,2,1,0:T(4,128)} %param.3, s32[]{:T(128)S(6)} %select_n.234), kind=kLoop, calls=%fused_computation.308 | loop fusion | bytes 131076 | tf_op jit(solution)/shard_map/jit(dynamic_index_in_dim)/dynamic_slice | solution.py:225
  1.5 0.8 %fusion.174 = f32[1,4,4,1024]{3,2,0,1:T(4,128)S(1)} fusion(f32[2,4,4,1024]{3,2,1,0:T(4,128)} %param.3, s32[]{:T(128)S(6)} %select_n.234), kind=kLoop, calls=%fused_computation.324 | loop fusion | bytes 131076 | tf_op jit(solution)/shard_map/jit(dynamic_index_in_dim)/dynamic_slice | solution.py:225
  2.5 0.2 fusion.147
  2.7 0.1 fusion.20
  2.8 0.1 reshape.121
  3.0 2.7 %collective-permute-start.1 = (f32[56,1024]{1,0:T(8,128)S(1)}, f32[56,1024]{1,0:T(8,128)S(1)}, u32[]{:S(2)}, u32[]{:S(2)}) collective-permute-start(f32[56,1024]{1,0:T(8,128)S(1)} %pad_maximum_fusion.2), channel_id=1, source_target_pairs={{1,0},{2,1},{3,2},{5,4},{6,5},{7,6},{9,8},{10,9},{11,10},{13,12},{... | collective-permute-start | bytes 688136 | tf_op jit(solution)/shard_map/ppermute | solution.py:38
  5.7 0.1 reshape.119
  5.8 1.3 %collective-permute-start = (f32[56,1024]{1,0:T(8,128)S(1)}, f32[56,1024]{1,0:T(8,128)S(1)}, u32[]{:S(2)}, u32[]{:S(2)}) collective-permute-start(f32[56,1024]{1,0:T(8,128)S(1)} %pad_maximum_fusion.1), channel_id=1, source_target_pairs={{0,1},{1,2},{2,3},{4,5},{5,6},{6,7},{8,9},{9,10},{10,11},{12,13},{... | collective-permute-start | bytes 688136 | tf_op jit(solution)/shard_map/ppermute | solution.py:38
  7.2 0.6 %constant_dynamic-slice_fusion.3 = s32[1,1]{0,1:T(1,128)} fusion(s32[2,1]{0,1:T(1,128)S(1)} %copy-done.1, s32[]{:T(128)S(6)} %select_n.234), kind=kLoop, calls=%fused_computation.309 | loop fusion | bytes 12 | tf_op jit(solution)/shard_map/jit(dynamic_index_in_dim)/dynamic_slice | solution.py:227
  10.8 4.0 %collective-permute-done = f32[56,1024]{1,0:T(8,128)S(1)} collective-permute-done((f32[56,1024]{1,0:T(8,128)S(1)}, f32[56,1024]{1,0:T(8,128)S(1)}, u32[]{:S(2)}, u32[]{:S(2)}) %collective-permute-start) | collective-permute-done | bytes 229408 | tf_op jit(solution)/shard_map/ppermute | solution.py:38
  15.3 0.7 %concatenate.33 = f32[4,4,12,1024]{3,2,0,1:T(8,128)S(1)} concatenate(f32[4,4,1,1024]{3,2,0,1:T(1,128)S(1)} %copy.19, f32[4,4,3,1024]{3,2,0,1:T(4,128)S(1)} %copy.20, f32[4,4,4,1024]{3,2,0,1:T(4,128)S(1)} %pad_maximum_fusion, f32[4,4,3,1024]{3,2,0,1:T(4,128)S(1)} %copy.21, f32[4,4,1,1024]{3,2,0,1:T(1,128)S(1)} %copy.22), dimensions={2} | concatenate | bytes 1572864 | tf_op jit(solution)/shard_map/concatenate | solution.py:101
  16.3 3.8 %collective-permute-start.2 = (f32[54,1024]{1,0:T(8,128)S(1)}, f32[54,1024]{1,0:T(8,128)S(1)}, u32[]{:S(2)}, u32[]{:S(2)}) collective-permute-start(f32[54,1024]{1,0:T(8,128)S(1)} %pad_maximum_fusion.3), channel_id=1, source_target_pairs={{0,4},{4,8},{8,12},{12,16},{16,20},{20,24},{24,28},{28,32},{32,36}... | collective-permute-start | bytes 663560 | tf_op jit(solution)/shard_map/ppermute | solution.py:35
  20.2 9.8 %collective-permute-start.3 = (f32[54,1024]{1,0:T(8,128)S(1)}, f32[54,1024]{1,0:T(8,128)S(1)}, u32[]{:S(2)}, u32[]{:S(2)}) collective-permute-start(f32[54,1024]{1,0:T(8,128)S(1)} %pad_maximum_fusion.4), channel_id=1, source_target_pairs={{4,0},{8,4},{12,8},{16,12},{20,16},{24,20},{28,24},{32,28},{36,32}... | collective-permute-start | bytes 663560 | tf_op jit(solution)/shard_map/ppermute | solution.py:35
  30.0 2.4 %collective-permute-done.2 = f32[54,1024]{1,0:T(8,128)S(1)} collective-permute-done((f32[54,1024]{1,0:T(8,128)S(1)}, f32[54,1024]{1,0:T(8,128)S(1)}, u32[]{:S(2)}, u32[]{:S(2)}) %collective-permute-start.2) | collective-permute-done | bytes 221216 | tf_op jit(solution)/shard_map/ppermute | solution.py:35
  32.4 1.2 %collective-permute-done.3 = f32[54,1024]{1,0:T(8,128)S(1)} collective-permute-done((f32[54,1024]{1,0:T(8,128)S(1)}, f32[54,1024]{1,0:T(8,128)S(1)}, u32[]{:S(2)}, u32[]{:S(2)}) %collective-permute-start.3) | collective-permute-done | bytes 221216 | tf_op jit(solution)/shard_map/ppermute | solution.py:35
  33.7 0.3 maximum_maximum_fusion
  34.2 0.1 slice_bitcast_fusion
  34.3 0.9 %fusion.8 = f32[6,12,1024]{2,1,0:T(8,128)S(1)} fusion(f32[6,12,1024]{2,1,0:T(8,128)S(1)} %get-tuple-element.43, f32[6,12,1024]{2,1,0:T(8,128)S(1)} %get-tuple-element.42, f32[6,12,1024]{2,1,0:T(8,128)S(1)} %get-tuple-element.41, f32[4,8,12,1024]{3,2,0,1:T(8,128)S(1)} %maximum_dynamic-update-slice_fusion, pred[12]{0:T(512)(128)(4,1)S(1)} %get-tuple-element.88, ...), kind=kLoop, calls=%fused_computation.43 | loop fusion | flops 3170304 | bytes 2656292 | tf_op jit(solution)/shard_map/add | solution.py:176
  35.3 0.6 %fusion.92 = f32[4,12,1024]{2,1,0:T(8,128)S(1)} fusion(f32[4,12,1024]{2,1,0:T(8,128)S(1)} %slice.609, f32[4,12,1024]{2,1,0:T(8,128)S(1)} %get-tuple-element.40, f32[4,12,1024]{2,1,0:T(8,128)S(1)} %get-tuple-element.39, f32[6,12,1024]{2,1,0:T(8,128)S(1)} %fusion.8, f32[4,8,12,1024]{3,2,0,1:T(8,128)S(1)} %maximum_dynamic-update-slice_fusion, ...), kind=kLoop, calls=%fused_computation.181 | loop fusion | flops 2113536 | bytes 1771552 | tf_op jit(solution)/shard_map/add | solution.py:176
  36.0 1.9 %collective-permute-start.4 = (f32[2,8,1024]{2,1,0:T(8,128)S(1)}, f32[2,8,1024]{2,1,0:T(8,128)S(1)}, u32[]{:S(2)}, u32[]{:S(2)}) collective-permute-start(f32[2,8,1024]{2,1,0:T(8,128)S(1)} %constant_dynamic-slice_fusion), channel_id=1, source_target_pairs={{0,4},{4,8},{8,12},{12,16},{16,20},{20,24},{24,28},{28,32},{32,36}... | collective-permute-start | bytes 196616 | tf_op jit(solution)/shard_map/ppermute | solution.py:35
  37.9 0.7 %iota_compare_fusion.4 = pred[4]{0:T(512)(128)(4,1)S(1)} fusion(s32[]{:T(128)} %bitcast), kind=kLoop, calls=%fused_computation.318 | loop fusion | flops 4 | bytes 8 | tf_op jit(solution)/shard_map/lt | solution.py:229
  38.6 6.5 %collective-permute-start.5 = (f32[2,8,1024]{2,1,0:T(8,128)S(1)}, f32[2,8,1024]{2,1,0:T(8,128)S(1)}, u32[]{:S(2)}, u32[]{:S(2)}) collective-permute-start(f32[2,8,1024]{2,1,0:T(8,128)S(1)} %slice.618), channel_id=1, source_target_pairs={{4,0},{8,4},{12,8},{16,12},{20,16},{24,20},{28,24},{32,28},{36,32}... | collective-permute-start | bytes 196616 | tf_op jit(solution)/shard_map/ppermute | solution.py:35
  45.2 1.8 %collective-permute-done.5 = f32[2,8,1024]{2,1,0:T(8,128)S(1)} collective-permute-done((f32[2,8,1024]{2,1,0:T(8,128)S(1)}, f32[2,8,1024]{2,1,0:T(8,128)S(1)}, u32[]{:S(2)}, u32[]{:S(2)}) %collective-permute-start.5) | collective-permute-done | bytes 65568 | tf_op jit(solution)/shard_map/ppermute | solution.py:35
  47.0 0.2 fusion.150
  47.2 0.2 fusion.149
  47.5 0.2 broadcast_multiply_fusion.1
  47.6 0.5 broadcast_multiply_fusion.3
  48.1 0.3 broadcast_multiply_fusion
  48.4 0.4 broadcast_multiply_fusion.2
  48.9 0.3 fusion.74
  49.2 0.7 %fusion.51 = (f32[8,8,1024]{2,1,0:T(8,128)S(1)}, f32[8,8,1024]{2,1,0:T(8,128)S(1)}, f32[8,8,1024]{2,1,0:T(8,128)S(1)}, f32[8,8,1024]{2,1,0:T(8,128)S(1)}) fusion(f32[8,8,1024]{2,1,0:T(8,128)S(1)} %get-tuple-element.66, f32[8,8,1024]{2,1,0:T(8,128)S(1)} %get-tuple-element.67, pred[1024]{0:T(1024)(128)(4,1)S(1)} %get-tuple-element.86, ...), kind=kLoop, calls=%fused_computation.140 | loop fusion | flops 1900544 | bytes 3147776 | tf_op jit(solution)/shard_map/add | solution.py:209
  49.9 0.9 %select_bitcast_fusion = (f32[1,4,4,1024]{3,2,1,0:T(4,128)}, f32[1,4,4,1024]{3,2,1,0:T(4,128)}) fusion(f32[8,8,1024]{2,1,0:T(8,128)S(1)} %get-tuple-element.49, f32[8,8,1024]{2,1,0:T(8,128)S(1)} %get-tuple-element.51, f32[8,8,1024]{2,1,0:T(8,128)S(1)} %get-tuple-element.13, f32[8,8,1024]{2,1,0:T(8,128)S(1)} %get-tuple-element.14, ...), kind=kLoop, calls=%fused_computation.289 | loop fusion | flops 409600 | bytes 983044 | tf_op jit(solution)/shard_map/broadcast_in_dim | solution.py:246
  (67 shorter events, 1.9 us)
Async XLA Ops:
  0.6 1.8 %copy-start = (bf16[3,2,4,4,1024]{4,3,2,1,0:T(4,128)(2,1)S(1)}, bf16[3,2,4,4,1024]{4,3,2,1,0:T(4,128)(2,1)}, u32[]{:S(2)}) copy-start(bf16[3,2,4,4,1024]{4,3,2,1,0:T(4,128)(2,1)} %param.4) | copy-start | bytes 589828
  2.4 4.7 %copy-start.1 = (s32[2,1]{0,1:T(1,128)S(1)}, s32[2,1]{0,1:T(1,128)}, u32[]{:S(2)}) copy-start(s32[2,1]{0,1:T(1,128)} %param.5) | copy-start | bytes 28
  3.0 7.9 %collective-permute-start.1 = (f32[56,1024]{1,0:T(8,128)S(1)}, f32[56,1024]{1,0:T(8,128)S(1)}, u32[]{:S(2)}, u32[]{:S(2)}) collective-permute-start(f32[56,1024]{1,0:T(8,128)S(1)} %pad_maximum_fusion.2), channel_id=1, source_target_pairs={{1,0},{2,1},{3,2},{5,4},{6,5},{7,6},{9,8},{10,9},{11,10},{13,12},{... | collective-permute-start | bytes 688136 | tf_op jit(solution)/shard_map/ppermute | solution.py:38
  5.8 9.0 %collective-permute-start = (f32[56,1024]{1,0:T(8,128)S(1)}, f32[56,1024]{1,0:T(8,128)S(1)}, u32[]{:S(2)}, u32[]{:S(2)}) collective-permute-start(f32[56,1024]{1,0:T(8,128)S(1)} %pad_maximum_fusion.1), channel_id=1, source_target_pairs={{0,1},{1,2},{2,3},{4,5},{5,6},{6,7},{8,9},{9,10},{10,11},{12,13},{... | collective-permute-start | bytes 688136 | tf_op jit(solution)/shard_map/ppermute | solution.py:38
  16.3 16.1 %collective-permute-start.2 = (f32[54,1024]{1,0:T(8,128)S(1)}, f32[54,1024]{1,0:T(8,128)S(1)}, u32[]{:S(2)}, u32[]{:S(2)}) collective-permute-start(f32[54,1024]{1,0:T(8,128)S(1)} %pad_maximum_fusion.3), channel_id=1, source_target_pairs={{0,4},{4,8},{8,12},{12,16},{16,20},{20,24},{24,28},{28,32},{32,36}... | collective-permute-start | bytes 663560 | tf_op jit(solution)/shard_map/ppermute | solution.py:35
  20.2 13.4 %collective-permute-start.3 = (f32[54,1024]{1,0:T(8,128)S(1)}, f32[54,1024]{1,0:T(8,128)S(1)}, u32[]{:S(2)}, u32[]{:S(2)}) collective-permute-start(f32[54,1024]{1,0:T(8,128)S(1)} %pad_maximum_fusion.4), channel_id=1, source_target_pairs={{4,0},{8,4},{12,8},{16,12},{20,16},{24,20},{28,24},{32,28},{36,32}... | collective-permute-start | bytes 663560 | tf_op jit(solution)/shard_map/ppermute | solution.py:35
  36.0 9.1 %collective-permute-start.4 = (f32[2,8,1024]{2,1,0:T(8,128)S(1)}, f32[2,8,1024]{2,1,0:T(8,128)S(1)}, u32[]{:S(2)}, u32[]{:S(2)}) collective-permute-start(f32[2,8,1024]{2,1,0:T(8,128)S(1)} %constant_dynamic-slice_fusion), channel_id=1, source_target_pairs={{0,4},{4,8},{8,12},{12,16},{16,20},{20,24},{24,28},{28,32},{32,36}... | collective-permute-start | bytes 196616 | tf_op jit(solution)/shard_map/ppermute | solution.py:35
  38.6 8.4 %collective-permute-start.5 = (f32[2,8,1024]{2,1,0:T(8,128)S(1)}, f32[2,8,1024]{2,1,0:T(8,128)S(1)}, u32[]{:S(2)}, u32[]{:S(2)}) collective-permute-start(f32[2,8,1024]{2,1,0:T(8,128)S(1)} %slice.618), channel_id=1, source_target_pairs={{4,0},{8,4},{12,8},{16,12},{20,16},{24,20},{28,24},{32,28},{36,32}... | collective-permute-start | bytes 196616 | tf_op jit(solution)/shard_map/ppermute | solution.py:35

commit v13 on v10

--- a/solution.py
+++ b/solution.py
@@ -45,6 +45,19 @@
     return lax.ppermute(value, ("inline", "xline"), pairs)
 
 
+def exchanged(to_next, to_prev, axis):
+    count = lax.axis_size(axis)
+    odd = lax.axis_index(axis) % 2 == 1
+    first = [(i, j) for a in range(1, count - 1, 2) for i, j in ((a, a + 1), (a + 1, a))]
+    second = [(i, i ^ 1) for i in range(count) if i ^ 1 < count]
+    send_first = jnp.where(odd, to_next, to_prev)
+    send_second = jnp.where(odd, to_prev, to_next)
+    send_second = send_second + 0.0 * send_first[(0,) * send_first.ndim]
+    got_first = lax.ppermute(send_first, axis, first)
+    got_second = lax.ppermute(send_second, axis, second)
+    return jnp.where(odd, got_second, got_first), jnp.where(odd, got_first, got_second)
+
+
 def with_columns(block, depth):
     ca = block.ndim - 2
     cols = block.shape[ca]
@@ -55,8 +68,9 @@
 
 def with_rows(block, width, depth):
     ra = block.ndim - 3
-    from_prev = moved(lax.dynamic_slice_in_dim(block, width - depth, depth, ra), 1, 0)
-    from_next = moved(lax.slice_in_dim(block, 0, depth, axis=ra), -1, 0)
+    from_prev, from_next = exchanged(
+        lax.dynamic_slice_in_dim(block, width - depth, depth, ra), lax.slice_in_dim(block, 0, depth, axis=ra), "inline"
+    )
     return placed_rows(block, from_prev, from_next, width, depth)
 
 
@@ -123,8 +137,9 @@
         row_far = jnp.pad(jnp.pad(p_far, pad_mid), [(0, 2), (0, 0), (0, 0)])
         return row_near, row_far
 
-    prev_near, prev_far = rebuilt(moved(to_next, 1, 0))
-    next_near, next_far = rebuilt(moved(to_prev, -1, 0))
+    got_prev, got_next = exchanged(to_next, to_prev, "inline")
+    prev_near, prev_far = rebuilt(got_prev)
+    next_near, next_far = rebuilt(got_next)
     from_prev = jnp.stack([prev_far, prev_near], 1)
     from_next = jnp.stack([next_near, next_far], 1)
     return placed_rows(wide, from_prev, from_next, width, h)

time: 51.1 us -> 53.3 us (1.043)
  starting transfers between devices: 26 us -> 21.5 us
  waiting for transfers between devices: 9.32 us -> 13.5 us
  between operations: 3.83 us -> 5.16 us
  local copies, waits for them, and re-layouts: 4.67 us -> 5.7 us
    ppermute x4, starting transfers between devices: 22 us -> 17.6 us  [the longest x2 13.7 us: exchanged(): got_first = lax.ppermute(send_first, axis, first)]
    ppermute x4, waiting for transfers between devices: 5.37 us -> 9.53 us  [the longest x2 8.32 us: exchanged(): got_second = lax.ppermute(send_second, axis, second)]
    slice x1 -> x2, local copies, waits for them, and re-layouts: 0.01 us -> 1.03 us  [exchanged(): send_second = send_second + 0.0 * send_first[(0,) * send_first.ndim]]
  transfers between devices with their start and end apart: 6 -> 6, of which waited for: 4 -> 4; matrix products, arithmetic and copies ran while one was open for 4% -> 5% of each run, Pallas kernels for 0% -> 0%
where the time goes in v13:
time: 53.3 us; the launch traced here: 53 us
  starting transfers between devices  21.5 us (40%)
  waiting for transfers between devices  13.5 us (25%)
  other arithmetic  7.14 us (13%)
  local copies, waits for them, and re-layouts  5.7 us (11%)
  between operations  5.16 us (10%)
    ppermute x2, starting transfers between devices, exchanged(): got_first = lax.ppermute(send_first, axis, first)  13.7 us
    ppermute x2, waiting for transfers between devices, exchanged(): got_second = lax.ppermute(send_second, axis, second)  8.32 us
    ppermute x2, starting transfers between devices, moved(): return lax.ppermute(value, 'xline', pairs)  3.95 us
    ppermute x2, waiting for transfers between devices, moved(): return lax.ppermute(value, 'xline', pairs)  3.94 us
    ppermute x2, starting transfers between devices, exchanged(): got_second = lax.ppermute(send_second, axis, second)  3.84 us
    dynamic_slice x2, local copies, waits for them, and re-layouts, on_device(): field = lax.dynamic_index_in_dim(survey, batch, 0, keepdims=False)  1.73 us
    add x2, other arithmetic, relax_rows(): return centre + step_size * change  1.54 us
    mul x4, other arithmetic, attributes(): 0.25 * (neighbor(member, which_axis, 1, up_open) + 2.0 * member + neighbo...  1.37 us
  transfers between devices with their start and end apart: 6, of which 4 were waited for; matrix products, arithmetic and copies ran while one was open for 5% of the time, Pallas kernels for 0%

profile of v13, /device:TPU:30, one launch (start us, length us, event | category | flops | bytes accessed | tf_op | source)
XLA Modules:
  0.0 53.0 jit_solution(13360670145439955485)
XLA Ops:
  0.7 0.9 %constant_dynamic-slice_fusion.1 = f32[1,4,4,1024]{3,2,1,0:T(4,128)S(1)} fusion(f32[2,4,4,1024]{3,2,1,0:T(4,128)} %param.3, s32[]{:T(128)S(6)} %select_n.283), kind=kLoop, calls=%fused_computation.315 | loop fusion | bytes 131076 | tf_op jit(solution)/shard_map/jit(dynamic_index_in_dim)/dynamic_slice | solution.py:239
  1.5 0.8 %fusion.178 = f32[1,4,4,1024]{3,2,0,1:T(4,128)S(1)} fusion(f32[2,4,4,1024]{3,2,1,0:T(4,128)} %param.3, s32[]{:T(128)S(6)} %select_n.283), kind=kLoop, calls=%fused_computation.331 | loop fusion | bytes 131076 | tf_op jit(solution)/shard_map/jit(dynamic_index_in_dim)/dynamic_slice | solution.py:239
  2.5 0.2 fusion.151
  2.7 0.1 fusion.20
  3.0 2.7 %collective-permute-start.1 = (f32[56,1024]{1,0:T(8,128)S(1)}, f32[56,1024]{1,0:T(8,128)S(1)}, u32[]{:S(2)}, u32[]{:S(2)}) collective-permute-start(f32[56,1024]{1,0:T(8,128)S(1)} %pad_maximum_fusion.2), channel_id=1, source_target_pairs={{1,0},{2,1},{3,2},{5,4},{6,5},{7,6},{9,8},{10,9},{11,10},{13,12},{... | collective-permute-start | bytes 688136 | tf_op jit(solution)/shard_map/ppermute | solution.py:38
  5.8 1.3 %collective-permute-start = (f32[56,1024]{1,0:T(8,128)S(1)}, f32[56,1024]{1,0:T(8,128)S(1)}, u32[]{:S(2)}, u32[]{:S(2)}) collective-permute-start(f32[56,1024]{1,0:T(8,128)S(1)} %pad_maximum_fusion.1), channel_id=1, source_target_pairs={{0,1},{1,2},{2,3},{4,5},{5,6},{6,7},{8,9},{9,10},{10,11},{12,13},{... | collective-permute-start | bytes 688136 | tf_op jit(solution)/shard_map/ppermute | solution.py:38
  7.2 0.6 %constant_dynamic-slice_fusion.2 = s32[1,1]{0,1:T(1,128)} fusion(s32[2,1]{0,1:T(1,128)S(1)} %copy-done.1, s32[]{:T(128)S(6)} %select_n.283), kind=kLoop, calls=%fused_computation.316 | loop fusion | bytes 12 | tf_op jit(solution)/shard_map/jit(dynamic_index_in_dim)/dynamic_slice | solution.py:241
  10.9 3.9 %collective-permute-done = f32[56,1024]{1,0:T(8,128)S(1)} collective-permute-done((f32[56,1024]{1,0:T(8,128)S(1)}, f32[56,1024]{1,0:T(8,128)S(1)}, u32[]{:S(2)}, u32[]{:S(2)}) %collective-permute-start) | collective-permute-done | bytes 229408 | tf_op jit(solution)/shard_map/ppermute | solution.py:38
  15.3 0.7 %concatenate.33 = f32[4,4,12,1024]{3,2,0,1:T(8,128)S(1)} concatenate(f32[4,4,1,1024]{3,2,0,1:T(1,128)S(1)} %copy.19, f32[4,4,3,1024]{3,2,0,1:T(4,128)S(1)} %copy.20, f32[4,4,4,1024]{3,2,0,1:T(4,128)S(1)} %pad_maximum_fusion, f32[4,4,3,1024]{3,2,0,1:T(4,128)S(1)} %copy.21, f32[4,4,1,1024]{3,2,0,1:T(1,128)S(1)} %copy.22), dimensions={2} | concatenate | bytes 1572864 | tf_op jit(solution)/shard_map/concatenate | solution.py:115
  16.3 11.7 %collective-permute-start.3 = (f32[54,1024]{1,0:T(8,128)S(1)}, f32[54,1024]{1,0:T(8,128)S(1)}, u32[]{:S(2)}, u32[]{:S(2)}) collective-permute-start(f32[54,1024]{1,0:T(8,128)S(1)} %fusion.131), channel_id=1, source_target_pairs={{4,8},{8,4},{12,16},{16,12},{20,24},{24,20},{28,32},{32,28},{36,40... | collective-permute-start | bytes 663560 | tf_op jit(solution)/shard_map/ppermute | solution.py:56
  28.0 0.5 slice.603
  29.2 1.9 %collective-permute-start.2 = (f32[54,1024]{1,0:T(8,128)S(1)}, f32[54,1024]{1,0:T(8,128)S(1)}, u32[]{:S(2)}, u32[]{:S(2)}) collective-permute-start(f32[54,1024]{1,0:T(8,128)S(1)} %select_add_fusion.12), channel_id=1, source_target_pairs={{0,4},{4,0},{8,12},{12,8},{16,20},{20,16},{24,28},{28,24},{32,36},... | collective-permute-start | bytes 663560 | tf_op jit(solution)/shard_map/ppermute | solution.py:57
  31.2 1.2 %collective-permute-done.3 = f32[54,1024]{1,0:T(8,128)S(1)} collective-permute-done((f32[54,1024]{1,0:T(8,128)S(1)}, f32[54,1024]{1,0:T(8,128)S(1)}, u32[]{:S(2)}, u32[]{:S(2)}) %collective-permute-start.3) | collective-permute-done | bytes 221216 | tf_op jit(solution)/shard_map/ppermute | solution.py:56
  32.4 4.7 %collective-permute-done.2 = f32[54,1024]{1,0:T(8,128)S(1)} collective-permute-done((f32[54,1024]{1,0:T(8,128)S(1)}, f32[54,1024]{1,0:T(8,128)S(1)}, u32[]{:S(2)}, u32[]{:S(2)}) %collective-permute-start.2) | collective-permute-done | bytes 221216 | tf_op jit(solution)/shard_map/ppermute | solution.py:57
  37.5 0.3 maximum_maximum_fusion
  37.8 0.1 slice_bitcast_fusion
  38.0 0.9 %fusion.8 = f32[6,12,1024]{2,1,0:T(8,128)S(1)} fusion(f32[6,12,1024]{2,1,0:T(8,128)S(1)} %get-tuple-element.43, f32[6,12,1024]{2,1,0:T(8,128)S(1)} %get-tuple-element.42, f32[6,12,1024]{2,1,0:T(8,128)S(1)} %get-tuple-element.41, f32[4,8,12,1024]{3,2,0,1:T(8,128)S(1)} %maximum_dynamic-update-slice_fusion, pred[12]{0:T(512)(128)(4,1)S(1)} %get-tuple-element.90, ...), kind=kLoop, calls=%fused_computation.43 | loop fusion | flops 3170304 | bytes 2656292 | tf_op jit(solution)/shard_map/add | solution.py:191
  39.0 0.6 %fusion.92 = f32[4,12,1024]{2,1,0:T(8,128)S(1)} fusion(f32[4,12,1024]{2,1,0:T(8,128)S(1)} %slice.618, f32[4,12,1024]{2,1,0:T(8,128)S(1)} %get-tuple-element.40, f32[4,12,1024]{2,1,0:T(8,128)S(1)} %get-tuple-element.39, f32[6,12,1024]{2,1,0:T(8,128)S(1)} %fusion.8, f32[4,8,12,1024]{3,2,0,1:T(8,128)S(1)} %maximum_dynamic-update-slice_fusion, ...), kind=kLoop, calls=%fused_computation.181 | loop fusion | flops 2113536 | bytes 1771552 | tf_op jit(solution)/shard_map/add | solution.py:191
  39.6 0.5 slice.628
  40.1 2.0 %collective-permute-start.5 = (f32[2,8,1024]{2,1,0:T(8,128)S(1)}, f32[2,8,1024]{2,1,0:T(8,128)S(1)}, u32[]{:S(2)}, u32[]{:S(2)}) collective-permute-start(f32[2,8,1024]{2,1,0:T(8,128)S(1)} %slice_select_fusion), channel_id=1, source_target_pairs={{4,8},{8,4},{12,16},{16,12},{20,24},{24,20},{28,32},{32,28},{36,40... | collective-permute-start | bytes 196616 | tf_op jit(solution)/shard_map/ppermute | solution.py:56
  42.9 1.9 %collective-permute-start.4 = (f32[2,8,1024]{2,1,0:T(8,128)S(1)}, f32[2,8,1024]{2,1,0:T(8,128)S(1)}, u32[]{:S(2)}, u32[]{:S(2)}) collective-permute-start(f32[2,8,1024]{2,1,0:T(8,128)S(1)} %select_add_fusion.13), channel_id=1, source_target_pairs={{0,4},{4,0},{8,12},{12,8},{16,20},{20,16},{24,28},{28,24},{32,36},... | collective-permute-start | bytes 196616 | tf_op jit(solution)/shard_map/ppermute | solution.py:57
  44.8 0.7 %iota_compare_fusion.4 = pred[4]{0:T(512)(128)(4,1)S(1)} fusion(s32[]{:T(128)} %bitcast), kind=kLoop, calls=%fused_computation.325 | loop fusion | flops 4 | bytes 8 | tf_op jit(solution)/shard_map/lt | solution.py:243
  45.4 3.6 %collective-permute-done.4 = f32[2,8,1024]{2,1,0:T(8,128)S(1)} collective-permute-done((f32[2,8,1024]{2,1,0:T(8,128)S(1)}, f32[2,8,1024]{2,1,0:T(8,128)S(1)}, u32[]{:S(2)}, u32[]{:S(2)}) %collective-permute-start.4) | collective-permute-done | bytes 65568 | tf_op jit(solution)/shard_map/ppermute | solution.py:57
  49.1 0.2 fusion.154
  49.3 0.2 fusion.153
  49.6 0.2 broadcast_multiply_fusion.1
  49.8 0.5 broadcast_multiply_fusion.3
  50.3 0.3 broadcast_multiply_fusion
  50.6 0.4 broadcast_multiply_fusion.2
  51.0 0.3 fusion.74
  51.4 0.7 %fusion.51 = (f32[8,8,1024]{2,1,0:T(8,128)S(1)}, f32[8,8,1024]{2,1,0:T(8,128)S(1)}, f32[8,8,1024]{2,1,0:T(8,128)S(1)}, f32[8,8,1024]{2,1,0:T(8,128)S(1)}) fusion(f32[8,8,1024]{2,1,0:T(8,128)S(1)} %get-tuple-element.68, f32[8,8,1024]{2,1,0:T(8,128)S(1)} %get-tuple-element.69, pred[1024]{0:T(1024)(128)(4,1)S(1)} %get-tuple-element.88, ...), kind=kLoop, calls=%fused_computation.140 | loop fusion | flops 1900544 | bytes 3147776 | tf_op jit(solution)/shard_map/add | solution.py:224
  52.1 0.9 %fusion.139 = (f32[1,4,4,1024]{3,2,1,0:T(4,128)}, f32[1,4,4,1024]{3,2,1,0:T(4,128)}) fusion(f32[8,8,1024]{2,1,0:T(8,128)S(1)} %get-tuple-element.49, f32[8,8,1024]{2,1,0:T(8,128)S(1)} %get-tuple-element.51, f32[8,8,1024]{2,1,0:T(8,128)S(1)} %get-tuple-element.13, f32[8,8,1024]{2,1,0:T(8,128)S(1)} %get-tuple-element.14, ...), kind=kLoop, calls=%fused_computation.271 | loop fusion | flops 393216 | bytes 983044 | tf_op jit(solution)/shard_map/broadcast_in_dim | solution.py:260
  (71 shorter events, 2.3 us)
Async XLA Ops:
  0.6 1.8 %copy-start = (bf16[3,2,4,4,1024]{4,3,2,1,0:T(4,128)(2,1)S(1)}, bf16[3,2,4,4,1024]{4,3,2,1,0:T(4,128)(2,1)}, u32[]{:S(2)}) copy-start(bf16[3,2,4,4,1024]{4,3,2,1,0:T(4,128)(2,1)} %param.4) | copy-start | bytes 589828
  2.4 4.7 %copy-start.1 = (s32[2,1]{0,1:T(1,128)S(1)}, s32[2,1]{0,1:T(1,128)}, u32[]{:S(2)}) copy-start(s32[2,1]{0,1:T(1,128)} %param.5) | copy-start | bytes 28
  3.0 7.9 %collective-permute-start.1 = (f32[56,1024]{1,0:T(8,128)S(1)}, f32[56,1024]{1,0:T(8,128)S(1)}, u32[]{:S(2)}, u32[]{:S(2)}) collective-permute-start(f32[56,1024]{1,0:T(8,128)S(1)} %pad_maximum_fusion.2), channel_id=1, source_target_pairs={{1,0},{2,1},{3,2},{5,4},{6,5},{7,6},{9,8},{10,9},{11,10},{13,12},{... | collective-permute-start | bytes 688136 | tf_op jit(solution)/shard_map/ppermute | solution.py:38
  5.8 9.0 %collective-permute-start = (f32[56,1024]{1,0:T(8,128)S(1)}, f32[56,1024]{1,0:T(8,128)S(1)}, u32[]{:S(2)}, u32[]{:S(2)}) collective-permute-start(f32[56,1024]{1,0:T(8,128)S(1)} %pad_maximum_fusion.1), channel_id=1, source_target_pairs={{0,1},{1,2},{2,3},{4,5},{5,6},{6,7},{8,9},{9,10},{10,11},{12,13},{... | collective-permute-start | bytes 688136 | tf_op jit(solution)/shard_map/ppermute | solution.py:38
  16.3 16.1 %collective-permute-start.3 = (f32[54,1024]{1,0:T(8,128)S(1)}, f32[54,1024]{1,0:T(8,128)S(1)}, u32[]{:S(2)}, u32[]{:S(2)}) collective-permute-start(f32[54,1024]{1,0:T(8,128)S(1)} %fusion.131), channel_id=1, source_target_pairs={{4,8},{8,4},{12,16},{16,12},{20,24},{24,20},{28,32},{32,28},{36,40... | collective-permute-start | bytes 663560 | tf_op jit(solution)/shard_map/ppermute | solution.py:56
  29.2 7.9 %collective-permute-start.2 = (f32[54,1024]{1,0:T(8,128)S(1)}, f32[54,1024]{1,0:T(8,128)S(1)}, u32[]{:S(2)}, u32[]{:S(2)}) collective-permute-start(f32[54,1024]{1,0:T(8,128)S(1)} %select_add_fusion.12), channel_id=1, source_target_pairs={{0,4},{4,0},{8,12},{12,8},{16,20},{20,16},{24,28},{28,24},{32,36},... | collective-permute-start | bytes 663560 | tf_op jit(solution)/shard_map/ppermute | solution.py:57
  40.1 8.9 %collective-permute-start.5 = (f32[2,8,1024]{2,1,0:T(8,128)S(1)}, f32[2,8,1024]{2,1,0:T(8,128)S(1)}, u32[]{:S(2)}, u32[]{:S(2)}) collective-permute-start(f32[2,8,1024]{2,1,0:T(8,128)S(1)} %slice_select_fusion), channel_id=1, source_target_pairs={{4,8},{8,4},{12,16},{16,12},{20,24},{24,20},{28,32},{32,28},{36,40... | collective-permute-start | bytes 196616 | tf_op jit(solution)/shard_map/ppermute | solution.py:56
  42.9 6.2 %collective-permute-start.4 = (f32[2,8,1024]{2,1,0:T(8,128)S(1)}, f32[2,8,1024]{2,1,0:T(8,128)S(1)}, u32[]{:S(2)}, u32[]{:S(2)}) collective-permute-start(f32[2,8,1024]{2,1,0:T(8,128)S(1)} %select_add_fusion.13), channel_id=1, source_target_pairs={{0,4},{4,0},{8,12},{12,8},{16,20},{20,16},{24,28},{28,24},{32,36},... | collective-permute-start | bytes 196616 | tf_op jit(solution)/shard_map/ppermute | solution.py:57

commit v14 on v10

--- a/solution.py
+++ b/solution.py
@@ -98,11 +98,11 @@
 
     left = edge(from_left[0], from_left[1], True)
     right = edge(from_right[0], from_right[1], False)
-    return jnp.concatenate([left, fields, right], 2)
-
-
-def diffusion_rows(wide, width, cols):
-    n_f, rows, n_c, samples = wide.shape
+    return left, fields, right
+
+
+def diffusion_rows(parts, width, cols):
+    n_f, rows, _, samples = parts[1].shape
     h = HALO
     near = slice(cols - 3, 2 * cols + 3)
     mid = slice(cols - 2, 2 * cols + 2)
@@ -110,9 +110,14 @@
     def pieces(row_near, row_far):
         return packed([row_near[0:3, near], row_near[3, mid], row_far[0:2, mid]])
 
-    last = lax.dynamic_slice_in_dim(wide, width - h, h, 1)
+    def rows_at(start):
+        return jnp.concatenate([lax.dynamic_slice_in_dim(part, start, h, 1) for part in parts], 2)
+
+    last = rows_at(width - h)
+    first = jnp.concatenate([part[:, :h] for part in parts], 2)
+    wide = jnp.concatenate(parts, 2)
     to_next = pieces(last[:, 1], last[:, 0])
-    to_prev = pieces(wide[:, 0], wide[:, 1])
+    to_prev = pieces(first[:, 0], first[:, 1])
     shapes = [(3, cols + 6, samples), (cols + 4, samples), (2, cols + 4, samples)]
 
     def rebuilt(flat):

time: 51.1 us -> 50.5 us (0.988)
  local copies, waits for them, and re-layouts: 4.67 us -> 2.76 us
  other arithmetic: 7.01 us -> 8.44 us
    dynamic_slice x2 -> x1, local copies, waits for them, and re-layouts: 1.73 us -> 0.01 us  [on_device(): field = lax.dynamic_index_in_dim(survey, batch, 0, keepdims=False)]
    convert_element_type x1, other arithmetic: 0.03 us -> 0.97 us  [on_device(): lax.dynamic_index_in_dim(conduct, batch, 1, keepdims=False)]
  transfers between devices with their start and end apart: 6 -> 6, of which waited for: 4 -> 4; matrix products, arithmetic and copies ran while one was open for 4% -> 6% of each run, Pallas kernels for 0% -> 0%
where the time goes in v14:
time: 50.5 us; the launch traced here: 50.2 us
  starting transfers between devices  26 us (51%)
  waiting for transfers between devices  9.18 us (18%)
  other arithmetic  8.44 us (17%)
  between operations  3.87 us (8%)
  local copies, waits for them, and re-layouts  2.76 us (5%)
    ppermute x4, starting transfers between devices, moved(): return lax.ppermute(value, 'inline', pairs)  22 us
    ppermute x4, waiting for transfers between devices, moved(): return lax.ppermute(value, 'inline', pairs)  5.35 us
    ppermute x2, starting transfers between devices, moved(): return lax.ppermute(value, 'xline', pairs)  3.95 us
    ppermute x2, waiting for transfers between devices, moved(): return lax.ppermute(value, 'xline', pairs)  3.83 us
    add x2, other arithmetic, relax_rows(): return centre + step_size * change  1.54 us
    mul x4, other arithmetic, attributes(): 0.25 * (neighbor(member, which_axis, 1, up_open) + 2.0 * member + neighbo...  1.37 us
  transfers between devices with their start and end apart: 6, of which 4 were waited for; matrix products, arithmetic and copies ran while one was open for 6% of the time, Pallas kernels for 0%

profile of v14, /device:TPU:30, one launch (start us, length us, event | category | flops | bytes accessed | tf_op | source)
XLA Modules:
  0.0 50.2 jit_solution(3982186200915315747)
XLA Ops:
  0.7 1.0 %fusion.157 = (f32[3,4,4,1024]{3,2,1,0:T(4,128)S(1)}, f32[3,1,4,4,1024]{4,3,2,0,1:T(4,128)S(1)}) fusion(bf16[3,2,4,4,1024]{4,3,2,1,0:T(4,128)(2,1)} %param.4, s32[]{:T(128)S(6)} %select_n.236), kind=kLoop, calls=%fused_computation.316 | loop fusion | flops 49152 | bytes 491524 | tf_op jit(solution)/shard_map/convert_element_type | solution.py:230
  1.7 0.2 fusion.156
  1.9 0.1 fusion.22
  2.0 0.1 reshape.121
  2.2 2.7 %collective-permute-start.1 = (f32[56,1024]{1,0:T(8,128)S(1)}, f32[56,1024]{1,0:T(8,128)S(1)}, u32[]{:S(2)}, u32[]{:S(2)}) collective-permute-start(f32[56,1024]{1,0:T(8,128)S(1)} %pad_maximum_fusion.5), channel_id=1, source_target_pairs={{1,0},{2,1},{3,2},{5,4},{6,5},{7,6},{9,8},{10,9},{11,10},{13,12},{... | collective-permute-start | bytes 688136 | tf_op jit(solution)/shard_map/ppermute | solution.py:38
  5.0 1.3 %collective-permute-start = (f32[56,1024]{1,0:T(8,128)S(1)}, f32[56,1024]{1,0:T(8,128)S(1)}, u32[]{:S(2)}, u32[]{:S(2)}) collective-permute-start(f32[56,1024]{1,0:T(8,128)S(1)} %pad_maximum_fusion.4), channel_id=1, source_target_pairs={{0,1},{1,2},{2,3},{4,5},{5,6},{6,7},{8,9},{9,10},{10,11},{12,13},{... | collective-permute-start | bytes 688136 | tf_op jit(solution)/shard_map/ppermute | solution.py:38
  6.4 0.6 %constant_dynamic-slice_fusion.2 = s32[1,1]{0,1:T(1,128)} fusion(s32[2,1]{0,1:T(1,128)S(1)} %copy-done.1, s32[]{:T(128)S(6)} %select_n.236), kind=kLoop, calls=%fused_computation.326 | loop fusion | bytes 12 | tf_op jit(solution)/shard_map/jit(dynamic_index_in_dim)/dynamic_slice | solution.py:231
  10.1 3.8 %collective-permute-done = f32[56,1024]{1,0:T(8,128)S(1)} collective-permute-done((f32[56,1024]{1,0:T(8,128)S(1)}, f32[56,1024]{1,0:T(8,128)S(1)}, u32[]{:S(2)}, u32[]{:S(2)}) %collective-permute-start) | collective-permute-done | bytes 229408 | tf_op jit(solution)/shard_map/ppermute | solution.py:38
  14.4 0.1 fusion.133
  14.8 3.8 %collective-permute-start.2 = (f32[54,1024]{1,0:T(8,128)S(1)}, f32[54,1024]{1,0:T(8,128)S(1)}, u32[]{:S(2)}, u32[]{:S(2)}) collective-permute-start(f32[54,1024]{1,0:T(8,128)S(1)} %pad_maximum_fusion.6), channel_id=1, source_target_pairs={{0,4},{4,8},{8,12},{12,16},{16,20},{20,24},{24,28},{28,32},{32,36}... | collective-permute-start | bytes 663560 | tf_op jit(solution)/shard_map/ppermute | solution.py:35
  18.6 0.2 fusion
  18.9 0.7 %concatenate.51 = f32[4,4,12,1024]{3,2,1,0:T(8,128)S(1)} concatenate(f32[4,4,1,1024]{3,2,1,0:T(1,128)S(1)} %copy.19, f32[4,4,3,1024]{3,2,1,0:T(4,128)S(1)} %reshape.120, f32[4,4,4,1024]{3,2,1,0:T(4,128)S(1)} %pad_maximum_fusion, f32[4,4,3,1024]{3,2,1,0:T(4,128)S(1)} %reshape.122, f32[4,4,1,1024]{3,2,1,0:T(1,128)S(1)} %copy.20), dimensions={2} | concatenate | bytes 1572864 | tf_op jit(solution)/shard_map/concatenate | solution.py:118
  19.6 9.8 %collective-permute-start.3 = (f32[54,1024]{1,0:T(8,128)S(1)}, f32[54,1024]{1,0:T(8,128)S(1)}, u32[]{:S(2)}, u32[]{:S(2)}) collective-permute-start(f32[54,1024]{1,0:T(8,128)S(1)} %pad_maximum_fusion.7), channel_id=1, source_target_pairs={{4,0},{8,4},{12,8},{16,12},{20,16},{24,20},{28,24},{32,28},{36,32}... | collective-permute-start | bytes 663560 | tf_op jit(solution)/shard_map/ppermute | solution.py:35
  29.4 1.5 %collective-permute-done.2 = f32[54,1024]{1,0:T(8,128)S(1)} collective-permute-done((f32[54,1024]{1,0:T(8,128)S(1)}, f32[54,1024]{1,0:T(8,128)S(1)}, u32[]{:S(2)}, u32[]{:S(2)}) %collective-permute-start.2) | collective-permute-done | bytes 221216 | tf_op jit(solution)/shard_map/ppermute | solution.py:35
  30.9 2.1 %collective-permute-done.3 = f32[54,1024]{1,0:T(8,128)S(1)} collective-permute-done((f32[54,1024]{1,0:T(8,128)S(1)}, f32[54,1024]{1,0:T(8,128)S(1)}, u32[]{:S(2)}, u32[]{:S(2)}) %collective-permute-start.3) | collective-permute-done | bytes 221216 | tf_op jit(solution)/shard_map/ppermute | solution.py:35
  33.2 0.3 maximum_maximum_fusion
  33.6 0.1 slice_bitcast_fusion
  33.8 0.9 %fusion.10 = f32[6,12,1024]{2,1,0:T(8,128)S(1)} fusion(f32[6,12,1024]{2,1,0:T(8,128)S(1)} %get-tuple-element.43, f32[6,12,1024]{2,1,0:T(8,128)S(1)} %get-tuple-element.42, f32[6,12,1024]{2,1,0:T(8,128)S(1)} %get-tuple-element.41, f32[4,8,12,1024]{3,2,1,0:T(8,128)S(1)} %maximum_dynamic-update-slice_fusion, pred[12]{0:T(512)(128)(4,1)S(1)} %get-tuple-element.90, ...), kind=kLoop, calls=%fused_computation.50 | loop fusion | flops 3170304 | bytes 2656292 | tf_op jit(solution)/shard_map/add | solution.py:181
  34.7 0.6 %fusion.94 = f32[4,12,1024]{2,1,0:T(8,128)S(1)} fusion(f32[4,12,1024]{2,1,0:T(8,128)S(1)} %slice.625, f32[4,12,1024]{2,1,0:T(8,128)S(1)} %get-tuple-element.40, f32[4,12,1024]{2,1,0:T(8,128)S(1)} %get-tuple-element.39, f32[6,12,1024]{2,1,0:T(8,128)S(1)} %fusion.10, f32[4,8,12,1024]{3,2,1,0:T(8,128)S(1)} %maximum_dynamic-update-slice_fusion, ...), kind=kLoop, calls=%fused_computation.190 | loop fusion | flops 2113536 | bytes 1771552 | tf_op jit(solution)/shard_map/add | solution.py:181
  35.4 1.9 %collective-permute-start.4 = (f32[2,8,1024]{2,1,0:T(8,128)S(1)}, f32[2,8,1024]{2,1,0:T(8,128)S(1)}, u32[]{:S(2)}, u32[]{:S(2)}) collective-permute-start(f32[2,8,1024]{2,1,0:T(8,128)S(1)} %constant_dynamic-slice_fusion), channel_id=1, source_target_pairs={{0,4},{4,8},{8,12},{12,16},{16,20},{20,24},{24,28},{28,32},{32,36}... | collective-permute-start | bytes 196616 | tf_op jit(solution)/shard_map/ppermute | solution.py:35
  37.3 0.7 %iota_compare_fusion.4 = pred[4]{0:T(512)(128)(4,1)S(1)} fusion(s32[]{:T(128)} %bitcast), kind=kLoop, calls=%fused_computation.335 | loop fusion | flops 4 | bytes 8 | tf_op jit(solution)/shard_map/lt | solution.py:233
  38.0 6.5 %collective-permute-start.5 = (f32[2,8,1024]{2,1,0:T(8,128)S(1)}, f32[2,8,1024]{2,1,0:T(8,128)S(1)}, u32[]{:S(2)}, u32[]{:S(2)}) collective-permute-start(f32[2,8,1024]{2,1,0:T(8,128)S(1)} %slice.634), channel_id=1, source_target_pairs={{4,0},{8,4},{12,8},{16,12},{20,16},{24,20},{28,24},{32,28},{36,32}... | collective-permute-start | bytes 196616 | tf_op jit(solution)/shard_map/ppermute | solution.py:35
  44.6 1.8 %collective-permute-done.5 = f32[2,8,1024]{2,1,0:T(8,128)S(1)} collective-permute-done((f32[2,8,1024]{2,1,0:T(8,128)S(1)}, f32[2,8,1024]{2,1,0:T(8,128)S(1)}, u32[]{:S(2)}, u32[]{:S(2)}) %collective-permute-start.5) | collective-permute-done | bytes 65568 | tf_op jit(solution)/shard_map/ppermute | solution.py:35
  46.4 0.2 fusion.159
  46.6 0.2 fusion.158
  46.9 0.2 broadcast_multiply_fusion.1
  47.0 0.5 %broadcast_multiply_fusion.3 = (f32[8,8,1024]{2,1,0:T(8,128)S(1)}, f32[8,8,1024]{2,1,0:T(8,128)S(1)}, f32[8,8,1024]{2,1,0:T(8,128)S(1)}, f32[8,8,1024]{2,1,0:T(8...) fusion(f32[8,8,1024]{2,1,0:T(8,128)S(1)} %get-tuple-element.21,, ...), kind=kLoop, calls=%fused_computation.262 | loop fusion | flops 1966080 | bytes 3932176 | tf_op jit(solution)/shard_map/mul | solution.py:206
  47.6 0.3 broadcast_multiply_fusion
  47.8 0.4 broadcast_multiply_fusion.2
  48.3 0.3 fusion.76
  48.6 0.7 %fusion.53 = (f32[8,8,1024]{2,1,0:T(8,128)S(1)}, f32[8,8,1024]{2,1,0:T(8,128)S(1)}, f32[8,8,1024]{2,1,0:T(8,128)S(1)}, f32[8,8,1024]{2,1,0:T(8,128)S(1)}) fusion(f32[8,8,1024]{2,1,0:T(8,128)S(1)} %get-tuple-element.68, f32[8,8,1024]{2,1,0:T(8,128)S(1)} %get-tuple-element.69, pred[1024]{0:T(1024)(128)(4,1)S(1)} %get-tuple-element.88, ...), kind=kLoop, calls=%fused_computation.149 | loop fusion | flops 1900544 | bytes 3147776 | tf_op jit(solution)/shard_map/add | solution.py:214
  49.3 0.9 %fusion.144 = (f32[1,4,4,1024]{3,2,1,0:T(4,128)}, f32[1,4,4,1024]{3,2,1,0:T(4,128)}) fusion(f32[8,8,1024]{2,1,0:T(8,128)S(1)} %get-tuple-element.45, f32[8,8,1024]{2,1,0:T(8,128)S(1)} %get-tuple-element.47, f32[8,8,1024]{2,1,0:T(8,128)S(1)} %get-tuple-element.13, f32[8,8,1024]{2,1,0:T(8,128)S(1)} %get-tuple-element.14, ...), kind=kLoop, calls=%fused_computation.284 | loop fusion | flops 393216 | bytes 983044 | tf_op jit(solution)/shard_map/broadcast_in_dim | solution.py:250
  (68 shorter events, 2.0 us)
Async XLA Ops:
  0.6 1.0 %copy-start = (f32[2,4,4,1024]{3,2,1,0:T(4,128)S(1)}, f32[2,4,4,1024]{3,2,1,0:T(4,128)}, u32[]{:S(2)}) copy-start(f32[2,4,4,1024]{3,2,1,0:T(4,128)} %param.3) | copy-start | bytes 393220
  0.7 5.8 %copy-start.1 = (s32[2,1]{0,1:T(1,128)S(1)}, s32[2,1]{0,1:T(1,128)}, u32[]{:S(2)}) copy-start(s32[2,1]{0,1:T(1,128)} %param.5) | copy-start | bytes 28
  2.2 7.9 %collective-permute-start.1 = (f32[56,1024]{1,0:T(8,128)S(1)}, f32[56,1024]{1,0:T(8,128)S(1)}, u32[]{:S(2)}, u32[]{:S(2)}) collective-permute-start(f32[56,1024]{1,0:T(8,128)S(1)} %pad_maximum_fusion.5), channel_id=1, source_target_pairs={{1,0},{2,1},{3,2},{5,4},{6,5},{7,6},{9,8},{10,9},{11,10},{13,12},{... | collective-permute-start | bytes 688136 | tf_op jit(solution)/shard_map/ppermute | solution.py:38
  5.0 9.0 %collective-permute-start = (f32[56,1024]{1,0:T(8,128)S(1)}, f32[56,1024]{1,0:T(8,128)S(1)}, u32[]{:S(2)}, u32[]{:S(2)}) collective-permute-start(f32[56,1024]{1,0:T(8,128)S(1)} %pad_maximum_fusion.4), channel_id=1, source_target_pairs={{0,1},{1,2},{2,3},{4,5},{5,6},{6,7},{8,9},{9,10},{10,11},{12,13},{... | collective-permute-start | bytes 688136 | tf_op jit(solution)/shard_map/ppermute | solution.py:38
  14.8 16.1 %collective-permute-start.2 = (f32[54,1024]{1,0:T(8,128)S(1)}, f32[54,1024]{1,0:T(8,128)S(1)}, u32[]{:S(2)}, u32[]{:S(2)}) collective-permute-start(f32[54,1024]{1,0:T(8,128)S(1)} %pad_maximum_fusion.6), channel_id=1, source_target_pairs={{0,4},{4,8},{8,12},{12,16},{16,20},{20,24},{24,28},{28,32},{32,36}... | collective-permute-start | bytes 663560 | tf_op jit(solution)/shard_map/ppermute | solution.py:35
  19.6 13.4 %collective-permute-start.3 = (f32[54,1024]{1,0:T(8,128)S(1)}, f32[54,1024]{1,0:T(8,128)S(1)}, u32[]{:S(2)}, u32[]{:S(2)}) collective-permute-start(f32[54,1024]{1,0:T(8,128)S(1)} %pad_maximum_fusion.7), channel_id=1, source_target_pairs={{4,0},{8,4},{12,8},{16,12},{20,16},{24,20},{28,24},{32,28},{36,32}... | collective-permute-start | bytes 663560 | tf_op jit(solution)/shard_map/ppermute | solution.py:35
  35.4 9.1 %collective-permute-start.4 = (f32[2,8,1024]{2,1,0:T(8,128)S(1)}, f32[2,8,1024]{2,1,0:T(8,128)S(1)}, u32[]{:S(2)}, u32[]{:S(2)}) collective-permute-start(f32[2,8,1024]{2,1,0:T(8,128)S(1)} %constant_dynamic-slice_fusion), channel_id=1, source_target_pairs={{0,4},{4,8},{8,12},{12,16},{16,20},{20,24},{24,28},{28,32},{32,36}... | collective-permute-start | bytes 196616 | tf_op jit(solution)/shard_map/ppermute | solution.py:35
  38.0 8.4 %collective-permute-start.5 = (f32[2,8,1024]{2,1,0:T(8,128)S(1)}, f32[2,8,1024]{2,1,0:T(8,128)S(1)}, u32[]{:S(2)}, u32[]{:S(2)}) collective-permute-start(f32[2,8,1024]{2,1,0:T(8,128)S(1)} %slice.634), channel_id=1, source_target_pairs={{4,0},{8,4},{12,8},{16,12},{20,16},{24,20},{28,24},{32,28},{36,32}... | collective-permute-start | bytes 196616 | tf_op jit(solution)/shard_map/ppermute | solution.py:35

commit v15 on v14

--- a/solution.py
+++ b/solution.py
@@ -154,29 +154,34 @@
     ]
 
 
-def near(source, lo, hi, at, which_axis, offset, opened):
-    centre = source[lo - at : hi - at]
+def near(source, lo, hi, at, which_axis, offset, opened, cols=None):
+    cut = slice(None) if cols is None else slice(*cols)
+    centre = source[lo - at : hi - at, cut]
     if which_axis == 0:
-        return jnp.where(opened, source[lo - at + offset : hi - at + offset], centre)
+        return jnp.where(opened, source[lo - at + offset : hi - at + offset, cut], centre)
+    if which_axis == 1 and cols is not None:
+        return jnp.where(opened, source[lo - at : hi - at, cols[0] + offset : cols[1] + offset], centre)
     return jnp.where(opened, shifted(centre, which_axis, offset), centre)
 
 
-def rows_of(masks, lo, hi):
+def rows_of(masks, lo, hi, cols=None):
     rows = masks[0]
-    return [(rows[0][lo:hi], rows[1][lo:hi])] + list(masks[1:])
-
-
-def relax_rows(values, coeffs, masks, lo, hi, at):
-    opened = rows_of(masks, lo, hi)
-    centre = values[lo - at : hi - at]
+    column = masks[1] if cols is None else tuple(m[:, cols[0] : cols[1]] for m in masks[1])
+    return [(rows[0][lo:hi], rows[1][lo:hi]), column, masks[2]]
+
+
+def relax_rows(values, coeffs, masks, lo, hi, at, cols=None):
+    opened = rows_of(masks, lo, hi, cols)
+    cut = slice(None) if cols is None else slice(*cols)
+    centre = values[lo - at : hi - at, cut]
     change = jnp.zeros_like(centre)
     for which_axis in range(3):
         kk = coeffs[which_axis]
-        k_centre = kk[lo - at : hi - at]
+        k_centre = kk[lo - at : hi - at, cut]
         up_open, down_open = opened[which_axis]
         for offset, mask in ((1, up_open), (-1, down_open)):
-            change = change + 0.5 * (k_centre + near(kk, lo, hi, at, which_axis, offset, mask)) * (
-                near(values, lo, hi, at, which_axis, offset, mask) - centre
+            change = change + 0.5 * (k_centre + near(kk, lo, hi, at, which_axis, offset, mask, cols)) * (
+                near(values, lo, hi, at, which_axis, offset, mask, cols) - centre
             )
     return centre + step_size * change
 
@@ -240,9 +245,10 @@
     at = 0
     for repeat in range(STEPS):
         lo, hi = repeat + 1, n_rows - repeat - 1
-        values = relax_rows(values, coeffs_grown[:, lo - 1 :], masks, lo, hi, at)
+        kept = (cols - h, 2 * cols + h) if repeat == STEPS - 1 else None
+        values = relax_rows(values, coeffs_grown[:, lo - 1 :], masks, lo, hi, at, kept)
         at = lo
-    smooth = values[h - at : h - at + rows, cols - h : 2 * cols + h]
+    smooth = values[h - at : h - at + rows]
 
     grown = with_rows(smooth, width, h)
     masks = face_masks(width, rows, cols, samples, h, h)

time: 50.5 us -> 50.3 us (level)
  no operation moved by 1% of the time
where the time goes in v15:
time: 50.3 us; the launch traced here: 50 us
  starting transfers between devices  26 us (52%)
  waiting for transfers between devices  9.08 us (18%)
  other arithmetic  8.18 us (16%)
  between operations  3.87 us (8%)
  local copies, waits for them, and re-layouts  2.92 us (6%)
    ppermute x4, starting transfers between devices, moved(): return lax.ppermute(value, 'inline', pairs)  22 us
    ppermute x4, waiting for transfers between devices, moved(): return lax.ppermute(value, 'inline', pairs)  5.35 us
    ppermute x2, starting transfers between devices, moved(): return lax.ppermute(value, 'xline', pairs)  3.95 us
    ppermute x2, waiting for transfers between devices, moved(): return lax.ppermute(value, 'xline', pairs)  3.73 us
    mul x4, other arithmetic, attributes(): 0.25 * (neighbor(member, which_axis, 1, up_open) + 2.0 * member + neighbo...  1.37 us
    add x2, other arithmetic, relax_rows(): return centre + step_size * change  1.26 us
  transfers between devices with their start and end apart: 6, of which 4 were waited for; matrix products, arithmetic and copies ran while one was open for 6% of the time, Pallas kernels for 0%

profile of v15, /device:TPU:30, one launch (start us, length us, event | category | flops | bytes accessed | tf_op | source)
XLA Modules:
  0.0 50.0 jit_solution(17565634246220904844)
XLA Ops:
  0.7 1.0 %fusion.157 = (f32[3,4,4,1024]{3,2,1,0:T(4,128)S(1)}, f32[3,1,4,4,1024]{4,3,2,0,1:T(4,128)S(1)}) fusion(bf16[3,2,4,4,1024]{4,3,2,1,0:T(4,128)(2,1)} %param.4, s32[]{:T(128)S(6)} %select_n.236), kind=kLoop, calls=%fused_computation.314 | loop fusion | flops 49152 | bytes 491524 | tf_op jit(solution)/shard_map/convert_element_type | solution.py:235
  1.7 0.2 fusion.156
  1.9 0.1 fusion.22
  2.2 2.7 %collective-permute-start.1 = (f32[56,1024]{1,0:T(8,128)S(1)}, f32[56,1024]{1,0:T(8,128)S(1)}, u32[]{:S(2)}, u32[]{:S(2)}) collective-permute-start(f32[56,1024]{1,0:T(8,128)S(1)} %pad_maximum_fusion.5), channel_id=1, source_target_pairs={{1,0},{2,1},{3,2},{5,4},{6,5},{7,6},{9,8},{10,9},{11,10},{13,12},{... | collective-permute-start | bytes 688136 | tf_op jit(solution)/shard_map/ppermute | solution.py:38
  5.0 1.3 %collective-permute-start = (f32[56,1024]{1,0:T(8,128)S(1)}, f32[56,1024]{1,0:T(8,128)S(1)}, u32[]{:S(2)}, u32[]{:S(2)}) collective-permute-start(f32[56,1024]{1,0:T(8,128)S(1)} %pad_maximum_fusion.4), channel_id=1, source_target_pairs={{0,1},{1,2},{2,3},{4,5},{5,6},{6,7},{8,9},{9,10},{10,11},{12,13},{... | collective-permute-start | bytes 688136 | tf_op jit(solution)/shard_map/ppermute | solution.py:38
  6.5 0.6 %constant_dynamic-slice_fusion.2 = s32[1,1]{0,1:T(1,128)} fusion(s32[2,1]{0,1:T(1,128)S(1)} %copy-done.1, s32[]{:T(128)S(6)} %select_n.236), kind=kLoop, calls=%fused_computation.324 | loop fusion | bytes 12 | tf_op jit(solution)/shard_map/jit(dynamic_index_in_dim)/dynamic_slice | solution.py:236
  10.2 3.7 %collective-permute-done = f32[56,1024]{1,0:T(8,128)S(1)} collective-permute-done((f32[56,1024]{1,0:T(8,128)S(1)}, f32[56,1024]{1,0:T(8,128)S(1)}, u32[]{:S(2)}, u32[]{:S(2)}) %collective-permute-start) | collective-permute-done | bytes 229408 | tf_op jit(solution)/shard_map/ppermute | solution.py:38
  14.4 0.1 fusion.133
  14.8 3.8 %collective-permute-start.2 = (f32[54,1024]{1,0:T(8,128)S(1)}, f32[54,1024]{1,0:T(8,128)S(1)}, u32[]{:S(2)}, u32[]{:S(2)}) collective-permute-start(f32[54,1024]{1,0:T(8,128)S(1)} %pad_maximum_fusion.6), channel_id=1, source_target_pairs={{0,4},{4,8},{8,12},{12,16},{16,20},{20,24},{24,28},{28,32},{32,36}... | collective-permute-start | bytes 663560 | tf_op jit(solution)/shard_map/ppermute | solution.py:35
  18.6 0.2 fusion
  18.9 0.7 %concatenate.51 = f32[4,4,12,1024]{3,2,1,0:T(8,128)S(1)} concatenate(f32[4,4,1,1024]{3,2,1,0:T(1,128)S(1)} %copy.19, f32[4,4,3,1024]{3,2,1,0:T(4,128)S(1)} %reshape.131, f32[4,4,4,1024]{3,2,1,0:T(4,128)S(1)} %pad_maximum_fusion, f32[4,4,3,1024]{3,2,1,0:T(4,128)S(1)} %reshape.133, f32[4,4,1,1024]{3,2,1,0:T(1,128)S(1)} %copy.20), dimensions={2} | concatenate | bytes 1572864 | tf_op jit(solution)/shard_map/concatenate | solution.py:118
  19.6 9.8 %collective-permute-start.3 = (f32[54,1024]{1,0:T(8,128)S(1)}, f32[54,1024]{1,0:T(8,128)S(1)}, u32[]{:S(2)}, u32[]{:S(2)}) collective-permute-start(f32[54,1024]{1,0:T(8,128)S(1)} %pad_maximum_fusion.7), channel_id=1, source_target_pairs={{4,0},{8,4},{12,8},{16,12},{20,16},{24,20},{28,24},{32,28},{36,32}... | collective-permute-start | bytes 663560 | tf_op jit(solution)/shard_map/ppermute | solution.py:35
  29.4 1.5 %collective-permute-done.2 = f32[54,1024]{1,0:T(8,128)S(1)} collective-permute-done((f32[54,1024]{1,0:T(8,128)S(1)}, f32[54,1024]{1,0:T(8,128)S(1)}, u32[]{:S(2)}, u32[]{:S(2)}) %collective-permute-start.2) | collective-permute-done | bytes 221216 | tf_op jit(solution)/shard_map/ppermute | solution.py:35
  30.9 2.1 %collective-permute-done.3 = f32[54,1024]{1,0:T(8,128)S(1)} collective-permute-done((f32[54,1024]{1,0:T(8,128)S(1)}, f32[54,1024]{1,0:T(8,128)S(1)}, u32[]{:S(2)}, u32[]{:S(2)}) %collective-permute-start.3) | collective-permute-done | bytes 221216 | tf_op jit(solution)/shard_map/ppermute | solution.py:35
  33.2 0.3 maximum_maximum_fusion
  33.6 0.1 slice_bitcast_fusion.3
  33.7 0.1 slice_bitcast_fusion.2
  33.9 0.9 %fusion.10 = f32[6,12,1024]{2,1,0:T(8,128)S(1)} fusion(f32[6,12,1024]{2,1,0:T(8,128)S(1)} %get-tuple-element.44, f32[6,12,1024]{2,1,0:T(8,128)S(1)} %get-tuple-element.43, f32[6,12,1024]{2,1,0:T(8,128)S(1)} %get-tuple-element.42, f32[4,8,12,1024]{3,2,1,0:T(8,128)S(1)} %maximum_dynamic-update-slice_fusion, pred[12]{0:T(512)(128)(4,1)S(1)} %get-tuple-element.93, ...), kind=kLoop, calls=%fused_computation.53 | loop fusion | flops 3170304 | bytes 2656292 | tf_op jit(solution)/shard_map/add | solution.py:186
  34.8 0.3 fusion.122
  35.2 1.9 %collective-permute-start.4 = (f32[2,8,1024]{2,1,0:T(8,128)S(1)}, f32[2,8,1024]{2,1,0:T(8,128)S(1)}, u32[]{:S(2)}, u32[]{:S(2)}) collective-permute-start(f32[2,8,1024]{2,1,0:T(8,128)S(1)} %get-tuple-element.64), channel_id=1, source_target_pairs={{0,4},{4,8},{8,12},{12,16},{16,20},{20,24},{24,28},{28,32},{32,36}... | collective-permute-start | bytes 196616 | tf_op jit(solution)/shard_map/ppermute | solution.py:35
  37.1 0.7 %iota_compare_fusion.4 = pred[4]{0:T(512)(128)(4,1)S(1)} fusion(s32[]{:T(128)} %bitcast), kind=kLoop, calls=%fused_computation.338 | loop fusion | flops 4 | bytes 8 | tf_op jit(solution)/shard_map/lt | solution.py:238
  37.8 6.5 %collective-permute-start.5 = (f32[2,8,1024]{2,1,0:T(8,128)S(1)}, f32[2,8,1024]{2,1,0:T(8,128)S(1)}, u32[]{:S(2)}, u32[]{:S(2)}) collective-permute-start(f32[2,8,1024]{2,1,0:T(8,128)S(1)} %get-tuple-element.63), channel_id=1, source_target_pairs={{4,0},{8,4},{12,8},{16,12},{20,16},{24,20},{28,24},{32,28},{36,32}... | collective-permute-start | bytes 196616 | tf_op jit(solution)/shard_map/ppermute | solution.py:35
  44.4 1.8 %collective-permute-done.5 = f32[2,8,1024]{2,1,0:T(8,128)S(1)} collective-permute-done((f32[2,8,1024]{2,1,0:T(8,128)S(1)}, f32[2,8,1024]{2,1,0:T(8,128)S(1)}, u32[]{:S(2)}, u32[]{:S(2)}) %collective-permute-start.5) | collective-permute-done | bytes 65568 | tf_op jit(solution)/shard_map/ppermute | solution.py:35
  46.2 0.2 fusion.159
  46.4 0.2 fusion.158
  46.7 0.2 broadcast_multiply_fusion.1
  46.8 0.5 %broadcast_multiply_fusion.3 = (f32[8,8,1024]{2,1,0:T(8,128)S(1)}, f32[8,8,1024]{2,1,0:T(8,128)S(1)}, f32[8,8,1024]{2,1,0:T(8,128)S(1)}, f32[8,8,1024]{2,1,0:T(8...) fusion(f32[8,8,1024]{2,1,0:T(8,128)S(1)} %get-tuple-element.21,, ...), kind=kLoop, calls=%fused_computation.260 | loop fusion | flops 1966080 | bytes 3932176 | tf_op jit(solution)/shard_map/mul | solution.py:211
  47.4 0.3 broadcast_multiply_fusion
  47.6 0.4 broadcast_multiply_fusion.2
  48.1 0.3 fusion.76
  48.4 0.7 %fusion.53 = (f32[8,8,1024]{2,1,0:T(8,128)S(1)}, f32[8,8,1024]{2,1,0:T(8,128)S(1)}, f32[8,8,1024]{2,1,0:T(8,128)S(1)}, f32[8,8,1024]{2,1,0:T(8,128)S(1)}) fusion(f32[8,8,1024]{2,1,0:T(8,128)S(1)} %get-tuple-element.71, f32[8,8,1024]{2,1,0:T(8,128)S(1)} %get-tuple-element.72, pred[1024]{0:T(1024)(128)(4,1)S(1)} %get-tuple-element.91, ...), kind=kLoop, calls=%fused_computation.136 | loop fusion | flops 1900544 | bytes 3147776 | tf_op jit(solution)/shard_map/add | solution.py:219
  49.1 0.9 %fusion.144 = (f32[1,4,4,1024]{3,2,1,0:T(4,128)}, f32[1,4,4,1024]{3,2,1,0:T(4,128)}) fusion(f32[8,8,1024]{2,1,0:T(8,128)S(1)} %get-tuple-element.46, f32[8,8,1024]{2,1,0:T(8,128)S(1)} %get-tuple-element.48, f32[8,8,1024]{2,1,0:T(8,128)S(1)} %get-tuple-element.13, f32[8,8,1024]{2,1,0:T(8,128)S(1)} %get-tuple-element.14, ...), kind=kLoop, calls=%fused_computation.282 | loop fusion | flops 393216 | bytes 983044 | tf_op jit(solution)/shard_map/broadcast_in_dim | solution.py:256
  (70 shorter events, 2.1 us)
Async XLA Ops:
  0.6 1.0 %copy-start = (f32[2,4,4,1024]{3,2,1,0:T(4,128)S(1)}, f32[2,4,4,1024]{3,2,1,0:T(4,128)}, u32[]{:S(2)}) copy-start(f32[2,4,4,1024]{3,2,1,0:T(4,128)} %param.3) | copy-start | bytes 393220
  0.7 5.8 %copy-start.1 = (s32[2,1]{0,1:T(1,128)S(1)}, s32[2,1]{0,1:T(1,128)}, u32[]{:S(2)}) copy-start(s32[2,1]{0,1:T(1,128)} %param.5) | copy-start | bytes 28
  2.2 8.0 %collective-permute-start.1 = (f32[56,1024]{1,0:T(8,128)S(1)}, f32[56,1024]{1,0:T(8,128)S(1)}, u32[]{:S(2)}, u32[]{:S(2)}) collective-permute-start(f32[56,1024]{1,0:T(8,128)S(1)} %pad_maximum_fusion.5), channel_id=1, source_target_pairs={{1,0},{2,1},{3,2},{5,4},{6,5},{7,6},{9,8},{10,9},{11,10},{13,12},{... | collective-permute-start | bytes 688136 | tf_op jit(solution)/shard_map/ppermute | solution.py:38
  5.0 9.0 %collective-permute-start = (f32[56,1024]{1,0:T(8,128)S(1)}, f32[56,1024]{1,0:T(8,128)S(1)}, u32[]{:S(2)}, u32[]{:S(2)}) collective-permute-start(f32[56,1024]{1,0:T(8,128)S(1)} %pad_maximum_fusion.4), channel_id=1, source_target_pairs={{0,1},{1,2},{2,3},{4,5},{5,6},{6,7},{8,9},{9,10},{10,11},{12,13},{... | collective-permute-start | bytes 688136 | tf_op jit(solution)/shard_map/ppermute | solution.py:38
  14.8 16.1 %collective-permute-start.2 = (f32[54,1024]{1,0:T(8,128)S(1)}, f32[54,1024]{1,0:T(8,128)S(1)}, u32[]{:S(2)}, u32[]{:S(2)}) collective-permute-start(f32[54,1024]{1,0:T(8,128)S(1)} %pad_maximum_fusion.6), channel_id=1, source_target_pairs={{0,4},{4,8},{8,12},{12,16},{16,20},{20,24},{24,28},{28,32},{32,36}... | collective-permute-start | bytes 663560 | tf_op jit(solution)/shard_map/ppermute | solution.py:35
  19.6 13.4 %collective-permute-start.3 = (f32[54,1024]{1,0:T(8,128)S(1)}, f32[54,1024]{1,0:T(8,128)S(1)}, u32[]{:S(2)}, u32[]{:S(2)}) collective-permute-start(f32[54,1024]{1,0:T(8,128)S(1)} %pad_maximum_fusion.7), channel_id=1, source_target_pairs={{4,0},{8,4},{12,8},{16,12},{20,16},{24,20},{28,24},{32,28},{36,32}... | collective-permute-start | bytes 663560 | tf_op jit(solution)/shard_map/ppermute | solution.py:35
  35.2 9.1 %collective-permute-start.4 = (f32[2,8,1024]{2,1,0:T(8,128)S(1)}, f32[2,8,1024]{2,1,0:T(8,128)S(1)}, u32[]{:S(2)}, u32[]{:S(2)}) collective-permute-start(f32[2,8,1024]{2,1,0:T(8,128)S(1)} %get-tuple-element.64), channel_id=1, source_target_pairs={{0,4},{4,8},{8,12},{12,16},{16,20},{20,24},{24,28},{28,32},{32,36}... | collective-permute-start | bytes 196616 | tf_op jit(solution)/shard_map/ppermute | solution.py:35
  37.8 8.4 %collective-permute-start.5 = (f32[2,8,1024]{2,1,0:T(8,128)S(1)}, f32[2,8,1024]{2,1,0:T(8,128)S(1)}, u32[]{:S(2)}, u32[]{:S(2)}) collective-permute-start(f32[2,8,1024]{2,1,0:T(8,128)S(1)} %get-tuple-element.63), channel_id=1, source_target_pairs={{4,0},{8,4},{12,8},{16,12},{20,16},{24,20},{28,24},{32,28},{36,32}... | collective-permute-start | bytes 196616 | tf_op jit(solution)/shard_map/ppermute | solution.py:35

commit v16 on v15

--- a/solution.py
+++ b/solution.py
@@ -54,9 +54,18 @@
 
 
 def with_rows(block, width, depth):
-    ra = block.ndim - 3
-    from_prev = moved(lax.dynamic_slice_in_dim(block, width - depth, depth, ra), 1, 0)
-    from_next = moved(lax.slice_in_dim(block, 0, depth, axis=ra), -1, 0)
+    cols = block.shape[1]
+    last = lax.dynamic_slice_in_dim(block, width - depth, depth, 0)
+    to_next = jnp.concatenate([last[1], last[0, 1 : cols - 1]], 0)
+    to_prev = jnp.concatenate([block[0], block[1, 1 : cols - 1]], 0)
+
+    def rebuilt(flat):
+        return flat[:cols], jnp.pad(flat[cols:], [(1, 1), (0, 0)])
+
+    prev_near, prev_far = rebuilt(moved(to_next, 1, 0))
+    next_near, next_far = rebuilt(moved(to_prev, -1, 0))
+    from_prev = jnp.stack([prev_far, prev_near], 0)
+    from_next = jnp.stack([next_near, next_far], 0)
     return placed_rows(block, from_prev, from_next, width, depth)
 
 

time: 50.3 us -> 49.9 us (level)
  waiting for transfers between devices: 9.08 us -> 8.51 us
    ppermute x2, waiting for transfers between devices: 3.73 us -> 3.07 us  [moved(): return lax.ppermute(value, 'xline', pairs)]
  transfers between devices with their start and end apart: 6 -> 6, of which waited for: 4 -> 5; matrix products, arithmetic and copies ran while one was open for 6% -> 6% of each run, Pallas kernels for 0% -> 0%
where the time goes in v16:
time: 49.9 us; the launch traced here: 49.6 us
  starting transfers between devices  26 us (52%)
  waiting for transfers between devices  8.51 us (17%)
  other arithmetic  8.21 us (16%)
  between operations  3.91 us (8%)
  local copies, waits for them, and re-layouts  2.97 us (6%)
    ppermute x4, starting transfers between devices, moved(): return lax.ppermute(value, 'inline', pairs)  22 us
    ppermute x4, waiting for transfers between devices, moved(): return lax.ppermute(value, 'inline', pairs)  5.43 us
    ppermute x2, starting transfers between devices, moved(): return lax.ppermute(value, 'xline', pairs)  3.95 us
    ppermute x2, waiting for transfers between devices, moved(): return lax.ppermute(value, 'xline', pairs)  3.07 us
    mul x4, other arithmetic, attributes(): 0.25 * (neighbor(member, which_axis, 1, up_open) + 2.0 * member + neighbo...  1.37 us
    add x2, other arithmetic, relax_rows(): return centre + step_size * change  1.26 us
  transfers between devices with their start and end apart: 6, of which 5 were waited for; matrix products, arithmetic and copies ran while one was open for 6% of the time, Pallas kernels for 0%

profile of v16, /device:TPU:30, one launch (start us, length us, event | category | flops | bytes accessed | tf_op | source)
XLA Modules:
  0.0 49.6 jit_solution(976286280482604082)
XLA Ops:
  0.7 1.0 %fusion.157 = (f32[3,4,4,1024]{3,2,1,0:T(4,128)S(1)}, f32[3,1,4,4,1024]{4,3,2,0,1:T(4,128)S(1)}) fusion(bf16[3,2,4,4,1024]{4,3,2,1,0:T(4,128)(2,1)} %param.4, s32[]{:T(128)S(6)} %select_n.236), kind=kLoop, calls=%fused_computation.325 | loop fusion | flops 49152 | bytes 491524 | tf_op jit(solution)/shard_map/convert_element_type | solution.py:244
  1.7 0.2 fusion.156
  1.9 0.1 fusion.22
  2.2 2.7 %collective-permute-start.1 = (f32[56,1024]{1,0:T(8,128)S(1)}, f32[56,1024]{1,0:T(8,128)S(1)}, u32[]{:S(2)}, u32[]{:S(2)}) collective-permute-start(f32[56,1024]{1,0:T(8,128)S(1)} %pad_maximum_fusion.5), channel_id=1, source_target_pairs={{1,0},{2,1},{3,2},{5,4},{6,5},{7,6},{9,8},{10,9},{11,10},{13,12},{... | collective-permute-start | bytes 688136 | tf_op jit(solution)/shard_map/ppermute | solution.py:38
  5.0 1.3 %collective-permute-start = (f32[56,1024]{1,0:T(8,128)S(1)}, f32[56,1024]{1,0:T(8,128)S(1)}, u32[]{:S(2)}, u32[]{:S(2)}) collective-permute-start(f32[56,1024]{1,0:T(8,128)S(1)} %pad_maximum_fusion.4), channel_id=1, source_target_pairs={{0,1},{1,2},{2,3},{4,5},{5,6},{6,7},{8,9},{9,10},{10,11},{12,13},{... | collective-permute-start | bytes 688136 | tf_op jit(solution)/shard_map/ppermute | solution.py:38
  6.5 0.6 %constant_dynamic-slice_fusion.1 = s32[1,1]{0,1:T(1,128)} fusion(s32[2,1]{0,1:T(1,128)S(1)} %copy-done.1, s32[]{:T(128)S(6)} %select_n.236), kind=kLoop, calls=%fused_computation.333 | loop fusion | bytes 12 | tf_op jit(solution)/shard_map/jit(dynamic_index_in_dim)/dynamic_slice | solution.py:245
  9.2 0.7 %iota_compare_fusion.4 = pred[4]{0:T(512)(128)(4,1)S(1)} fusion(s32[]{:T(128)} %bitcast), kind=kLoop, calls=%fused_computation.347 | loop fusion | flops 4 | bytes 8 | tf_op jit(solution)/shard_map/lt | solution.py:247
  10.9 3.1 %collective-permute-done = f32[56,1024]{1,0:T(8,128)S(1)} collective-permute-done((f32[56,1024]{1,0:T(8,128)S(1)}, f32[56,1024]{1,0:T(8,128)S(1)}, u32[]{:S(2)}, u32[]{:S(2)}) %collective-permute-start) | collective-permute-done | bytes 229408 | tf_op jit(solution)/shard_map/ppermute | solution.py:38
  14.4 0.1 fusion.133
  14.8 3.8 %collective-permute-start.2 = (f32[54,1024]{1,0:T(8,128)S(1)}, f32[54,1024]{1,0:T(8,128)S(1)}, u32[]{:S(2)}, u32[]{:S(2)}) collective-permute-start(f32[54,1024]{1,0:T(8,128)S(1)} %pad_maximum_fusion.6), channel_id=1, source_target_pairs={{0,4},{4,8},{8,12},{12,16},{16,20},{20,24},{24,28},{28,32},{32,36}... | collective-permute-start | bytes 663560 | tf_op jit(solution)/shard_map/ppermute | solution.py:35
  18.6 0.2 fusion
  18.9 0.7 %concatenate.57 = f32[4,4,12,1024]{3,2,1,0:T(8,128)S(1)} concatenate(f32[4,4,1,1024]{3,2,1,0:T(1,128)S(1)} %copy.19, f32[4,4,3,1024]{3,2,1,0:T(4,128)S(1)} %reshape.131, f32[4,4,4,1024]{3,2,1,0:T(4,128)S(1)} %pad_maximum_fusion, f32[4,4,3,1024]{3,2,1,0:T(4,128)S(1)} %reshape.133, f32[4,4,1,1024]{3,2,1,0:T(1,128)S(1)} %copy.20), dimensions={2} | concatenate | bytes 1572864 | tf_op jit(solution)/shard_map/concatenate | solution.py:127
  19.6 9.8 %collective-permute-start.3 = (f32[54,1024]{1,0:T(8,128)S(1)}, f32[54,1024]{1,0:T(8,128)S(1)}, u32[]{:S(2)}, u32[]{:S(2)}) collective-permute-start(f32[54,1024]{1,0:T(8,128)S(1)} %pad_maximum_fusion.7), channel_id=1, source_target_pairs={{4,0},{8,4},{12,8},{16,12},{20,16},{24,20},{28,24},{32,28},{36,32}... | collective-permute-start | bytes 663560 | tf_op jit(solution)/shard_map/ppermute | solution.py:35
  29.4 1.5 %collective-permute-done.2 = f32[54,1024]{1,0:T(8,128)S(1)} collective-permute-done((f32[54,1024]{1,0:T(8,128)S(1)}, f32[54,1024]{1,0:T(8,128)S(1)}, u32[]{:S(2)}, u32[]{:S(2)}) %collective-permute-start.2) | collective-permute-done | bytes 221216 | tf_op jit(solution)/shard_map/ppermute | solution.py:35
  30.9 2.1 %collective-permute-done.3 = f32[54,1024]{1,0:T(8,128)S(1)} collective-permute-done((f32[54,1024]{1,0:T(8,128)S(1)}, f32[54,1024]{1,0:T(8,128)S(1)}, u32[]{:S(2)}, u32[]{:S(2)}) %collective-permute-start.3) | collective-permute-done | bytes 221216 | tf_op jit(solution)/shard_map/ppermute | solution.py:35
  33.2 0.3 maximum_maximum_fusion
  33.7 0.1 slice_bitcast_fusion.2
  33.9 0.9 %fusion.10 = f32[6,12,1024]{2,1,0:T(8,128)S(1)} fusion(f32[6,12,1024]{2,1,0:T(8,128)S(1)} %get-tuple-element.44, f32[6,12,1024]{2,1,0:T(8,128)S(1)} %get-tuple-element.43, f32[6,12,1024]{2,1,0:T(8,128)S(1)} %get-tuple-element.42, f32[4,8,12,1024]{3,2,1,0:T(8,128)S(1)} %maximum_dynamic-update-slice_fusion, pred[12]{0:T(512)(128)(4,1)S(1)} %get-tuple-element.95, ...), kind=kLoop, calls=%fused_computation.53 | loop fusion | flops 3170304 | bytes 2656292 | tf_op jit(solution)/shard_map/add | solution.py:195
  34.8 0.3 fusion.122
  35.2 1.9 %collective-permute-start.4 = (f32[14,1024]{1,0:T(8,128)S(1)}, f32[14,1024]{1,0:T(8,128)S(1)}, u32[]{:S(2)}, u32[]{:S(2)}) collective-permute-start(f32[14,1024]{1,0:T(8,128)S(1)} %pad_maximum_fusion.12), channel_id=1, source_target_pairs={{0,4},{4,8},{8,12},{12,16},{16,20},{20,24},{24,28},{28,32},{32,36}... | collective-permute-start | bytes 172040 | tf_op jit(solution)/shard_map/ppermute | solution.py:35
  37.2 6.5 %collective-permute-start.5 = (f32[14,1024]{1,0:T(8,128)S(1)}, f32[14,1024]{1,0:T(8,128)S(1)}, u32[]{:S(2)}, u32[]{:S(2)}) collective-permute-start(f32[14,1024]{1,0:T(8,128)S(1)} %pad_maximum_fusion.13), channel_id=1, source_target_pairs={{4,0},{8,4},{12,8},{16,12},{20,16},{24,20},{28,24},{32,28},{36,32}... | collective-permute-start | bytes 172040 | tf_op jit(solution)/shard_map/ppermute | solution.py:35
  43.7 0.3 collective-permute-done.4
  44.0 1.6 %collective-permute-done.5 = f32[14,1024]{1,0:T(8,128)S(1)} collective-permute-done((f32[14,1024]{1,0:T(8,128)S(1)}, f32[14,1024]{1,0:T(8,128)S(1)}, u32[]{:S(2)}, u32[]{:S(2)}) %collective-permute-start.5) | collective-permute-done | bytes 57376 | tf_op jit(solution)/shard_map/ppermute | solution.py:35
  45.7 0.2 fusion.159
  45.9 0.2 fusion.158
  46.2 0.2 broadcast_multiply_fusion.1
  46.4 0.5 %broadcast_multiply_fusion.3 = (f32[8,8,1024]{2,1,0:T(8,128)S(1)}, f32[8,8,1024]{2,1,0:T(8,128)S(1)}, f32[8,8,1024]{2,1,0:T(8,128)S(1)}, f32[8,8,1024]{2,1,0:T(8...) fusion(f32[8,8,1024]{2,1,0:T(8,128)S(1)} %get-tuple-element.21,, ...), kind=kLoop, calls=%fused_computation.260 | loop fusion | flops 1966080 | bytes 3932176 | tf_op jit(solution)/shard_map/mul | solution.py:220
  46.9 0.3 broadcast_multiply_fusion
  47.2 0.4 broadcast_multiply_fusion.2
  47.6 0.3 fusion.76
  48.0 0.7 %fusion.53 = (f32[8,8,1024]{2,1,0:T(8,128)S(1)}, f32[8,8,1024]{2,1,0:T(8,128)S(1)}, f32[8,8,1024]{2,1,0:T(8,128)S(1)}, f32[8,8,1024]{2,1,0:T(8,128)S(1)}) fusion(f32[8,8,1024]{2,1,0:T(8,128)S(1)} %get-tuple-element.73, f32[8,8,1024]{2,1,0:T(8,128)S(1)} %get-tuple-element.74, pred[1024]{0:T(1024)(128)(4,1)S(1)} %get-tuple-element.93, ...), kind=kLoop, calls=%fused_computation.136 | loop fusion | flops 1900544 | bytes 3147776 | tf_op jit(solution)/shard_map/add | solution.py:228
  48.6 0.9 %fusion.144 = (f32[1,4,4,1024]{3,2,1,0:T(4,128)}, f32[1,4,4,1024]{3,2,1,0:T(4,128)}) fusion(f32[8,8,1024]{2,1,0:T(8,128)S(1)} %get-tuple-element.46, f32[8,8,1024]{2,1,0:T(8,128)S(1)} %get-tuple-element.48, f32[8,8,1024]{2,1,0:T(8,128)S(1)} %get-tuple-element.13, f32[8,8,1024]{2,1,0:T(8,128)S(1)} %get-tuple-element.14, ...), kind=kLoop, calls=%fused_computation.282 | loop fusion | flops 393216 | bytes 983044 | tf_op jit(solution)/shard_map/broadcast_in_dim | solution.py:265
  (79 shorter events, 2.3 us)
Async XLA Ops:
  0.6 1.0 %copy-start = (f32[2,4,4,1024]{3,2,1,0:T(4,128)S(1)}, f32[2,4,4,1024]{3,2,1,0:T(4,128)}, u32[]{:S(2)}) copy-start(f32[2,4,4,1024]{3,2,1,0:T(4,128)} %param.3) | copy-start | bytes 393220
  0.7 5.8 %copy-start.1 = (s32[2,1]{0,1:T(1,128)S(1)}, s32[2,1]{0,1:T(1,128)}, u32[]{:S(2)}) copy-start(s32[2,1]{0,1:T(1,128)} %param.5) | copy-start | bytes 28
  2.2 8.7 %collective-permute-start.1 = (f32[56,1024]{1,0:T(8,128)S(1)}, f32[56,1024]{1,0:T(8,128)S(1)}, u32[]{:S(2)}, u32[]{:S(2)}) collective-permute-start(f32[56,1024]{1,0:T(8,128)S(1)} %pad_maximum_fusion.5), channel_id=1, source_target_pairs={{1,0},{2,1},{3,2},{5,4},{6,5},{7,6},{9,8},{10,9},{11,10},{13,12},{... | collective-permute-start | bytes 688136 | tf_op jit(solution)/shard_map/ppermute | solution.py:38
  5.0 9.0 %collective-permute-start = (f32[56,1024]{1,0:T(8,128)S(1)}, f32[56,1024]{1,0:T(8,128)S(1)}, u32[]{:S(2)}, u32[]{:S(2)}) collective-permute-start(f32[56,1024]{1,0:T(8,128)S(1)} %pad_maximum_fusion.4), channel_id=1, source_target_pairs={{0,1},{1,2},{2,3},{4,5},{5,6},{6,7},{8,9},{9,10},{10,11},{12,13},{... | collective-permute-start | bytes 688136 | tf_op jit(solution)/shard_map/ppermute | solution.py:38
  14.8 16.1 %collective-permute-start.2 = (f32[54,1024]{1,0:T(8,128)S(1)}, f32[54,1024]{1,0:T(8,128)S(1)}, u32[]{:S(2)}, u32[]{:S(2)}) collective-permute-start(f32[54,1024]{1,0:T(8,128)S(1)} %pad_maximum_fusion.6), channel_id=1, source_target_pairs={{0,4},{4,8},{8,12},{12,16},{16,20},{20,24},{24,28},{28,32},{32,36}... | collective-permute-start | bytes 663560 | tf_op jit(solution)/shard_map/ppermute | solution.py:35
  19.6 13.4 %collective-permute-start.3 = (f32[54,1024]{1,0:T(8,128)S(1)}, f32[54,1024]{1,0:T(8,128)S(1)}, u32[]{:S(2)}, u32[]{:S(2)}) collective-permute-start(f32[54,1024]{1,0:T(8,128)S(1)} %pad_maximum_fusion.7), channel_id=1, source_target_pairs={{4,0},{8,4},{12,8},{16,12},{20,16},{24,20},{28,24},{32,28},{36,32}... | collective-permute-start | bytes 663560 | tf_op jit(solution)/shard_map/ppermute | solution.py:35
  35.2 8.7 %collective-permute-start.4 = (f32[14,1024]{1,0:T(8,128)S(1)}, f32[14,1024]{1,0:T(8,128)S(1)}, u32[]{:S(2)}, u32[]{:S(2)}) collective-permute-start(f32[14,1024]{1,0:T(8,128)S(1)} %pad_maximum_fusion.12), channel_id=1, source_target_pairs={{0,4},{4,8},{8,12},{12,16},{16,20},{20,24},{24,28},{28,32},{32,36}... | collective-permute-start | bytes 172040 | tf_op jit(solution)/shard_map/ppermute | solution.py:35
  37.2 8.4 %collective-permute-start.5 = (f32[14,1024]{1,0:T(8,128)S(1)}, f32[14,1024]{1,0:T(8,128)S(1)}, u32[]{:S(2)}, u32[]{:S(2)}) collective-permute-start(f32[14,1024]{1,0:T(8,128)S(1)} %pad_maximum_fusion.13), channel_id=1, source_target_pairs={{4,0},{8,4},{12,8},{16,12},{20,16},{24,20},{28,24},{32,28},{36,32}... | collective-permute-start | bytes 172040 | tf_op jit(solution)/shard_map/ppermute | solution.py:35
